TPU v7x, 256 devices: a whole 4x4x8 slice. The times are simulated.
256 devices in a mesh: walker: 2 (over core), elec: 128 (over x, z, y).
Axes of the slice: x: 4, y: 4, z: 8, core: 2. Of those that a mesh axis runs over, the one named last changes fastest.
Arguments:
- inverse_rows: float32 [16384, 8192], P(('walker', 'elec')), parts along dimension 0
- row_values: float32 [128, 8, 64], P('walker'), parts along dimension 0
- orbital_blocks: int32 [128, 8], P('walker'), parts along dimension 0, may hold values from 0 to 127, as said below
- moved: int32 [128], P('walker'), parts along dimension 0, may hold values from 0 to 8191
- accepted: int32 [128], P('walker'), parts along dimension 0, may hold values 0 or 1
Outputs:
- new_inverse: float32 [16384, 8192], P(('walker', 'elec')), parts along dimension 0
- ratios: float32 [128], P('walker'), parts along dimension 0
There are 2 independent parts, one for each index of `walker`. A program takes and returns all parts, laid end to end along the dimension named above; each array names one. Nothing has to cross between parts.
Inputs may be any that keep to these rules, and one draw needn't show every extreme that they name: `orbital_blocks`: the 8 blocks of a move are distinct, and the first is the block holding orbital number moved[k].
All inputs are finite; a program needn't handle non-finite values.
Results may differ from a plain program's by a relative error of at most 0.0001.
Values sent between devices are 32-bit elements; how exact they have to be, the bound alone decides.
No kernel may reach another device: no remote copies, remote signals or barrier semaphores. Data moves between devices by JAX's collectives and lax.ppermute only.
A program may use at most 64 MiB of HBM per device.

v0:
```python
import jax
import jax.numpy as jnp
from jax import lax
from jax.sharding import PartitionSpec as P
from jax.experimental import pallas as pl
from jax.experimental.pallas import tpu as pltpu

MOVES = 64


HI = lax.Precision.HIGHEST


def border_step(coupling, row_vec, col_vec, accept_flag, unit_row):
    left_vec = jnp.dot(row_vec, coupling, precision=HI)
    right_vec = jnp.dot(coupling, col_vec, precision=HI)
    det_ratio = (
        1.0 + jnp.dot(row_vec, unit_row, precision=HI) - jnp.dot(left_vec, col_vec, precision=HI)
    )
    coupling = (
        coupling + accept_flag * jnp.outer(right_vec - unit_row, left_vec - unit_row) / det_ratio
    )
    return (coupling, det_ratio)


def run_border(intersection, accepted):

    def one_step(coupling, step_items):
        row_vec, col_vec, accept_flag, unit_row = step_items
        return border_step(coupling, row_vec, col_vec, accept_flag, unit_row)

    start_value = jnp.zeros((MOVES, MOVES), jnp.float32)
    step_items = (
        intersection,
        intersection.T,
        accepted.astype(jnp.float32),
        jnp.eye(MOVES, dtype=jnp.float32),
    )
    return lax.scan(one_step, start_value, step_items)


def _border_kernel(m_ref, mt_ref, acc_ref, c_ref, r_ref):
    n = m_ref.shape[0]
    lane = lax.broadcasted_iota(jnp.int32, (1, n), 1)
    sub = lax.broadcasted_iota(jnp.int32, (n, 1), 0)
    mt = mt_ref[...]
    acc = acc_ref[...]

    def step(k, carry):
        c, ratios = carry
        e_row = (lane == k).astype(jnp.float32)
        e_col = (sub == k).astype(jnp.float32)
        row_row = m_ref[pl.ds(k, 1), :]
        col_row = mt_ref[pl.ds(k, 1), :]
        row_col = jnp.sum(mt * e_row, axis=1, keepdims=True)
        left = jnp.sum(c * row_col, axis=0, keepdims=True)
        right = jnp.sum(c * col_row, axis=1, keepdims=True)
        diag = jnp.sum(row_row * e_row, axis=1, keepdims=True)
        lc = jnp.sum(left * col_row, axis=1, keepdims=True)
        ratio = 1.0 + diag - lc
        flag = jnp.sum(acc * e_row, axis=1, keepdims=True)
        c = c + flag * ((right - e_col) * (left - e_row)) / ratio
        ratios = ratios + e_row * ratio
        return c, ratios

    c0 = jnp.zeros((n, n), jnp.float32)
    r0 = jnp.zeros((1, n), jnp.float32)
    c, ratios = lax.fori_loop(0, n, step, (c0, r0))
    c_ref[...] = c
    r_ref[...] = ratios


def border(intersection, accepted):
    n = intersection.shape[0]
    vm = pl.BlockSpec(memory_space=pltpu.VMEM)
    c, r = pl.pallas_call(
        _border_kernel,
        out_shape=(jax.ShapeDtypeStruct((n, n), jnp.float32), jax.ShapeDtypeStruct((1, n), jnp.float32)),
        in_specs=[vm, vm, vm],
        out_specs=(vm, vm),
    )(intersection, intersection.T, accepted.astype(jnp.float32).reshape(1, n))
    return c, r.reshape(n)


def on_device(inverse_rows, row_values, orbital_blocks, moved, accepted):
    row_count = inverse_rows.shape[0]
    block_width = row_values.shape[2]
    blocks_here = row_count // block_width
    owned_blocks = lax.axis_index("elec") * blocks_here + jnp.arange(blocks_here, dtype=jnp.int32)
    onehot = (orbital_blocks[:, :, None] == owned_blocks[None, None, :]).astype(jnp.float32)
    change = jnp.einsum("ksb,kst->kbt", onehot, row_values, precision=HI).reshape(MOVES, row_count)
    picked = jnp.take(inverse_rows, moved, axis=1)
    local_weights = jnp.dot(change, inverse_rows, precision=HI)
    full_weights = lax.psum(local_weights, "elec")
    intersection = jnp.take(full_weights, moved, axis=1)
    coupling, ratios = border(intersection, accepted)
    factor = jnp.dot(picked, coupling, precision=HI)
    new_inverse = inverse_rows - jnp.dot(factor, full_weights, precision=HI)
    return (new_inverse, ratios)


def solution(mesh):
    placed = (
        P(("walker", "elec"), None),
        P("walker", None, None),
        P("walker", None),
        P("walker"),
        P("walker"),
    )
    return jax.shard_map(
        on_device,
        mesh=mesh,
        in_specs=placed,
        out_specs=(P(("walker", "elec"), None), P("walker")),
        check_vma=False,
    )
```

profile of v0, /device:TPU:0, one launch (start us, length us, event | category | flops | bytes accessed | tf_op | source)
XLA Modules:
  0.0 277.7 jit_solution(9035715569080380229)
XLA Ops:
  7.2 0.0 copy-start
  7.2 0.0 all-reduce.2.cloned.1.call-start
  7.2 0.7 compare_bitcast_fusion
  8.0 0.1 copy.10
  8.1 0.0 copy-done
  8.1 0.3 fusion.6
  8.5 4.8 %fusion.7 = f32[64,8192]{1,0:T(8,128)} fusion(f32[64,64]{1,0:T(8,128)S(1)} %bitcast.21, f32[64,8192]{1,0:T(8,128)} %param.7), kind=kOutput, calls=%fused_computation.16 | convolution fusion | flops 402653184 | bytes 4210688 | tf_op jit(solution)/shard_map/dot_general | solution.py:93
  13.3 0.0 copy-start.1
  13.3 0.0 all-reduce.2.cloned.1.call-update
  13.3 1.6 copy-done.1
  14.9 0.0 copy-start.2
  14.9 0.0 copy-start.3
  14.9 2.7 copy.7
  17.6 0.0 copy-done.2
  17.6 2.8 %gather_fusion = f32[64,64]{1,0:T(8,128)S(1)} fusion(f32[64,8192]{0,1:T(8,128)} %copy.7, s32[1024]{0:T(1024)S(1)} %pad_clamp_fusion), kind=kCustom, calls=%fused_computation.clone | custom fusion | bytes 33024 | tf_op jit(solution)/shard_map/jit(_take)/gather | solution.py:92
  20.4 0.0 copy-done.3
  20.4 0.6 convert_bitcast_fusion.acc_ref
  21.0 222.9 %all-reduce.2.cloned.1.call-done = f32[64,8192]{1,0:T(8,128)} async-done(((f32[64,8192]{1,0:T(8,128)}), f32[64,8192]{1,0:T(8,128)}) %all-reduce.2.cloned.1.call-update) | async-done | bytes 2097168 | tf_op jit(solution)/shard_map/psum | solution.py:94
  243.9 3.8 %copy.8 = f32[64,8192]{0,1:T(8,128)} copy(f32[64,8192]{1,0:T(8,128)} %all-reduce.2.cloned.1.call-done) | data formatting | bytes 4194304 | tf_op jit(solution)/shard_map/psum | solution.py:94
  247.6 2.8 %gather_fusion.1 = f32[64,64]{1,0:T(8,128)S(1)} fusion(f32[64,8192]{0,1:T(8,128)} %copy.8, s32[1024]{0:T(1024)S(1)} %pad_clamp_fusion), kind=kCustom, calls=%fused_computation.1.clone | custom fusion | bytes 33024 | tf_op jit(solution)/shard_map/jit(_take)/gather | solution.py:95
  250.4 0.1 fusion.15
  250.5 0.7 broadcast_select_fusion.mt_ref
  251.2 0.7 copy.9.m_ref
  251.9 13.1 %shard_map.68 = (f32[64,64]{1,0:T(8,128)}, f32[1,64]{1,0:T(1,128)}) custom-call(f32[64,64]{1,0:T(8,128)} %copy.9.m_ref, f32[64,64]{1,0:T(8,128)} %broadcast_select_fusion.mt_ref, f32[1,64]{1,0:T(1,128)} %convert_bitcast_fusion.acc_ref), custom_call_target="tpu_custom_call" | custom-call | tf_op jit(solution)/shard_map/pallas_call | solution.py:76
  265.0 1.1 fusion
  266.1 4.8 %convolution_subtract_fusion = f32[64,8192]{1,0:T(8,128)} fusion(f32[64,8192]{1,0:T(8,128)S(1)} %copy-done.1, f32[64,64]{1,0:T(8,128)S(1)} %fusion, f32[64,8192]{1,0:T(8,128)} %all-reduce.2.cloned.1.call-done), kind=kOutput, calls=%fused_computation.2 | convolution fusion | flops 403177472 | bytes 6307840 | tf_op jit(solution)/shard_map/dot_general | solution.py:98
  (3 shorter events, 0.0 us)
Async XLA Ops:
  7.2 1.0 copy-start
  7.2 236.7 %all-reduce.2.cloned.1.call-start = ((), (), s32[]{:S(2)}) async-start(), calls=%async_computation | async-start | bytes 4194304 | tf_op jit(solution)/shard_map/psum | solution.py:94
  13.3 1.6 copy-start.1
  14.9 2.7 copy-start.2
  14.9 5.5 %copy-start.3 = (s32[64]{0:T(128)S(1)}, s32[64]{0:T(128)}, u32[]{:S(2)}) copy-start(s32[64]{0:T(128)} %param.11) | copy-start | bytes 772
Sparse Core Ops, SparseCore 0:
  14.0 229.8 all-reduce.1
where the time goes:
time: 280 us; the launch traced here: 278 us
  waiting for transfers between devices  223 us (80%)
  local copies, waits for them, and re-layouts  14.5 us (5%)
  between operations  14.1 us (5%)
  Pallas kernels  13.1 us (5%)
  matrix products  11 us (4%)
    psum x1, waiting for transfers between devices, on_device(): full_weights = lax.psum(local_weights, 'elec')  223 us
    pallas_call x1, Pallas kernels, border(): pl.pallas_call(_border_kernel, out_shape=(jax.ShapeDtypeStruct((n, n), jn...  13.1 us
  transfers between devices with their start and end apart: 1, of which 1 were waited for; matrix products, arithmetic and copies ran while one was open for 2% of the time, Pallas kernels for 0%

commit v1 on v0

--- a/solution.py
+++ b/solution.py
@@ -1,7 +1,7 @@
 import jax
 import jax.numpy as jnp
 from jax import lax
-from jax.sharding import PartitionSpec as P
+from jax.sharding import Mesh, PartitionSpec as P
 from jax.experimental import pallas as pl
 from jax.experimental.pallas import tpu as pltpu
 
@@ -82,16 +82,67 @@
     return c, r.reshape(n)
 
 
+def shift_perm(n, d):
+    return [(j, (j + d) % n) for j in range(n)]
+
+
+def half_ring_rs(x, axis, n):
+    if n == 1:
+        return x
+    i = lax.axis_index(axis)
+    width = x.shape[1] // n
+    chunk = lambda c: lax.dynamic_slice_in_dim(x, (c % n) * width, width, 1)
+    up, down = n // 2, n - 1 - n // 2
+    cw, ccw = chunk(i + up), chunk(i - down)
+    for s in range(1, up + 1):
+        cw = lax.ppermute(cw, axis, shift_perm(n, 1))
+        if s <= down:
+            ccw = lax.ppermute(ccw, axis, shift_perm(n, -1))
+        if s < up:
+            cw = cw + chunk(i + up - s)
+        if s < down:
+            ccw = ccw + chunk(i - down + s)
+    if down == 0:
+        return chunk(i) + cw
+    return chunk(i) + cw + ccw
+
+
+def half_ring_ag(x, axis, n):
+    if n == 1:
+        return x
+    i = lax.axis_index(axis)
+    width = x.shape[1]
+    up, down = n // 2, n - 1 - n // 2
+    out = jnp.zeros(x.shape[:1] + (n * width,), x.dtype)
+    out = lax.dynamic_update_slice_in_dim(out, x, i * width, 1)
+    cw, ccw = x, x
+    for s in range(1, up + 1):
+        cw = lax.ppermute(cw, axis, shift_perm(n, 1))
+        out = lax.dynamic_update_slice_in_dim(out, cw, ((i - s) % n) * width, 1)
+        if s <= down:
+            ccw = lax.ppermute(ccw, axis, shift_perm(n, -1))
+            out = lax.dynamic_update_slice_in_dim(out, ccw, ((i + s) % n) * width, 1)
+    return out
+
+
+def ring_allreduce(x, phases):
+    for axis, n in phases:
+        x = half_ring_rs(x, axis, n)
+    for axis, n in reversed(phases):
+        x = half_ring_ag(x, axis, n)
+    return x
+
+
 def on_device(inverse_rows, row_values, orbital_blocks, moved, accepted):
     row_count = inverse_rows.shape[0]
     block_width = row_values.shape[2]
     blocks_here = row_count // block_width
-    owned_blocks = lax.axis_index("elec") * blocks_here + jnp.arange(blocks_here, dtype=jnp.int32)
+    owned_blocks = lax.axis_index(ELEC) * blocks_here + jnp.arange(blocks_here, dtype=jnp.int32)
     onehot = (orbital_blocks[:, :, None] == owned_blocks[None, None, :]).astype(jnp.float32)
     change = jnp.einsum("ksb,kst->kbt", onehot, row_values, precision=HI).reshape(MOVES, row_count)
     picked = jnp.take(inverse_rows, moved, axis=1)
     local_weights = jnp.dot(change, inverse_rows, precision=HI)
-    full_weights = lax.psum(local_weights, "elec")
+    full_weights = ring_allreduce(local_weights, PHASES)
     intersection = jnp.take(full_weights, moved, axis=1)
     coupling, ratios = border(intersection, accepted)
     factor = jnp.dot(picked, coupling, precision=HI)
@@ -99,9 +150,17 @@
     return (new_inverse, ratios)
 
 
+ELEC = ("x", "z", "y")
+PHASES = (("z", 8), ("y", 4), ("x", 4))
+
+
 def solution(mesh):
+    walkers, elec = mesh.devices.shape
+    torus = mesh.devices.reshape(walkers, 4, 8, elec // 32)
+    mesh = Mesh(torus, ("walker",) + ELEC)
+    rows = ("walker",) + ELEC
     placed = (
-        P(("walker", "elec"), None),
+        P(rows, None),
         P("walker", None, None),
         P("walker", None),
         P("walker"),
@@ -111,6 +170,6 @@
         on_device,
         mesh=mesh,
         in_specs=placed,
-        out_specs=(P(("walker", "elec"), None), P("walker")),
+        out_specs=(P(rows, None), P("walker")),
         check_vma=False,
     )

time: 280 us -> 165 us (0.59)
  waiting for transfers between devices: 223 us -> 70.1 us
  starting transfers between devices: 0.04 us -> 40.8 us
  between operations: 14.1 us -> 0.92 us
  local copies, waits for them, and re-layouts: 14.5 us -> 19.7 us
  other arithmetic: 2.08 us -> 5.52 us
    psum x1 -> x0, waiting for transfers between devices: 223 us -> none  [on_device(): full_weights = lax.psum(local_weights, 'elec')]
    ppermute x0 -> x26, waiting for transfers between devices: none -> 70.1 us  [the longest x8 36.3 us: half_ring_rs(): cw = lax.ppermute(cw, axis, shift_perm(n, 1))]
    ppermute x0 -> x26, starting transfers between devices: none -> 40.8 us  [the longest x8 13.7 us: half_ring_ag(): cw = lax.ppermute(cw, axis, shift_perm(n, 1))]
    dynamic_update_slice x0 -> x16, local copies, waits for them, and re-layouts: none -> 7.79 us  [the longest x5 3.55 us: half_ring_ag(): out = lax.dynamic_update_slice_in_dim(out, ccw, (i + s) % n * width, 1)]
    psum x1 -> x0, local copies, waits for them, and re-layouts: 3.77 us -> none  [on_device(): full_weights = lax.psum(local_weights, 'elec')]
    add x0 -> x8, other arithmetic: none -> 3.49 us  [the longest x5 2.33 us: half_ring_rs(): cw = cw + chunk(i + up - s)]
    dot_general x1, matrix products: 4.8 us -> 8.07 us  [on_device(): new_inverse = inverse_rows - jnp.dot(factor, full_weights, precision=HI)]
  transfers between devices with their start and end apart: 1 -> 26, of which waited for: 1 -> 18; matrix products, arithmetic and copies ran while one was open for 2% -> 9% of each run, Pallas kernels for 0% -> 0%
where the time goes in v1:
time: 165 us; the launch traced here: 163 us
  waiting for transfers between devices  70.1 us (42%)
  starting transfers between devices  40.8 us (25%)
  local copies, waits for them, and re-layouts  19.7 us (12%)
  Pallas kernels  13.1 us (8%)
  matrix products  13 us (8%)
  other arithmetic  5.52 us (3%)
    ppermute x8, waiting for transfers between devices, half_ring_rs(): cw = lax.ppermute(cw, axis, shift_perm(n, 1))  36.3 us
    ppermute x8, waiting for transfers between devices, half_ring_ag(): cw = lax.ppermute(cw, axis, shift_perm(n, 1))  31.4 us
    ppermute x8, starting transfers between devices, half_ring_ag(): cw = lax.ppermute(cw, axis, shift_perm(n, 1))  13.7 us
    ppermute x5, starting transfers between devices, half_ring_rs(): ccw = lax.ppermute(ccw, axis, shift_perm(n, -1))  13.6 us
    pallas_call x1, Pallas kernels, border(): pl.pallas_call(_border_kernel, out_shape=(jax.ShapeDtypeStruct((n, n), jn...  13.1 us
    dot_general x1, matrix products, on_device(): new_inverse = inverse_rows - jnp.dot(factor, full_weights, precision=HI)  8.07 us
    ppermute x5, starting transfers between devices, half_ring_ag(): ccw = lax.ppermute(ccw, axis, shift_perm(n, -1))  7.13 us
    ppermute x8, starting transfers between devices, half_ring_rs(): cw = lax.ppermute(cw, axis, shift_perm(n, 1))  6.42 us
  transfers between devices with their start and end apart: 26, of which 18 were waited for; matrix products, arithmetic and copies ran while one was open for 9% of the time, Pallas kernels for 0%

profile of v1, /device:TPU:0, one launch (start us, length us, event | category | flops | bytes accessed | tf_op | source)
XLA Modules:
  0.0 163.1 jit_solution(1066475990135172298)
XLA Ops:
  2.0 3.5 %fusion.7 = f32[64,8192]{1,0:T(8,128)S(1)} fusion(f32[64,64]{1,0:T(8,128)S(1)} %bitcast.21, f32[64,8192]{1,0:T(8,128)} %param.7), kind=kOutput, calls=%fused_computation.48 | convolution fusion | flops 402653184 | bytes 4210688 | tf_op jit(solution)/shard_map/dot_general | solution.py:144
  5.8 10.2 %collective-permute-done = f32[64,1024]{1,0:T(8,128)S(1)} collective-permute-done((f32[64,1024]{1,0:T(8,128)S(1)}, f32[64,1024]{1,0:T(8,128)S(1)}, u32[]{:S(2)}, u32[]{:S(2)}) %collective-permute-start) | collective-permute-done | bytes 262176 | tf_op jit(solution)/shard_map/ppermute | solution.py:98
  16.2 3.2 %collective-permute-start.4 = (f32[64,1024]{1,0:T(8,128)S(1)}, f32[64,1024]{1,0:T(8,128)S(1)}, u32[]{:S(2)}, u32[]{:S(2)}) collective-permute-start(f32[64,1024]{1,0:T(8,128)S(1)} %get-tuple-element.12), channel_id=1, source_target_pairs={{0,28},{4,0},{8,4},{12,8},{16,12},{20,16},{24,20},{28,24},{1,29},{... | collective-permute-start | bytes 786440 | tf_op jit(solution)/shard_map/ppermute | solution.py:100
  19.4 5.4 %collective-permute-done.1 = f32[64,1024]{1,0:T(8,128)S(1)} collective-permute-done((f32[64,1024]{1,0:T(8,128)S(1)}, f32[64,1024]{1,0:T(8,128)S(1)}, u32[]{:S(2)}, u32[]{:S(2)}) %collective-permute-start.1) | collective-permute-done | bytes 262176 | tf_op jit(solution)/shard_map/ppermute | solution.py:98
  24.9 1.1 dynamic-slice_add_fusion.3
  26.0 3.2 %collective-permute-start.5 = (f32[64,1024]{1,0:T(8,128)S(1)}, f32[64,1024]{1,0:T(8,128)S(1)}, u32[]{:S(2)}, u32[]{:S(2)}) collective-permute-start(f32[64,1024]{1,0:T(8,128)S(1)} %get-tuple-element.10), channel_id=1, source_target_pairs={{0,28},{4,0},{8,4},{12,8},{16,12},{20,16},{24,20},{28,24},{1,29},{... | collective-permute-start | bytes 786440 | tf_op jit(solution)/shard_map/ppermute | solution.py:100
  29.3 4.6 %collective-permute-done.2 = f32[64,1024]{1,0:T(8,128)S(1)} collective-permute-done((f32[64,1024]{1,0:T(8,128)S(1)}, f32[64,1024]{1,0:T(8,128)S(1)}, u32[]{:S(2)}, u32[]{:S(2)}) %collective-permute-start.2) | collective-permute-done | bytes 262176 | tf_op jit(solution)/shard_map/ppermute | solution.py:98
  33.9 1.1 dynamic-slice_add_fusion.2
  35.0 2.0 %collective-permute-start.3 = (f32[64,1024]{1,0:T(8,128)S(1)}, f32[64,1024]{1,0:T(8,128)S(1)}, u32[]{:S(2)}, u32[]{:S(2)}) collective-permute-start(f32[64,1024]{1,0:T(8,128)S(1)} %get-tuple-element.7), channel_id=1, source_target_pairs={{0,4},{4,8},{8,12},{12,16},{16,20},{20,24},{24,28},{28,0},{1,5},{5... | collective-permute-start | bytes 786440 | tf_op jit(solution)/shard_map/ppermute | solution.py:98
  37.0 1.3 collective-permute-start.6
  38.3 4.3 %collective-permute-done.3 = f32[64,1024]{1,0:T(8,128)S(1)} collective-permute-done((f32[64,1024]{1,0:T(8,128)S(1)}, f32[64,1024]{1,0:T(8,128)S(1)}, u32[]{:S(2)}, u32[]{:S(2)}) %collective-permute-start.3) | collective-permute-done | bytes 262176 | tf_op jit(solution)/shard_map/ppermute | solution.py:98
  43.4 1.1 add_add_fusion
  44.5 1.6 %collective-permute-start.7 = (f32[64,256]{1,0:T(8,128)S(1)}, f32[64,256]{1,0:T(8,128)S(1)}, u32[]{:S(2)}, u32[]{:S(2)}) collective-permute-start(f32[64,256]{1,0:T(8,128)S(1)} %constant_dynamic-slice_fusion.3), channel_id=1, source_target_pairs={{0,1},{1,2},{2,3},{3,0},{4,5},{5,6},{6,7},{7,4},{8,9},{9,10},{10,1... | collective-permute-start | bytes 196616 | tf_op jit(solution)/shard_map/ppermute | solution.py:98
  46.2 3.9 %collective-permute-done.7 = f32[64,256]{1,0:T(8,128)S(1)} collective-permute-done((f32[64,256]{1,0:T(8,128)S(1)}, f32[64,256]{1,0:T(8,128)S(1)}, u32[]{:S(2)}, u32[]{:S(2)}) %collective-permute-start.7) | collective-permute-done | bytes 65568 | tf_op jit(solution)/shard_map/ppermute | solution.py:98
  50.5 2.9 %collective-permute-start.9 = (f32[64,256]{1,0:T(8,128)S(1)}, f32[64,256]{1,0:T(8,128)S(1)}, u32[]{:S(2)}, u32[]{:S(2)}) collective-permute-start(f32[64,256]{1,0:T(8,128)S(1)} %get-tuple-element.14), channel_id=1, source_target_pairs={{0,3},{1,0},{2,1},{3,2},{4,7},{5,4},{6,5},{7,6},{8,11},{9,8},{10,9... | collective-permute-start | bytes 196616 | tf_op jit(solution)/shard_map/ppermute | solution.py:100
  53.4 2.2 %collective-permute-done.8 = f32[64,256]{1,0:T(8,128)S(1)} collective-permute-done((f32[64,256]{1,0:T(8,128)S(1)}, f32[64,256]{1,0:T(8,128)S(1)}, u32[]{:S(2)}, u32[]{:S(2)}) %collective-permute-start.8) | collective-permute-done | bytes 65568 | tf_op jit(solution)/shard_map/ppermute | solution.py:98
  55.8 1.5 collective-permute-start.10
  57.3 3.6 %collective-permute-done.10 = f32[64,64]{1,0:T(8,128)S(1)} collective-permute-done((f32[64,64]{1,0:T(8,128)S(1)}, f32[64,64]{1,0:T(8,128)S(1)}, u32[]{:S(2)}, u32[]{:S(2)}) %collective-permute-start.10) | collective-permute-done | bytes 16416 | tf_op jit(solution)/shard_map/ppermute | solution.py:98
  61.4 3.0 %collective-permute-start.12 = (f32[64,64]{1,0:T(8,128)S(1)}, f32[64,64]{1,0:T(8,128)S(1)}, u32[]{:S(2)}, u32[]{:S(2)}) collective-permute-start(f32[64,64]{1,0:T(8,128)S(1)} %get-tuple-element.16), channel_id=1, source_target_pairs={{0,96},{32,0},{64,32},{96,64},{1,97},{33,1},{65,33},{97,65},{2,98}... | collective-permute-start | bytes 49160 | tf_op jit(solution)/shard_map/ppermute | solution.py:100
  64.3 1.9 %collective-permute-done.11 = f32[64,64]{1,0:T(8,128)S(1)} collective-permute-done((f32[64,64]{1,0:T(8,128)S(1)}, f32[64,64]{1,0:T(8,128)S(1)}, u32[]{:S(2)}, u32[]{:S(2)}) %collective-permute-start.11) | collective-permute-done | bytes 16416 | tf_op jit(solution)/shard_map/ppermute | solution.py:98
  67.0 2.8 %collective-permute-start.14 = (f32[64,64]{1,0:T(8,128)S(1)}, f32[64,64]{1,0:T(8,128)S(1)}, u32[]{:S(2)}, u32[]{:S(2)}) collective-permute-start(f32[64,64]{1,0:T(8,128)S(1)} %add_add_fusion.2), channel_id=1, source_target_pairs={{0,96},{32,0},{64,32},{96,64},{1,97},{33,1},{65,33},{97,65},{2,98}... | collective-permute-start | bytes 49160 | tf_op jit(solution)/shard_map/ppermute | solution.py:123
  69.8 1.8 %collective-permute-done.13 = f32[64,64]{1,0:T(8,128)S(1)} collective-permute-done((f32[64,64]{1,0:T(8,128)S(1)}, f32[64,64]{1,0:T(8,128)S(1)}, u32[]{:S(2)}, u32[]{:S(2)}) %collective-permute-start.13) | collective-permute-done | bytes 16416 | tf_op jit(solution)/shard_map/ppermute | solution.py:120
  71.8 5.0 %collective-permute-done.15 = f32[64,64]{1,0:T(8,128)S(1)} collective-permute-done((f32[64,64]{1,0:T(8,128)S(1)}, f32[64,64]{1,0:T(8,128)S(1)}, u32[]{:S(2)}, u32[]{:S(2)}) %collective-permute-start.15) | collective-permute-done | bytes 16416 | tf_op jit(solution)/shard_map/ppermute | solution.py:120
  76.9 0.9 collective-permute-start.16
  77.8 2.5 %collective-permute-start.17 = (f32[64,256]{0,1:T(8,128)S(1)}, f32[64,256]{0,1:T(8,128)S(1)}, u32[]{:S(2)}, u32[]{:S(2)}) collective-permute-start(f32[64,256]{0,1:T(8,128)S(1)} %constant_dynamic-update-slice_fusion.12), channel_id=1, source_target_pairs={{0,3},{1,0},{2,1},{3,2},{4,7},{5,4},{6,5},{7,6},{8,11},{9,8},{10,9... | collective-permute-start | bytes 196616 | tf_op jit(solution)/shard_map/ppermute | solution.py:123
  80.4 2.8 %collective-permute-done.16 = f32[64,256]{0,1:T(8,128)S(1)} collective-permute-done((f32[64,256]{0,1:T(8,128)S(1)}, f32[64,256]{0,1:T(8,128)S(1)}, u32[]{:S(2)}, u32[]{:S(2)}) %collective-permute-start.16) | collective-permute-done | bytes 65568 | tf_op jit(solution)/shard_map/ppermute | solution.py:120
  83.3 6.1 %collective-permute-done.18 = f32[64,256]{0,1:T(8,128)S(1)} collective-permute-done((f32[64,256]{0,1:T(8,128)S(1)}, f32[64,256]{0,1:T(8,128)S(1)}, u32[]{:S(2)}, u32[]{:S(2)}) %collective-permute-start.18) | collective-permute-done | bytes 65568 | tf_op jit(solution)/shard_map/ppermute | solution.py:120
  89.4 2.1 %collective-permute-start.19 = (f32[64,1024]{0,1:T(8,128)S(1)}, f32[64,1024]{0,1:T(8,128)S(1)}, u32[]{:S(2)}, u32[]{:S(2)}) collective-permute-start(f32[64,1024]{0,1:T(8,128)S(1)} %constant_dynamic-update-slice_fusion.8), channel_id=1, source_target_pairs={{0,4},{4,8},{8,12},{12,16},{16,20},{20,24},{24,28},{28,0},{1,5},{5... | collective-permute-start | bytes 786440 | tf_op jit(solution)/shard_map/ppermute | solution.py:120
  91.5 1.2 collective-permute-start.20
  92.7 2.7 %copy.7 = f32[64,8192]{0,1:T(8,128)} copy(f32[64,8192]{1,0:T(8,128)S(1)} %copy-done.1) | data formatting | bytes 4194304 | tf_op args[0]
  95.5 2.8 %gather_fusion = f32[64,64]{1,0:T(8,128)S(1)} fusion(f32[64,8192]{0,1:T(8,128)} %copy.7, s32[1024]{0:T(1024)S(1)} %pad_clamp_fusion), kind=kCustom, calls=%fused_computation.clone | custom fusion | bytes 33024 | tf_op jit(solution)/shard_map/jit(_take)/gather | solution.py:143
  98.2 3.3 %collective-permute-done.19 = f32[64,1024]{0,1:T(8,128)S(1)} collective-permute-done((f32[64,1024]{0,1:T(8,128)S(1)}, f32[64,1024]{0,1:T(8,128)S(1)}, u32[]{:S(2)}, u32[]{:S(2)}) %collective-permute-start.19) | collective-permute-done | bytes 262176 | tf_op jit(solution)/shard_map/ppermute | solution.py:120
  101.6 2.6 %collective-permute-start.21 = (f32[64,1024]{0,1:T(8,128)S(1)}, f32[64,1024]{0,1:T(8,128)S(1)}, u32[]{:S(2)}, u32[]{:S(2)}) collective-permute-start(f32[64,1024]{0,1:T(8,128)S(1)} %collective-permute-done.19), channel_id=1, source_target_pairs={{0,4},{4,8},{8,12},{12,16},{16,20},{20,24},{24,28},{28,0},{1,5},{5... | collective-permute-start | bytes 786440 | tf_op jit(solution)/shard_map/ppermute | solution.py:120
  105.3 2.2 %broadcast_in_dim.19 = f32[64,8192]{0,1:T(8,128)} broadcast(f32[]{:T(128)} %constant.171.clone.1), dimensions={} | broadcast | bytes 2097156 | tf_op jit(solution)/shard_map/broadcast_in_dim | solution.py:116
  107.6 0.8 constant_dynamic-update-slice_fusion.7
  108.4 5.4 %collective-permute-done.21 = f32[64,1024]{0,1:T(8,128)S(1)} collective-permute-done((f32[64,1024]{0,1:T(8,128)S(1)}, f32[64,1024]{0,1:T(8,128)S(1)}, u32[]{:S(2)}, u32[]{:S(2)}) %collective-permute-start.21) | collective-permute-done | bytes 262176 | tf_op jit(solution)/shard_map/ppermute | solution.py:120
  113.8 4.9 %collective-permute-start.23 = (f32[64,1024]{0,1:T(8,128)S(1)}, f32[64,1024]{0,1:T(8,128)S(1)}, u32[]{:S(2)}, u32[]{:S(2)}) collective-permute-start(f32[64,1024]{0,1:T(8,128)S(1)} %collective-permute-done.21), channel_id=1, source_target_pairs={{0,4},{4,8},{8,12},{12,16},{16,20},{20,24},{24,28},{28,0},{1,5},{5... | collective-permute-start | bytes 786440 | tf_op jit(solution)/shard_map/ppermute | solution.py:120
  118.7 0.9 constant_dynamic-update-slice_fusion.6
  119.5 1.9 %constant_dynamic-update-slice_fusion.5 = f32[64,8192]{0,1:T(8,128)} fusion(f32[64,8192]{0,1:T(8,128)} %constant_dynamic-update-slice_fusion.6, f32[64,1024]{0,1:T(8,128)} %collective-permute-done.20, s32[]{:T(128)S(6)} %select_n.191), kind=kLoop, calls=%fused_computation.24 | loop fusion | bytes 1048580 | tf_op jit(solution)/shard_map/dynamic_update_slice | solution.py:124
  122.2 3.1 %collective-permute-done.23 = f32[64,1024]{0,1:T(8,128)S(1)} collective-permute-done((f32[64,1024]{0,1:T(8,128)S(1)}, f32[64,1024]{0,1:T(8,128)S(1)}, u32[]{:S(2)}, u32[]{:S(2)}) %collective-permute-start.23) | collective-permute-done | bytes 262176 | tf_op jit(solution)/shard_map/ppermute | solution.py:120
  125.4 2.5 %collective-permute-start.25 = (f32[64,1024]{0,1:T(8,128)S(1)}, f32[64,1024]{0,1:T(8,128)S(1)}, u32[]{:S(2)}, u32[]{:S(2)}) collective-permute-start(f32[64,1024]{0,1:T(8,128)S(1)} %collective-permute-done.23), channel_id=1, source_target_pairs={{0,4},{4,8},{8,12},{12,16},{16,20},{20,24},{24,28},{28,0},{1,5},{5... | collective-permute-start | bytes 786440 | tf_op jit(solution)/shard_map/ppermute | solution.py:120
  129.5 1.5 collective-permute-done.24
  131.8 3.9 %collective-permute-done.25 = f32[64,1024]{0,1:T(8,128)S(1)} collective-permute-done((f32[64,1024]{0,1:T(8,128)S(1)}, f32[64,1024]{0,1:T(8,128)S(1)}, u32[]{:S(2)}, u32[]{:S(2)}) %collective-permute-start.25) | collective-permute-done | bytes 262176 | tf_op jit(solution)/shard_map/ppermute | solution.py:120
  135.8 0.8 constant_dynamic-update-slice_fusion
  136.6 2.8 %gather_fusion.1 = f32[64,64]{1,0:T(8,128)S(1)} fusion(f32[64,8192]{0,1:T(8,128)} %constant_dynamic-update-slice_fusion, s32[1024]{0:T(1024)S(1)} %pad_clamp_fusion), kind=kCustom, calls=%fused_computation.1.clone | custom fusion | bytes 33024 | tf_op jit(solution)/shard_map/jit(_take)/gather | solution.py:146
  140.8 13.1 %shard_map.68 = (f32[64,64]{1,0:T(8,128)}, f32[1,64]{1,0:T(1,128)}) custom-call(f32[64,64]{1,0:T(8,128)} %copy.12.m_ref, f32[64,64]{1,0:T(8,128)} %broadcast_select_fusion.mt_ref, f32[1,64]{1,0:T(1,128)} %convert_bitcast_fusion.acc_ref), custom_call_target="tpu_custom_call" | custom-call | tf_op jit(solution)/shard_map/pallas_call | solution.py:76
  154.0 1.1 fusion
  155.1 8.1 %convolution_subtract_fusion = f32[64,8192]{1,0:T(8,128)} fusion(f32[64,8192]{1,0:T(8,128)S(1)} %copy-done.1, f32[64,64]{1,0:T(8,128)S(1)} %fusion, f32[64,8192]{0,1:T(8,128)} %constant_dynamic-update-slice_fusion), kind=kOutput, calls=%fused_computation.2 | convolution fusion | flops 403177472 | bytes 6307840 | tf_op jit(solution)/shard_map/dot_general | solution.py:149
  (65 shorter events, 10.8 us)
Async XLA Ops:
  0.6 1.0 copy-start
  5.4 10.6 %copy-start.2 = (f32[64,8192]{1,0:T(8,128)}, f32[64,8192]{1,0:T(8,128)S(1)}, u32[]{:S(2)}) copy-start(f32[64,8192]{1,0:T(8,128)S(1)} %fusion.7) | copy-start | bytes 6291460
  5.5 58.9 %copy-start.3 = (s32[64]{0:T(128)S(1)}, s32[64]{0:T(128)}, u32[]{:S(2)}) copy-start(s32[64]{0:T(128)} %param.10) | copy-start | bytes 772
  5.5 10.5 %collective-permute-start = (f32[64,1024]{1,0:T(8,128)S(1)}, f32[64,1024]{1,0:T(8,128)S(1)}, u32[]{:S(2)}, u32[]{:S(2)}) collective-permute-start(f32[64,1024]{1,0:T(8,128)S(1)} %constant_dynamic-slice_fusion.5), channel_id=1, source_target_pairs={{0,4},{4,8},{8,12},{12,16},{16,20},{20,24},{24,28},{28,0},{1,5},{5... | collective-permute-start | bytes 786440 | tf_op jit(solution)/shard_map/ppermute | solution.py:98
  16.1 76.6 %copy-start.1 = (f32[64,8192]{1,0:T(8,128)S(1)}, f32[64,8192]{1,0:T(8,128)}, u32[]{:S(2)}) copy-start(f32[64,8192]{1,0:T(8,128)} %param.7) | copy-start | bytes 6291460
  16.1 8.8 %collective-permute-start.1 = (f32[64,1024]{1,0:T(8,128)S(1)}, f32[64,1024]{1,0:T(8,128)S(1)}, u32[]{:S(2)}, u32[]{:S(2)}) collective-permute-start(f32[64,1024]{1,0:T(8,128)S(1)} %get-tuple-element.11), channel_id=1, source_target_pairs={{0,4},{4,8},{8,12},{12,16},{16,20},{20,24},{24,28},{28,0},{1,5},{5... | collective-permute-start | bytes 786440 | tf_op jit(solution)/shard_map/ppermute | solution.py:98
  16.2 8.7 %collective-permute-start.4 = (f32[64,1024]{1,0:T(8,128)S(1)}, f32[64,1024]{1,0:T(8,128)S(1)}, u32[]{:S(2)}, u32[]{:S(2)}) collective-permute-start(f32[64,1024]{1,0:T(8,128)S(1)} %get-tuple-element.12), channel_id=1, source_target_pairs={{0,28},{4,0},{8,4},{12,8},{16,12},{20,16},{24,20},{28,24},{1,29},{... | collective-permute-start | bytes 786440 | tf_op jit(solution)/shard_map/ppermute | solution.py:100
  26.0 7.9 %collective-permute-start.2 = (f32[64,1024]{1,0:T(8,128)S(1)}, f32[64,1024]{1,0:T(8,128)S(1)}, u32[]{:S(2)}, u32[]{:S(2)}) collective-permute-start(f32[64,1024]{1,0:T(8,128)S(1)} %get-tuple-element.9), channel_id=1, source_target_pairs={{0,4},{4,8},{8,12},{12,16},{16,20},{20,24},{24,28},{28,0},{1,5},{5... | collective-permute-start | bytes 786440 | tf_op jit(solution)/shard_map/ppermute | solution.py:98
  26.0 7.8 %collective-permute-start.5 = (f32[64,1024]{1,0:T(8,128)S(1)}, f32[64,1024]{1,0:T(8,128)S(1)}, u32[]{:S(2)}, u32[]{:S(2)}) collective-permute-start(f32[64,1024]{1,0:T(8,128)S(1)} %get-tuple-element.10), channel_id=1, source_target_pairs={{0,28},{4,0},{8,4},{12,8},{16,12},{20,16},{24,20},{28,24},{1,29},{... | collective-permute-start | bytes 786440 | tf_op jit(solution)/shard_map/ppermute | solution.py:100
  35.0 7.7 %collective-permute-start.3 = (f32[64,1024]{1,0:T(8,128)S(1)}, f32[64,1024]{1,0:T(8,128)S(1)}, u32[]{:S(2)}, u32[]{:S(2)}) collective-permute-start(f32[64,1024]{1,0:T(8,128)S(1)} %get-tuple-element.7), channel_id=1, source_target_pairs={{0,4},{4,8},{8,12},{12,16},{16,20},{20,24},{24,28},{28,0},{1,5},{5... | collective-permute-start | bytes 786440 | tf_op jit(solution)/shard_map/ppermute | solution.py:98
  37.0 6.5 %collective-permute-start.6 = (f32[64,1024]{1,0:T(8,128)S(1)}, f32[64,1024]{1,0:T(8,128)}, u32[]{:S(2)}, u32[]{:S(2)}) collective-permute-start(f32[64,1024]{1,0:T(8,128)S(1)} %get-tuple-element.8), channel_id=1, source_target_pairs={{0,28},{4,0},{8,4},{12,8},{16,12},{20,16},{24,20},{28,24},{1,29},{... | collective-permute-start | bytes 786440 | tf_op jit(solution)/shard_map/ppermute | solution.py:100
  44.5 5.6 %collective-permute-start.7 = (f32[64,256]{1,0:T(8,128)S(1)}, f32[64,256]{1,0:T(8,128)S(1)}, u32[]{:S(2)}, u32[]{:S(2)}) collective-permute-start(f32[64,256]{1,0:T(8,128)S(1)} %constant_dynamic-slice_fusion.3), channel_id=1, source_target_pairs={{0,1},{1,2},{2,3},{3,0},{4,5},{5,6},{6,7},{7,4},{8,9},{9,10},{10,1... | collective-permute-start | bytes 196616 | tf_op jit(solution)/shard_map/ppermute | solution.py:98
  50.1 5.6 %collective-permute-start.8 = (f32[64,256]{1,0:T(8,128)S(1)}, f32[64,256]{1,0:T(8,128)S(1)}, u32[]{:S(2)}, u32[]{:S(2)}) collective-permute-start(f32[64,256]{1,0:T(8,128)S(1)} %get-tuple-element.13), channel_id=1, source_target_pairs={{0,1},{1,2},{2,3},{3,0},{4,5},{5,6},{6,7},{7,4},{8,9},{9,10},{10,1... | collective-permute-start | bytes 196616 | tf_op jit(solution)/shard_map/ppermute | solution.py:98
  50.5 5.1 %collective-permute-start.9 = (f32[64,256]{1,0:T(8,128)S(1)}, f32[64,256]{1,0:T(8,128)S(1)}, u32[]{:S(2)}, u32[]{:S(2)}) collective-permute-start(f32[64,256]{1,0:T(8,128)S(1)} %get-tuple-element.14), channel_id=1, source_target_pairs={{0,3},{1,0},{2,1},{3,2},{4,7},{5,4},{6,5},{7,6},{8,11},{9,8},{10,9... | collective-permute-start | bytes 196616 | tf_op jit(solution)/shard_map/ppermute | solution.py:100
  55.8 5.1 %collective-permute-start.10 = (f32[64,64]{1,0:T(8,128)S(1)}, f32[64,64]{1,0:T(8,128)S(1)}, u32[]{:S(2)}, u32[]{:S(2)}) collective-permute-start(f32[64,64]{1,0:T(8,128)S(1)} %constant_dynamic-slice_fusion.1), channel_id=1, source_target_pairs={{0,32},{32,64},{64,96},{96,0},{1,33},{33,65},{65,97},{97,1},{2,34}... | collective-permute-start | bytes 49160 | tf_op jit(solution)/shard_map/ppermute | solution.py:98
  61.0 5.2 %collective-permute-start.11 = (f32[64,64]{1,0:T(8,128)S(1)}, f32[64,64]{1,0:T(8,128)S(1)}, u32[]{:S(2)}, u32[]{:S(2)}) collective-permute-start(f32[64,64]{1,0:T(8,128)S(1)} %get-tuple-element.15), channel_id=1, source_target_pairs={{0,32},{32,64},{64,96},{96,0},{1,33},{33,65},{65,97},{97,1},{2,34}... | collective-permute-start | bytes 49160 | tf_op jit(solution)/shard_map/ppermute | solution.py:98
  61.4 4.8 %collective-permute-start.12 = (f32[64,64]{1,0:T(8,128)S(1)}, f32[64,64]{1,0:T(8,128)S(1)}, u32[]{:S(2)}, u32[]{:S(2)}) collective-permute-start(f32[64,64]{1,0:T(8,128)S(1)} %get-tuple-element.16), channel_id=1, source_target_pairs={{0,96},{32,0},{64,32},{96,64},{1,97},{33,1},{65,33},{97,65},{2,98}... | collective-permute-start | bytes 49160 | tf_op jit(solution)/shard_map/ppermute | solution.py:100
  66.4 5.2 %collective-permute-start.13 = (f32[64,64]{1,0:T(8,128)S(1)}, f32[64,64]{1,0:T(8,128)S(1)}, u32[]{:S(2)}, u32[]{:S(2)}) collective-permute-start(f32[64,64]{1,0:T(8,128)S(1)} %add_add_fusion.2), channel_id=1, source_target_pairs={{0,32},{32,64},{64,96},{96,0},{1,33},{33,65},{65,97},{97,1},{2,34}... | collective-permute-start | bytes 49160 | tf_op jit(solution)/shard_map/ppermute | solution.py:120
  67.0 4.8 %collective-permute-start.14 = (f32[64,64]{1,0:T(8,128)S(1)}, f32[64,64]{1,0:T(8,128)S(1)}, u32[]{:S(2)}, u32[]{:S(2)}) collective-permute-start(f32[64,64]{1,0:T(8,128)S(1)} %add_add_fusion.2), channel_id=1, source_target_pairs={{0,96},{32,0},{64,32},{96,64},{1,97},{33,1},{65,33},{97,65},{2,98}... | collective-permute-start | bytes 49160 | tf_op jit(solution)/shard_map/ppermute | solution.py:123
  71.6 5.2 %collective-permute-start.15 = (f32[64,64]{1,0:T(8,128)S(1)}, f32[64,64]{1,0:T(8,128)S(1)}, u32[]{:S(2)}, u32[]{:S(2)}) collective-permute-start(f32[64,64]{1,0:T(8,128)S(1)} %collective-permute-done.13), channel_id=1, source_target_pairs={{0,32},{32,64},{64,96},{96,0},{1,33},{33,65},{65,97},{97,1},{2,34}... | collective-permute-start | bytes 49160 | tf_op jit(solution)/shard_map/ppermute | solution.py:120
  71.8 32.3 %copy-start.4 = (s32[64]{0:T(128)S(1)}, s32[64]{0:T(128)}, u32[]{:S(2)}) copy-start(s32[64]{0:T(128)} %param.11) | copy-start | bytes 772
  76.9 6.3 %collective-permute-start.16 = (f32[64,256]{0,1:T(8,128)S(1)}, f32[64,256]{0,1:T(8,128)S(1)}, u32[]{:S(2)}, u32[]{:S(2)}) collective-permute-start(f32[64,256]{0,1:T(8,128)S(1)} %constant_dynamic-update-slice_fusion.12), channel_id=1, source_target_pairs={{0,1},{1,2},{2,3},{3,0},{4,5},{5,6},{6,7},{7,4},{8,9},{9,10},{10,1... | collective-permute-start | bytes 196616 | tf_op jit(solution)/shard_map/ppermute | solution.py:120
  77.8 5.4 %collective-permute-start.17 = (f32[64,256]{0,1:T(8,128)S(1)}, f32[64,256]{0,1:T(8,128)S(1)}, u32[]{:S(2)}, u32[]{:S(2)}) collective-permute-start(f32[64,256]{0,1:T(8,128)S(1)} %constant_dynamic-update-slice_fusion.12), channel_id=1, source_target_pairs={{0,3},{1,0},{2,1},{3,2},{4,7},{5,4},{6,5},{7,6},{8,11},{9,8},{10,9... | collective-permute-start | bytes 196616 | tf_op jit(solution)/shard_map/ppermute | solution.py:123
  83.2 6.2 %collective-permute-start.18 = (f32[64,256]{0,1:T(8,128)S(1)}, f32[64,256]{0,1:T(8,128)S(1)}, u32[]{:S(2)}, u32[]{:S(2)}) collective-permute-start(f32[64,256]{0,1:T(8,128)S(1)} %collective-permute-done.16), channel_id=1, source_target_pairs={{0,1},{1,2},{2,3},{3,0},{4,5},{5,6},{6,7},{7,4},{8,9},{9,10},{10,1... | collective-permute-start | bytes 196616 | tf_op jit(solution)/shard_map/ppermute | solution.py:120
  89.4 12.2 %collective-permute-start.19 = (f32[64,1024]{0,1:T(8,128)S(1)}, f32[64,1024]{0,1:T(8,128)S(1)}, u32[]{:S(2)}, u32[]{:S(2)}) collective-permute-start(f32[64,1024]{0,1:T(8,128)S(1)} %constant_dynamic-update-slice_fusion.8), channel_id=1, source_target_pairs={{0,4},{4,8},{8,12},{12,16},{16,20},{20,24},{24,28},{28,0},{1,5},{5... | collective-permute-start | bytes 786440 | tf_op jit(solution)/shard_map/ppermute | solution.py:120
  91.5 13.1 %collective-permute-start.20 = (f32[64,1024]{0,1:T(8,128)S(1)}, f32[64,1024]{0,1:T(8,128)}, u32[]{:S(2)}, u32[]{:S(2)}) collective-permute-start(f32[64,1024]{0,1:T(8,128)S(1)} %constant_dynamic-update-slice_fusion.8), channel_id=1, source_target_pairs={{0,28},{4,0},{8,4},{12,8},{16,12},{20,16},{24,20},{28,24},{1,29},{... | collective-permute-start | bytes 786440 | tf_op jit(solution)/shard_map/ppermute | solution.py:123
  101.6 12.2 %collective-permute-start.21 = (f32[64,1024]{0,1:T(8,128)S(1)}, f32[64,1024]{0,1:T(8,128)S(1)}, u32[]{:S(2)}, u32[]{:S(2)}) collective-permute-start(f32[64,1024]{0,1:T(8,128)S(1)} %collective-permute-done.19), channel_id=1, source_target_pairs={{0,4},{4,8},{8,12},{12,16},{16,20},{20,24},{24,28},{28,0},{1,5},{5... | collective-permute-start | bytes 786440 | tf_op jit(solution)/shard_map/ppermute | solution.py:120
  104.7 16.7 %collective-permute-start.22 = (f32[64,1024]{0,1:T(8,128)}, f32[64,1024]{0,1:T(8,128)S(1)}, u32[]{:S(2)}, u32[]{:S(2)}) collective-permute-start(f32[64,1024]{0,1:T(8,128)} %collective-permute-done.20), channel_id=1, source_target_pairs={{0,28},{4,0},{8,4},{12,8},{16,12},{20,16},{24,20},{28,24},{1,29},{... | collective-permute-start | bytes 786440 | tf_op jit(solution)/shard_map/ppermute | solution.py:123
  113.8 11.6 %collective-permute-start.23 = (f32[64,1024]{0,1:T(8,128)S(1)}, f32[64,1024]{0,1:T(8,128)S(1)}, u32[]{:S(2)}, u32[]{:S(2)}) collective-permute-start(f32[64,1024]{0,1:T(8,128)S(1)} %collective-permute-done.21), channel_id=1, source_target_pairs={{0,4},{4,8},{8,12},{12,16},{16,20},{20,24},{24,28},{28,0},{1,5},{5... | collective-permute-start | bytes 786440 | tf_op jit(solution)/shard_map/ppermute | solution.py:120
  121.4 9.6 %collective-permute-start.24 = (f32[64,1024]{0,1:T(8,128)S(1)}, f32[64,1024]{0,1:T(8,128)S(1)}, u32[]{:S(2)}, u32[]{:S(2)}) collective-permute-start(f32[64,1024]{0,1:T(8,128)S(1)} %collective-permute-done.22), channel_id=1, source_target_pairs={{0,28},{4,0},{8,4},{12,8},{16,12},{20,16},{24,20},{28,24},{1,29},{... | collective-permute-start | bytes 786440 | tf_op jit(solution)/shard_map/ppermute | solution.py:123
  125.4 10.4 %collective-permute-start.25 = (f32[64,1024]{0,1:T(8,128)S(1)}, f32[64,1024]{0,1:T(8,128)S(1)}, u32[]{:S(2)}, u32[]{:S(2)}) collective-permute-start(f32[64,1024]{0,1:T(8,128)S(1)} %collective-permute-done.23), channel_id=1, source_target_pairs={{0,4},{4,8},{8,12},{12,16},{16,20},{20,24},{24,28},{28,0},{1,5},{5... | collective-permute-start | bytes 786440 | tf_op jit(solution)/shard_map/ppermute | solution.py:120

commit v2 on v1

--- a/solution.py
+++ b/solution.py
@@ -65,7 +65,7 @@
 
     c0 = jnp.zeros((n, n), jnp.float32)
     r0 = jnp.zeros((1, n), jnp.float32)
-    c, ratios = lax.fori_loop(0, n, step, (c0, r0))
+    c, ratios = lax.fori_loop(0, n, step, (c0, r0), unroll=8)
     c_ref[...] = c
     r_ref[...] = ratios
 
@@ -124,12 +124,35 @@
             out = lax.dynamic_update_slice_in_dim(out, ccw, ((i + s) % n) * width, 1)
     return out
 
+def direct_rs(x, axis, n):
+    i = lax.axis_index(axis)
+    width = x.shape[1] // n
+    chunk = lambda c: lax.dynamic_slice_in_dim(x, (c % n) * width, width, 1)
+    total = chunk(i)
+    for d in SHIFTS[n]:
+        total = total + lax.ppermute(chunk(i + d), axis, shift_perm(n, d))
+    return total
+
+
+def direct_ag(x, axis, n):
+    i = lax.axis_index(axis)
+    width = x.shape[1]
+    out = jnp.zeros(x.shape[:1] + (n * width,), x.dtype)
+    out = lax.dynamic_update_slice_in_dim(out, x, i * width, 1)
+    for d in SHIFTS[n]:
+        got = lax.ppermute(x, axis, shift_perm(n, d))
+        out = lax.dynamic_update_slice_in_dim(out, got, ((i - d) % n) * width, 1)
+    return out
+
+
+SHIFTS = {2: (1,), 4: (1, -1, 2)}
+
 
 def ring_allreduce(x, phases):
     for axis, n in phases:
-        x = half_ring_rs(x, axis, n)
+        x = direct_rs(x, axis, n) if n in SHIFTS else half_ring_rs(x, axis, n)
     for axis, n in reversed(phases):
-        x = half_ring_ag(x, axis, n)
+        x = direct_ag(x, axis, n) if n in SHIFTS else half_ring_ag(x, axis, n)
     return x
 
 

time: 165 us -> 156 us (0.945)
  Pallas kernels: 13.1 us -> 8.64 us
  starting transfers between devices: 40.8 us -> 37.8 us
    ppermute x0 -> x12, waiting for transfers between devices: none -> 18.4 us  [the longest x6 10.7 us: direct_ag(): got = lax.ppermute(x, axis, shift_perm(n, d))]
    ppermute x0 -> x12, starting transfers between devices: none -> 17.9 us  [the longest x6 10.4 us: direct_rs(): total = total + lax.ppermute(chunk(i + d), axis, shift_perm(n, d))]
    ppermute x8 -> x4, starting transfers between devices: 13.7 us -> 1.8 us  [half_ring_ag(): cw = lax.ppermute(cw, axis, shift_perm(n, 1))]
    ppermute x8 -> x4, waiting for transfers between devices: 36.3 us -> 24.8 us  [half_ring_rs(): cw = lax.ppermute(cw, axis, shift_perm(n, 1))]
    ppermute x8 -> x4, waiting for transfers between devices: 31.4 us -> 25.2 us  [half_ring_ag(): cw = lax.ppermute(cw, axis, shift_perm(n, 1))]
    ppermute x5 -> x3, starting transfers between devices: 13.6 us -> 7.97 us  [half_ring_rs(): ccw = lax.ppermute(ccw, axis, shift_perm(n, -1))]
    pallas_call x1, Pallas kernels: 13.1 us -> 8.64 us  [border(): pl.pallas_call(_border_kernel, out_shape=(jax.ShapeDtypeStruct((n, n), jn...]
    ppermute x8 -> x4, starting transfers between devices: 6.42 us -> 2.17 us  [half_ring_rs(): cw = lax.ppermute(cw, axis, shift_perm(n, 1))]
  transfers between devices with their start and end apart: 26 -> 26, of which waited for: 18 -> 20; matrix products, arithmetic and copies ran while one was open for 9% -> 10% of each run, Pallas kernels for 0% -> 0%
where the time goes in v2:
time: 156 us; the launch traced here: 155 us
  waiting for transfers between devices  68.9 us (44%)
  starting transfers between devices  37.8 us (24%)
  local copies, waits for them, and re-layouts  19.7 us (13%)
  matrix products  13 us (8%)
  Pallas kernels  8.64 us (6%)
  other arithmetic  6.04 us (4%)
    ppermute x4, waiting for transfers between devices, half_ring_ag(): cw = lax.ppermute(cw, axis, shift_perm(n, 1))  25.2 us
    ppermute x4, waiting for transfers between devices, half_ring_rs(): cw = lax.ppermute(cw, axis, shift_perm(n, 1))  24.8 us
    ppermute x6, waiting for transfers between devices, direct_ag(): got = lax.ppermute(x, axis, shift_perm(n, d))  10.7 us
    ppermute x6, starting transfers between devices, direct_rs(): total = total + lax.ppermute(chunk(i + d), axis, shift_perm(n, d))  10.4 us
    pallas_call x1, Pallas kernels, border(): pl.pallas_call(_border_kernel, out_shape=(jax.ShapeDtypeStruct((n, n), jn...  8.64 us
    dot_general x1, matrix products, on_device(): new_inverse = inverse_rows - jnp.dot(factor, full_weights, precision=HI)  8.07 us
    ppermute x3, starting transfers between devices, half_ring_ag(): ccw = lax.ppermute(ccw, axis, shift_perm(n, -1))  7.99 us
    ppermute x3, starting transfers between devices, half_ring_rs(): ccw = lax.ppermute(ccw, axis, shift_perm(n, -1))  7.97 us
  transfers between devices with their start and end apart: 26, of which 20 were waited for; matrix products, arithmetic and copies ran while one was open for 10% of the time, Pallas kernels for 0%

profile of v2, /device:TPU:0, one launch (start us, length us, event | category | flops | bytes accessed | tf_op | source)
XLA Modules:
  0.0 155.0 jit_solution(13526335893045698496)
XLA Ops:
  2.0 3.5 %fusion.7 = f32[64,8192]{1,0:T(8,128)S(1)} fusion(f32[64,64]{1,0:T(8,128)S(1)} %bitcast.21, f32[64,8192]{1,0:T(8,128)} %param.7), kind=kOutput, calls=%fused_computation.48 | convolution fusion | flops 402653184 | bytes 4210688 | tf_op jit(solution)/shard_map/dot_general | solution.py:167
  5.8 10.2 %collective-permute-done = f32[64,1024]{1,0:T(8,128)S(1)} collective-permute-done((f32[64,1024]{1,0:T(8,128)S(1)}, f32[64,1024]{1,0:T(8,128)S(1)}, u32[]{:S(2)}, u32[]{:S(2)}) %collective-permute-start) | collective-permute-done | bytes 262176 | tf_op jit(solution)/shard_map/ppermute | solution.py:98
  16.2 3.2 %collective-permute-start.4 = (f32[64,1024]{1,0:T(8,128)S(1)}, f32[64,1024]{1,0:T(8,128)S(1)}, u32[]{:S(2)}, u32[]{:S(2)}) collective-permute-start(f32[64,1024]{1,0:T(8,128)S(1)} %get-tuple-element.12), channel_id=1, source_target_pairs={{0,28},{4,0},{8,4},{12,8},{16,12},{20,16},{24,20},{28,24},{1,29},{... | collective-permute-start | bytes 786440 | tf_op jit(solution)/shard_map/ppermute | solution.py:100
  19.4 5.4 %collective-permute-done.1 = f32[64,1024]{1,0:T(8,128)S(1)} collective-permute-done((f32[64,1024]{1,0:T(8,128)S(1)}, f32[64,1024]{1,0:T(8,128)S(1)}, u32[]{:S(2)}, u32[]{:S(2)}) %collective-permute-start.1) | collective-permute-done | bytes 262176 | tf_op jit(solution)/shard_map/ppermute | solution.py:98
  24.9 1.8 %dynamic-slice_add_fusion.3 = (f32[64,1024]{1,0:T(8,128)}, f32[64,1024]{1,0:T(8,128)S(1)}) fusion(f32[64,1024]{1,0:T(8,128)S(1)} %collective-permute-done.1, f32[64,8192]{1,0:T(8,128)} %copy-done.2, s32[]{:T(128)S(6)} %select_n.189, f32[64,1024]{1,0:T(8,128)S(1)} %collective-permute-done.4, s32[]{:T(128)S(6)} %select_n.195), kind=kLoop, calls=%fused_computation.7 | loop fusion | flops 131072 | bytes 1572872 | tf_op jit(solution)/shard_map/add | solution.py:102
  26.6 3.2 %collective-permute-start.5 = (f32[64,1024]{1,0:T(8,128)S(1)}, f32[64,1024]{1,0:T(8,128)S(1)}, u32[]{:S(2)}, u32[]{:S(2)}) collective-permute-start(f32[64,1024]{1,0:T(8,128)S(1)} %get-tuple-element.10), channel_id=1, source_target_pairs={{0,28},{4,0},{8,4},{12,8},{16,12},{20,16},{24,20},{28,24},{1,29},{... | collective-permute-start | bytes 786440 | tf_op jit(solution)/shard_map/ppermute | solution.py:100
  29.9 4.8 %collective-permute-done.2 = f32[64,1024]{1,0:T(8,128)S(1)} collective-permute-done((f32[64,1024]{1,0:T(8,128)}, f32[64,1024]{1,0:T(8,128)S(1)}, u32[]{:S(2)}, u32[]{:S(2)}) %collective-permute-start.2) | collective-permute-done | bytes 262176 | tf_op jit(solution)/shard_map/ppermute | solution.py:98
  34.7 1.1 dynamic-slice_add_fusion.2
  35.8 1.8 %collective-permute-start.3 = (f32[64,1024]{1,0:T(8,128)S(1)}, f32[64,1024]{1,0:T(8,128)S(1)}, u32[]{:S(2)}, u32[]{:S(2)}) collective-permute-start(f32[64,1024]{1,0:T(8,128)S(1)} %get-tuple-element.7), channel_id=1, source_target_pairs={{0,4},{4,8},{8,12},{12,16},{16,20},{20,24},{24,28},{28,0},{1,5},{5... | collective-permute-start | bytes 786440 | tf_op jit(solution)/shard_map/ppermute | solution.py:98
  37.6 1.5 collective-permute-start.6
  39.1 4.3 %collective-permute-done.3 = f32[64,1024]{1,0:T(8,128)S(1)} collective-permute-done((f32[64,1024]{1,0:T(8,128)S(1)}, f32[64,1024]{1,0:T(8,128)S(1)}, u32[]{:S(2)}, u32[]{:S(2)}) %collective-permute-start.3) | collective-permute-done | bytes 262176 | tf_op jit(solution)/shard_map/ppermute | solution.py:98
  44.0 1.0 add_add_fusion
  45.0 1.6 %collective-permute-start.7 = (f32[64,256]{1,0:T(8,128)S(1)}, f32[64,256]{1,0:T(8,128)S(1)}, u32[]{:S(2)}, u32[]{:S(2)}) collective-permute-start(f32[64,256]{1,0:T(8,128)S(1)} %get-tuple-element.13), channel_id=1, source_target_pairs={{0,1},{1,2},{2,3},{3,0},{4,5},{5,6},{6,7},{7,4},{8,9},{9,10},{10,1... | collective-permute-start | bytes 196616 | tf_op jit(solution)/shard_map/ppermute | solution.py:133
  46.6 1.7 %collective-permute-start.8 = (f32[64,256]{1,0:T(8,128)S(1)}, f32[64,256]{1,0:T(8,128)S(1)}, u32[]{:S(2)}, u32[]{:S(2)}) collective-permute-start(f32[64,256]{1,0:T(8,128)S(1)} %get-tuple-element.15), channel_id=1, source_target_pairs={{0,3},{1,0},{2,1},{3,2},{4,7},{5,4},{6,5},{7,6},{8,11},{9,8},{10,9... | collective-permute-start | bytes 196616 | tf_op jit(solution)/shard_map/ppermute | solution.py:133
  48.3 2.0 %collective-permute-start.9 = (f32[64,256]{1,0:T(8,128)S(1)}, f32[64,256]{1,0:T(8,128)S(1)}, u32[]{:S(2)}, u32[]{:S(2)}) collective-permute-start(f32[64,256]{1,0:T(8,128)S(1)} %get-tuple-element.14), channel_id=1, source_target_pairs={{0,2},{1,3},{2,0},{3,1},{4,6},{5,7},{6,4},{7,5},{8,10},{9,11},{10,... | collective-permute-start | bytes 196616 | tf_op jit(solution)/shard_map/ppermute | solution.py:133
  50.9 3.2 %collective-permute-done.9 = f32[64,256]{1,0:T(8,128)S(1)} collective-permute-done((f32[64,256]{1,0:T(8,128)S(1)}, f32[64,256]{1,0:T(8,128)S(1)}, u32[]{:S(2)}, u32[]{:S(2)}) %collective-permute-start.9) | collective-permute-done | bytes 65568 | tf_op jit(solution)/shard_map/ppermute | solution.py:133
  54.2 1.6 %collective-permute-start.10 = (f32[64,64]{1,0:T(8,128)S(1)}, f32[64,64]{1,0:T(8,128)S(1)}, u32[]{:S(2)}, u32[]{:S(2)}) collective-permute-start(f32[64,64]{1,0:T(8,128)S(1)} %get-tuple-element.16), channel_id=1, source_target_pairs={{0,32},{32,64},{64,96},{96,0},{1,33},{33,65},{65,97},{97,1},{2,34}... | collective-permute-start | bytes 49160 | tf_op jit(solution)/shard_map/ppermute | solution.py:133
  55.8 1.7 %collective-permute-start.11 = (f32[64,64]{1,0:T(8,128)S(1)}, f32[64,64]{1,0:T(8,128)S(1)}, u32[]{:S(2)}, u32[]{:S(2)}) collective-permute-start(f32[64,64]{1,0:T(8,128)S(1)} %get-tuple-element.18), channel_id=1, source_target_pairs={{0,96},{32,0},{64,32},{96,64},{1,97},{33,1},{65,33},{97,65},{2,98}... | collective-permute-start | bytes 49160 | tf_op jit(solution)/shard_map/ppermute | solution.py:133
  57.5 1.8 %collective-permute-start.12 = (f32[64,64]{1,0:T(8,128)S(1)}, f32[64,64]{1,0:T(8,128)S(1)}, u32[]{:S(2)}, u32[]{:S(2)}) collective-permute-start(f32[64,64]{1,0:T(8,128)S(1)} %get-tuple-element.17), channel_id=1, source_target_pairs={{0,64},{32,96},{64,0},{96,32},{1,65},{33,97},{65,1},{97,33},{2,66}... | collective-permute-start | bytes 49160 | tf_op jit(solution)/shard_map/ppermute | solution.py:133
  59.7 3.6 %collective-permute-done.12 = f32[64,64]{1,0:T(8,128)S(1)} collective-permute-done((f32[64,64]{1,0:T(8,128)S(1)}, f32[64,64]{1,0:T(8,128)S(1)}, u32[]{:S(2)}, u32[]{:S(2)}) %collective-permute-start.12) | collective-permute-done | bytes 16416 | tf_op jit(solution)/shard_map/ppermute | solution.py:133
  63.5 3.2 %collective-permute-start.14 = (f32[64,64]{1,0:T(8,128)S(1)}, f32[64,64]{1,0:T(8,128)S(1)}, u32[]{:S(2)}, u32[]{:S(2)}) collective-permute-start(f32[64,64]{1,0:T(8,128)S(1)} %add_add_fusion.2), channel_id=1, source_target_pairs={{0,96},{32,0},{64,32},{96,64},{1,97},{33,1},{65,33},{97,65},{2,98}... | collective-permute-start | bytes 49160 | tf_op jit(solution)/shard_map/ppermute | solution.py:143
  67.0 1.6 %collective-permute-done.13 = f32[64,64]{1,0:T(8,128)S(1)} collective-permute-done((f32[64,64]{1,0:T(8,128)S(1)}, f32[64,64]{1,0:T(8,128)S(1)}, u32[]{:S(2)}, u32[]{:S(2)}) %collective-permute-start.13) | collective-permute-done | bytes 16416 | tf_op jit(solution)/shard_map/ppermute | solution.py:143
  68.8 3.3 %collective-permute-done.15 = f32[64,64]{1,0:T(8,128)S(1)} collective-permute-done((f32[64,64]{1,0:T(8,128)S(1)}, f32[64,64]{1,0:T(8,128)S(1)}, u32[]{:S(2)}, u32[]{:S(2)}) %collective-permute-start.15) | collective-permute-done | bytes 16416 | tf_op jit(solution)/shard_map/ppermute | solution.py:143
  72.5 3.0 %collective-permute-start.17 = (f32[64,256]{0,1:T(8,128)S(1)}, f32[64,256]{0,1:T(8,128)S(1)}, u32[]{:S(2)}, u32[]{:S(2)}) collective-permute-start(f32[64,256]{0,1:T(8,128)S(1)} %constant_dynamic-update-slice_fusion.12), channel_id=1, source_target_pairs={{0,3},{1,0},{2,1},{3,2},{4,7},{5,4},{6,5},{7,6},{8,11},{9,8},{10,9... | collective-permute-start | bytes 196616 | tf_op jit(solution)/shard_map/ppermute | solution.py:143
  76.2 2.3 %collective-permute-done.16 = f32[64,256]{0,1:T(8,128)S(1)} collective-permute-done((f32[64,256]{0,1:T(8,128)S(1)}, f32[64,256]{0,1:T(8,128)S(1)}, u32[]{:S(2)}, u32[]{:S(2)}) %collective-permute-start.16) | collective-permute-done | bytes 65568 | tf_op jit(solution)/shard_map/ppermute | solution.py:143
  78.5 1.0 collective-permute-done.17
  79.5 2.5 %collective-permute-done.18 = f32[64,256]{0,1:T(8,128)S(1)} collective-permute-done((f32[64,256]{0,1:T(8,128)S(1)}, f32[64,256]{0,1:T(8,128)S(1)}, u32[]{:S(2)}, u32[]{:S(2)}) %collective-permute-start.18) | collective-permute-done | bytes 65568 | tf_op jit(solution)/shard_map/ppermute | solution.py:143
  82.0 1.8 %collective-permute-start.19 = (f32[64,1024]{0,1:T(8,128)S(1)}, f32[64,1024]{0,1:T(8,128)S(1)}, u32[]{:S(2)}, u32[]{:S(2)}) collective-permute-start(f32[64,1024]{0,1:T(8,128)S(1)} %constant_dynamic-update-slice_fusion.8), channel_id=1, source_target_pairs={{0,4},{4,8},{8,12},{12,16},{16,20},{20,24},{24,28},{28,0},{1,5},{5... | collective-permute-start | bytes 786440 | tf_op jit(solution)/shard_map/ppermute | solution.py:120
  83.8 1.5 collective-permute-start.20
  85.3 2.7 %copy.7 = f32[64,8192]{0,1:T(8,128)} copy(f32[64,8192]{1,0:T(8,128)S(1)} %copy-done.1) | data formatting | bytes 4194304 | tf_op args[0]
  88.1 2.8 %gather_fusion = f32[64,64]{1,0:T(8,128)S(1)} fusion(f32[64,8192]{0,1:T(8,128)} %copy.7, s32[1024]{0:T(1024)S(1)} %pad_clamp_fusion), kind=kCustom, calls=%fused_computation.clone | custom fusion | bytes 33024 | tf_op jit(solution)/shard_map/jit(_take)/gather | solution.py:166
  90.8 5.3 %collective-permute-done.19 = f32[64,1024]{0,1:T(8,128)S(1)} collective-permute-done((f32[64,1024]{0,1:T(8,128)S(1)}, f32[64,1024]{0,1:T(8,128)S(1)}, u32[]{:S(2)}, u32[]{:S(2)}) %collective-permute-start.19) | collective-permute-done | bytes 262176 | tf_op jit(solution)/shard_map/ppermute | solution.py:120
  96.7 3.3 %collective-permute-start.22 = (f32[64,1024]{0,1:T(8,128)}, f32[64,1024]{0,1:T(8,128)S(1)}, u32[]{:S(2)}, u32[]{:S(2)}) collective-permute-start(f32[64,1024]{0,1:T(8,128)} %collective-permute-done.20), channel_id=1, source_target_pairs={{0,28},{4,0},{8,4},{12,8},{16,12},{20,16},{24,20},{28,24},{1,29},{... | collective-permute-start | bytes 786440 | tf_op jit(solution)/shard_map/ppermute | solution.py:123
  99.9 2.2 %broadcast_in_dim.19 = f32[64,8192]{0,1:T(8,128)} broadcast(f32[]{:T(128)} %constant.166.clone.1), dimensions={} | broadcast | bytes 2097156 | tf_op jit(solution)/shard_map/broadcast_in_dim | solution.py:116
  102.2 0.8 constant_dynamic-update-slice_fusion.7
  103.0 6.3 %collective-permute-done.21 = f32[64,1024]{0,1:T(8,128)S(1)} collective-permute-done((f32[64,1024]{0,1:T(8,128)S(1)}, f32[64,1024]{0,1:T(8,128)S(1)}, u32[]{:S(2)}, u32[]{:S(2)}) %collective-permute-start.21) | collective-permute-done | bytes 262176 | tf_op jit(solution)/shard_map/ppermute | solution.py:120
  109.4 0.9 constant_dynamic-update-slice_fusion.6
  110.2 1.9 %constant_dynamic-update-slice_fusion.5 = f32[64,8192]{0,1:T(8,128)} fusion(f32[64,8192]{0,1:T(8,128)} %constant_dynamic-update-slice_fusion.6, f32[64,1024]{0,1:T(8,128)} %collective-permute-done.20, s32[]{:T(128)S(6)} %select_n.191), kind=kLoop, calls=%fused_computation.22 | loop fusion | bytes 1048580 | tf_op jit(solution)/shard_map/dynamic_update_slice | solution.py:124
  112.1 3.2 %collective-permute-start.24 = (f32[64,1024]{0,1:T(8,128)S(1)}, f32[64,1024]{0,1:T(8,128)S(1)}, u32[]{:S(2)}, u32[]{:S(2)}) collective-permute-start(f32[64,1024]{0,1:T(8,128)S(1)} %collective-permute-done.22), channel_id=1, source_target_pairs={{0,28},{4,0},{8,4},{12,8},{16,12},{20,16},{24,20},{28,24},{1,29},{... | collective-permute-start | bytes 786440 | tf_op jit(solution)/shard_map/ppermute | solution.py:123
  115.3 0.8 constant_dynamic-update-slice_fusion.4
  116.1 5.6 %collective-permute-done.23 = f32[64,1024]{0,1:T(8,128)S(1)} collective-permute-done((f32[64,1024]{0,1:T(8,128)S(1)}, f32[64,1024]{0,1:T(8,128)S(1)}, u32[]{:S(2)}, u32[]{:S(2)}) %collective-permute-start.23) | collective-permute-done | bytes 262176 | tf_op jit(solution)/shard_map/ppermute | solution.py:120
  123.4 0.8 constant_dynamic-update-slice_fusion.1
  124.2 7.9 %collective-permute-done.25 = f32[64,1024]{0,1:T(8,128)S(1)} collective-permute-done((f32[64,1024]{0,1:T(8,128)S(1)}, f32[64,1024]{0,1:T(8,128)S(1)}, u32[]{:S(2)}, u32[]{:S(2)}) %collective-permute-start.25) | collective-permute-done | bytes 262176 | tf_op jit(solution)/shard_map/ppermute | solution.py:120
  132.1 0.8 constant_dynamic-update-slice_fusion
  132.9 2.8 %gather_fusion.1 = f32[64,64]{1,0:T(8,128)S(1)} fusion(f32[64,8192]{0,1:T(8,128)} %constant_dynamic-update-slice_fusion, s32[1024]{0:T(1024)S(1)} %pad_clamp_fusion), kind=kCustom, calls=%fused_computation.1.clone | custom fusion | bytes 33024 | tf_op jit(solution)/shard_map/jit(_take)/gather | solution.py:169
  137.2 8.6 %shard_map.68 = (f32[64,64]{1,0:T(8,128)}, f32[1,64]{1,0:T(1,128)}) custom-call(f32[64,64]{1,0:T(8,128)} %copy.12.m_ref, f32[64,64]{1,0:T(8,128)} %broadcast_select_fusion.mt_ref, f32[1,64]{1,0:T(1,128)} %convert_bitcast_fusion.acc_ref), custom_call_target="tpu_custom_call" | custom-call | tf_op jit(solution)/shard_map/pallas_call | solution.py:76
  145.8 1.1 fusion
  146.9 8.1 %convolution_subtract_fusion = f32[64,8192]{1,0:T(8,128)} fusion(f32[64,8192]{1,0:T(8,128)S(1)} %copy-done.1, f32[64,64]{1,0:T(8,128)S(1)} %fusion, f32[64,8192]{0,1:T(8,128)} %constant_dynamic-update-slice_fusion), kind=kOutput, calls=%fused_computation.2 | convolution fusion | flops 403177472 | bytes 6307840 | tf_op jit(solution)/shard_map/dot_general | solution.py:172
  (63 shorter events, 8.8 us)
Async XLA Ops:
  0.6 1.0 copy-start
  5.4 10.6 %copy-start.2 = (f32[64,8192]{1,0:T(8,128)}, f32[64,8192]{1,0:T(8,128)S(1)}, u32[]{:S(2)}) copy-start(f32[64,8192]{1,0:T(8,128)S(1)} %fusion.7) | copy-start | bytes 6291460
  5.5 53.9 %copy-start.3 = (s32[64]{0:T(128)S(1)}, s32[64]{0:T(128)}, u32[]{:S(2)}) copy-start(s32[64]{0:T(128)} %param.10) | copy-start | bytes 772
  5.5 10.5 %collective-permute-start = (f32[64,1024]{1,0:T(8,128)S(1)}, f32[64,1024]{1,0:T(8,128)S(1)}, u32[]{:S(2)}, u32[]{:S(2)}) collective-permute-start(f32[64,1024]{1,0:T(8,128)S(1)} %constant_dynamic-slice_fusion.7), channel_id=1, source_target_pairs={{0,4},{4,8},{8,12},{12,16},{16,20},{20,24},{24,28},{28,0},{1,5},{5... | collective-permute-start | bytes 786440 | tf_op jit(solution)/shard_map/ppermute | solution.py:98
  16.1 69.2 %copy-start.1 = (f32[64,8192]{1,0:T(8,128)S(1)}, f32[64,8192]{1,0:T(8,128)}, u32[]{:S(2)}) copy-start(f32[64,8192]{1,0:T(8,128)} %param.7) | copy-start | bytes 6291460
  16.1 8.8 %collective-permute-start.1 = (f32[64,1024]{1,0:T(8,128)S(1)}, f32[64,1024]{1,0:T(8,128)S(1)}, u32[]{:S(2)}, u32[]{:S(2)}) collective-permute-start(f32[64,1024]{1,0:T(8,128)S(1)} %get-tuple-element.11), channel_id=1, source_target_pairs={{0,4},{4,8},{8,12},{12,16},{16,20},{20,24},{24,28},{28,0},{1,5},{5... | collective-permute-start | bytes 786440 | tf_op jit(solution)/shard_map/ppermute | solution.py:98
  16.2 8.7 %collective-permute-start.4 = (f32[64,1024]{1,0:T(8,128)S(1)}, f32[64,1024]{1,0:T(8,128)S(1)}, u32[]{:S(2)}, u32[]{:S(2)}) collective-permute-start(f32[64,1024]{1,0:T(8,128)S(1)} %get-tuple-element.12), channel_id=1, source_target_pairs={{0,28},{4,0},{8,4},{12,8},{16,12},{20,16},{24,20},{28,24},{1,29},{... | collective-permute-start | bytes 786440 | tf_op jit(solution)/shard_map/ppermute | solution.py:100
  26.6 8.0 %collective-permute-start.2 = (f32[64,1024]{1,0:T(8,128)}, f32[64,1024]{1,0:T(8,128)S(1)}, u32[]{:S(2)}, u32[]{:S(2)}) collective-permute-start(f32[64,1024]{1,0:T(8,128)} %get-tuple-element.9), channel_id=1, source_target_pairs={{0,4},{4,8},{8,12},{12,16},{16,20},{20,24},{24,28},{28,0},{1,5},{5... | collective-permute-start | bytes 786440 | tf_op jit(solution)/shard_map/ppermute | solution.py:98
  26.6 8.0 %collective-permute-start.5 = (f32[64,1024]{1,0:T(8,128)S(1)}, f32[64,1024]{1,0:T(8,128)S(1)}, u32[]{:S(2)}, u32[]{:S(2)}) collective-permute-start(f32[64,1024]{1,0:T(8,128)S(1)} %get-tuple-element.10), channel_id=1, source_target_pairs={{0,28},{4,0},{8,4},{12,8},{16,12},{20,16},{24,20},{28,24},{1,29},{... | collective-permute-start | bytes 786440 | tf_op jit(solution)/shard_map/ppermute | solution.py:100
  35.8 7.7 %collective-permute-start.3 = (f32[64,1024]{1,0:T(8,128)S(1)}, f32[64,1024]{1,0:T(8,128)S(1)}, u32[]{:S(2)}, u32[]{:S(2)}) collective-permute-start(f32[64,1024]{1,0:T(8,128)S(1)} %get-tuple-element.7), channel_id=1, source_target_pairs={{0,4},{4,8},{8,12},{12,16},{16,20},{20,24},{24,28},{28,0},{1,5},{5... | collective-permute-start | bytes 786440 | tf_op jit(solution)/shard_map/ppermute | solution.py:98
  37.6 6.4 %collective-permute-start.6 = (f32[64,1024]{1,0:T(8,128)S(1)}, f32[64,1024]{1,0:T(8,128)S(1)}, u32[]{:S(2)}, u32[]{:S(2)}) collective-permute-start(f32[64,1024]{1,0:T(8,128)S(1)} %get-tuple-element.8), channel_id=1, source_target_pairs={{0,28},{4,0},{8,4},{12,8},{16,12},{20,16},{24,20},{28,24},{1,29},{... | collective-permute-start | bytes 786440 | tf_op jit(solution)/shard_map/ppermute | solution.py:100
  45.0 5.6 %collective-permute-start.7 = (f32[64,256]{1,0:T(8,128)S(1)}, f32[64,256]{1,0:T(8,128)S(1)}, u32[]{:S(2)}, u32[]{:S(2)}) collective-permute-start(f32[64,256]{1,0:T(8,128)S(1)} %get-tuple-element.13), channel_id=1, source_target_pairs={{0,1},{1,2},{2,3},{3,0},{4,5},{5,6},{6,7},{7,4},{8,9},{9,10},{10,1... | collective-permute-start | bytes 196616 | tf_op jit(solution)/shard_map/ppermute | solution.py:133
  46.6 4.3 %collective-permute-start.8 = (f32[64,256]{1,0:T(8,128)S(1)}, f32[64,256]{1,0:T(8,128)S(1)}, u32[]{:S(2)}, u32[]{:S(2)}) collective-permute-start(f32[64,256]{1,0:T(8,128)S(1)} %get-tuple-element.15), channel_id=1, source_target_pairs={{0,3},{1,0},{2,1},{3,2},{4,7},{5,4},{6,5},{7,6},{8,11},{9,8},{10,9... | collective-permute-start | bytes 196616 | tf_op jit(solution)/shard_map/ppermute | solution.py:133
  48.3 5.8 %collective-permute-start.9 = (f32[64,256]{1,0:T(8,128)S(1)}, f32[64,256]{1,0:T(8,128)S(1)}, u32[]{:S(2)}, u32[]{:S(2)}) collective-permute-start(f32[64,256]{1,0:T(8,128)S(1)} %get-tuple-element.14), channel_id=1, source_target_pairs={{0,2},{1,3},{2,0},{3,1},{4,6},{5,7},{6,4},{7,5},{8,10},{9,11},{10,... | collective-permute-start | bytes 196616 | tf_op jit(solution)/shard_map/ppermute | solution.py:133
  54.2 5.2 %collective-permute-start.10 = (f32[64,64]{1,0:T(8,128)S(1)}, f32[64,64]{1,0:T(8,128)S(1)}, u32[]{:S(2)}, u32[]{:S(2)}) collective-permute-start(f32[64,64]{1,0:T(8,128)S(1)} %get-tuple-element.16), channel_id=1, source_target_pairs={{0,32},{32,64},{64,96},{96,0},{1,33},{33,65},{65,97},{97,1},{2,34}... | collective-permute-start | bytes 49160 | tf_op jit(solution)/shard_map/ppermute | solution.py:133
  55.8 3.9 %collective-permute-start.11 = (f32[64,64]{1,0:T(8,128)S(1)}, f32[64,64]{1,0:T(8,128)S(1)}, u32[]{:S(2)}, u32[]{:S(2)}) collective-permute-start(f32[64,64]{1,0:T(8,128)S(1)} %get-tuple-element.18), channel_id=1, source_target_pairs={{0,96},{32,0},{64,32},{96,64},{1,97},{33,1},{65,33},{97,65},{2,98}... | collective-permute-start | bytes 49160 | tf_op jit(solution)/shard_map/ppermute | solution.py:133
  57.5 5.7 %collective-permute-start.12 = (f32[64,64]{1,0:T(8,128)S(1)}, f32[64,64]{1,0:T(8,128)S(1)}, u32[]{:S(2)}, u32[]{:S(2)}) collective-permute-start(f32[64,64]{1,0:T(8,128)S(1)} %get-tuple-element.17), channel_id=1, source_target_pairs={{0,64},{32,96},{64,0},{96,32},{1,65},{33,97},{65,1},{97,33},{2,66}... | collective-permute-start | bytes 49160 | tf_op jit(solution)/shard_map/ppermute | solution.py:133
  63.4 5.2 %collective-permute-start.13 = (f32[64,64]{1,0:T(8,128)S(1)}, f32[64,64]{1,0:T(8,128)S(1)}, u32[]{:S(2)}, u32[]{:S(2)}) collective-permute-start(f32[64,64]{1,0:T(8,128)S(1)} %add_add_fusion.2), channel_id=1, source_target_pairs={{0,32},{32,64},{64,96},{96,0},{1,33},{33,65},{65,97},{97,1},{2,34}... | collective-permute-start | bytes 49160 | tf_op jit(solution)/shard_map/ppermute | solution.py:143
  63.5 5.2 %collective-permute-start.14 = (f32[64,64]{1,0:T(8,128)S(1)}, f32[64,64]{1,0:T(8,128)S(1)}, u32[]{:S(2)}, u32[]{:S(2)}) collective-permute-start(f32[64,64]{1,0:T(8,128)S(1)} %add_add_fusion.2), channel_id=1, source_target_pairs={{0,96},{32,0},{64,32},{96,64},{1,97},{33,1},{65,33},{97,65},{2,98}... | collective-permute-start | bytes 49160 | tf_op jit(solution)/shard_map/ppermute | solution.py:143
  66.7 5.4 %collective-permute-start.15 = (f32[64,64]{1,0:T(8,128)S(1)}, f32[64,64]{1,0:T(8,128)S(1)}, u32[]{:S(2)}, u32[]{:S(2)}) collective-permute-start(f32[64,64]{1,0:T(8,128)S(1)} %add_add_fusion.2), channel_id=1, source_target_pairs={{0,64},{32,96},{64,0},{96,32},{1,65},{33,97},{65,1},{97,33},{2,66}... | collective-permute-start | bytes 49160 | tf_op jit(solution)/shard_map/ppermute | solution.py:143
  68.7 27.4 %copy-start.4 = (s32[64]{0:T(128)S(1)}, s32[64]{0:T(128)}, u32[]{:S(2)}) copy-start(s32[64]{0:T(128)} %param.11) | copy-start | bytes 772
  72.2 6.3 %collective-permute-start.16 = (f32[64,256]{0,1:T(8,128)S(1)}, f32[64,256]{0,1:T(8,128)S(1)}, u32[]{:S(2)}, u32[]{:S(2)}) collective-permute-start(f32[64,256]{0,1:T(8,128)S(1)} %constant_dynamic-update-slice_fusion.12), channel_id=1, source_target_pairs={{0,1},{1,2},{2,3},{3,0},{4,5},{5,6},{6,7},{7,4},{8,9},{9,10},{10,1... | collective-permute-start | bytes 196616 | tf_op jit(solution)/shard_map/ppermute | solution.py:143
  72.5 6.9 %collective-permute-start.17 = (f32[64,256]{0,1:T(8,128)S(1)}, f32[64,256]{0,1:T(8,128)S(1)}, u32[]{:S(2)}, u32[]{:S(2)}) collective-permute-start(f32[64,256]{0,1:T(8,128)S(1)} %constant_dynamic-update-slice_fusion.12), channel_id=1, source_target_pairs={{0,3},{1,0},{2,1},{3,2},{4,7},{5,4},{6,5},{7,6},{8,11},{9,8},{10,9... | collective-permute-start | bytes 196616 | tf_op jit(solution)/shard_map/ppermute | solution.py:143
  75.5 6.5 %collective-permute-start.18 = (f32[64,256]{0,1:T(8,128)S(1)}, f32[64,256]{0,1:T(8,128)S(1)}, u32[]{:S(2)}, u32[]{:S(2)}) collective-permute-start(f32[64,256]{0,1:T(8,128)S(1)} %constant_dynamic-update-slice_fusion.12), channel_id=1, source_target_pairs={{0,2},{1,3},{2,0},{3,1},{4,6},{5,7},{6,4},{7,5},{8,10},{9,11},{10,... | collective-permute-start | bytes 196616 | tf_op jit(solution)/shard_map/ppermute | solution.py:143
  82.0 14.1 %collective-permute-start.19 = (f32[64,1024]{0,1:T(8,128)S(1)}, f32[64,1024]{0,1:T(8,128)S(1)}, u32[]{:S(2)}, u32[]{:S(2)}) collective-permute-start(f32[64,1024]{0,1:T(8,128)S(1)} %constant_dynamic-update-slice_fusion.8), channel_id=1, source_target_pairs={{0,4},{4,8},{8,12},{12,16},{16,20},{20,24},{24,28},{28,0},{1,5},{5... | collective-permute-start | bytes 786440 | tf_op jit(solution)/shard_map/ppermute | solution.py:120
  83.8 12.9 %collective-permute-start.20 = (f32[64,1024]{0,1:T(8,128)S(1)}, f32[64,1024]{0,1:T(8,128)}, u32[]{:S(2)}, u32[]{:S(2)}) collective-permute-start(f32[64,1024]{0,1:T(8,128)S(1)} %constant_dynamic-update-slice_fusion.8), channel_id=1, source_target_pairs={{0,28},{4,0},{8,4},{12,8},{16,12},{20,16},{24,20},{28,24},{1,29},{... | collective-permute-start | bytes 786440 | tf_op jit(solution)/shard_map/ppermute | solution.py:123
  96.1 13.2 %collective-permute-start.21 = (f32[64,1024]{0,1:T(8,128)S(1)}, f32[64,1024]{0,1:T(8,128)S(1)}, u32[]{:S(2)}, u32[]{:S(2)}) collective-permute-start(f32[64,1024]{0,1:T(8,128)S(1)} %collective-permute-done.19), channel_id=1, source_target_pairs={{0,4},{4,8},{8,12},{12,16},{16,20},{20,24},{24,28},{28,0},{1,5},{5... | collective-permute-start | bytes 786440 | tf_op jit(solution)/shard_map/ppermute | solution.py:120
  96.7 15.4 %collective-permute-start.22 = (f32[64,1024]{0,1:T(8,128)}, f32[64,1024]{0,1:T(8,128)S(1)}, u32[]{:S(2)}, u32[]{:S(2)}) collective-permute-start(f32[64,1024]{0,1:T(8,128)} %collective-permute-done.20), channel_id=1, source_target_pairs={{0,28},{4,0},{8,4},{12,8},{16,12},{20,16},{24,20},{28,24},{1,29},{... | collective-permute-start | bytes 786440 | tf_op jit(solution)/shard_map/ppermute | solution.py:123
  109.4 12.4 %collective-permute-start.23 = (f32[64,1024]{0,1:T(8,128)S(1)}, f32[64,1024]{0,1:T(8,128)S(1)}, u32[]{:S(2)}, u32[]{:S(2)}) collective-permute-start(f32[64,1024]{0,1:T(8,128)S(1)} %collective-permute-done.21), channel_id=1, source_target_pairs={{0,4},{4,8},{8,12},{12,16},{16,20},{20,24},{24,28},{28,0},{1,5},{5... | collective-permute-start | bytes 786440 | tf_op jit(solution)/shard_map/ppermute | solution.py:120
  112.1 11.3 %collective-permute-start.24 = (f32[64,1024]{0,1:T(8,128)S(1)}, f32[64,1024]{0,1:T(8,128)S(1)}, u32[]{:S(2)}, u32[]{:S(2)}) collective-permute-start(f32[64,1024]{0,1:T(8,128)S(1)} %collective-permute-done.22), channel_id=1, source_target_pairs={{0,28},{4,0},{8,4},{12,8},{16,12},{20,16},{24,20},{28,24},{1,29},{... | collective-permute-start | bytes 786440 | tf_op jit(solution)/shard_map/ppermute | solution.py:123
  121.7 10.4 %collective-permute-start.25 = (f32[64,1024]{0,1:T(8,128)S(1)}, f32[64,1024]{0,1:T(8,128)S(1)}, u32[]{:S(2)}, u32[]{:S(2)}) collective-permute-start(f32[64,1024]{0,1:T(8,128)S(1)} %collective-permute-done.23), channel_id=1, source_target_pairs={{0,4},{4,8},{8,12},{12,16},{16,20},{20,24},{24,28},{28,0},{1,5},{5... | collective-permute-start | bytes 786440 | tf_op jit(solution)/shard_map/ppermute | solution.py:120

commit v3 on v2

--- a/solution.py
+++ b/solution.py
@@ -166,7 +166,9 @@
     picked = jnp.take(inverse_rows, moved, axis=1)
     local_weights = jnp.dot(change, inverse_rows, precision=HI)
     full_weights = ring_allreduce(local_weights, PHASES)
-    intersection = jnp.take(full_weights, moved, axis=1)
+    electrons = full_weights.shape[1]
+    pick = (lax.broadcasted_iota(jnp.int32, (electrons, MOVES), 0) == moved[None, :]).astype(jnp.float32)
+    intersection = jnp.dot(full_weights, pick, precision=HI)
     coupling, ratios = border(intersection, accepted)
     factor = jnp.dot(picked, coupling, precision=HI)
     new_inverse = inverse_rows - jnp.dot(factor, full_weights, precision=HI)

time: 156 us -> 131 us (0.84)
  waiting for transfers between devices: 68.9 us -> 59 us
  local copies, waits for them, and re-layouts: 19.7 us -> 10 us
  other arithmetic: 6.04 us -> 3.23 us
  matrix products: 13 us -> 11.1 us
    ppermute x4, waiting for transfers between devices: 25.2 us -> 17.3 us  [half_ring_ag(): cw = lax.ppermute(cw, axis, shift_perm(n, 1))]
    dynamic_update_slice x3, local copies, waits for them, and re-layouts: 3.53 us -> 0.07 us  [half_ring_ag(): out = lax.dynamic_update_slice_in_dim(out, ccw, (i + s) % n * width, 1)]
    dot_general x1, matrix products: 8.07 us -> 4.8 us  [on_device(): new_inverse = inverse_rows - jnp.dot(factor, full_weights, precision=HI)]
    dynamic_update_slice x4, local copies, waits for them, and re-layouts: 3.33 us -> 0.09 us  [half_ring_ag(): out = lax.dynamic_update_slice_in_dim(out, cw, (i - s) % n * width, 1)]
    gather x1 -> x0, local copies, waits for them, and re-layouts: 2.78 us -> none  [on_device(): intersection = jnp.take(full_weights, moved, axis=1)]
    broadcast_in_dim x1, local copies, waits for them, and re-layouts: 2.23 us -> 0.14 us  [half_ring_ag(): out = jnp.zeros(x.shape[:1] + (n * width,), x.dtype)]
    add x3, other arithmetic: 2.92 us -> 0.88 us  [half_ring_rs(): cw = cw + chunk(i + up - s)]
    ppermute x6, waiting for transfers between devices: 10.7 us -> 8.67 us  [direct_ag(): got = lax.ppermute(x, axis, shift_perm(n, d))]
  transfers between devices with their start and end apart: 26 -> 26, of which waited for: 20 -> 18; matrix products, arithmetic and copies ran while one was open for 10% -> 6% of each run, Pallas kernels for 0% -> 0%
where the time goes in v3:
time: 131 us
  waiting for transfers between devices  59 us (45%)
  starting transfers between devices  38.1 us (29%)
  matrix products  11.1 us (8%)
  local copies, waits for them, and re-layouts  10 us (8%)
  Pallas kernels  8.64 us (7%)
  other arithmetic  3.23 us (2%)
    ppermute x4, waiting for transfers between devices, half_ring_rs(): cw = lax.ppermute(cw, axis, shift_perm(n, 1))  24.8 us
    ppermute x4, waiting for transfers between devices, half_ring_ag(): cw = lax.ppermute(cw, axis, shift_perm(n, 1))  17.3 us
    ppermute x6, starting transfers between devices, direct_rs(): total = total + lax.ppermute(chunk(i + d), axis, shift_perm(n, d))  10.4 us
    ppermute x6, waiting for transfers between devices, direct_ag(): got = lax.ppermute(x, axis, shift_perm(n, d))  8.67 us
    pallas_call x1, Pallas kernels, border(): pl.pallas_call(_border_kernel, out_shape=(jax.ShapeDtypeStruct((n, n), jn...  8.64 us
    ppermute x3, starting transfers between devices, half_ring_rs(): ccw = lax.ppermute(ccw, axis, shift_perm(n, -1))  7.97 us
    ppermute x6, waiting for transfers between devices, direct_rs(): total = total + lax.ppermute(chunk(i + d), axis, shift_perm(n, d))  7.66 us
    ppermute x6, starting transfers between devices, direct_ag(): got = lax.ppermute(x, axis, shift_perm(n, d))  7.59 us
  transfers between devices with their start and end apart: 26, of which 18 were waited for; matrix products, arithmetic and copies ran while one was open for 6% of the time, Pallas kernels for 0%

profile of v3, /device:TPU:0, one launch (start us, length us, event | category | flops | bytes accessed | tf_op | source)
XLA Modules:
  0.0 131.0 jit_solution(10698955304480444471)
XLA Ops:
  0.7 0.7 compare_bitcast_fusion
  2.0 3.5 %fusion.8 = f32[64,8192]{1,0:T(8,128)S(1)} fusion(f32[64,64]{1,0:T(8,128)S(1)} %bitcast.16, f32[64,8192]{1,0:T(8,128)} %param.5), kind=kOutput, calls=%fused_computation.44 | convolution fusion | flops 402653184 | bytes 4210688 | tf_op jit(solution)/shard_map/dot_general | solution.py:167
  5.8 10.2 %collective-permute-done = f32[64,1024]{1,0:T(8,128)S(1)} collective-permute-done((f32[64,1024]{1,0:T(8,128)S(1)}, f32[64,1024]{1,0:T(8,128)S(1)}, u32[]{:S(2)}, u32[]{:S(2)}) %collective-permute-start) | collective-permute-done | bytes 262176 | tf_op jit(solution)/shard_map/ppermute | solution.py:98
  16.2 3.2 %collective-permute-start.4 = (f32[64,1024]{1,0:T(8,128)S(1)}, f32[64,1024]{1,0:T(8,128)S(1)}, u32[]{:S(2)}, u32[]{:S(2)}) collective-permute-start(f32[64,1024]{1,0:T(8,128)S(1)} %get-tuple-element.11), channel_id=1, source_target_pairs={{0,28},{4,0},{8,4},{12,8},{16,12},{20,16},{24,20},{28,24},{1,29},{... | collective-permute-start | bytes 786440 | tf_op jit(solution)/shard_map/ppermute | solution.py:100
  19.4 5.4 %collective-permute-done.1 = f32[64,1024]{1,0:T(8,128)S(1)} collective-permute-done((f32[64,1024]{1,0:T(8,128)S(1)}, f32[64,1024]{1,0:T(8,128)S(1)}, u32[]{:S(2)}, u32[]{:S(2)}) %collective-permute-start.1) | collective-permute-done | bytes 262176 | tf_op jit(solution)/shard_map/ppermute | solution.py:98
  24.8 0.8 dynamic-slice_add_fusion.3
  25.6 3.2 %collective-permute-start.5 = (f32[64,1024]{1,0:T(8,128)S(1)}, f32[64,1024]{1,0:T(8,128)S(1)}, u32[]{:S(2)}, u32[]{:S(2)}) collective-permute-start(f32[64,1024]{1,0:T(8,128)S(1)} %get-tuple-element.9), channel_id=1, source_target_pairs={{0,28},{4,0},{8,4},{12,8},{16,12},{20,16},{24,20},{28,24},{1,29},{... | collective-permute-start | bytes 786440 | tf_op jit(solution)/shard_map/ppermute | solution.py:100
  28.8 4.8 %collective-permute-done.2 = f32[64,1024]{1,0:T(8,128)S(1)} collective-permute-done((f32[64,1024]{1,0:T(8,128)}, f32[64,1024]{1,0:T(8,128)S(1)}, u32[]{:S(2)}, u32[]{:S(2)}) %collective-permute-start.2) | collective-permute-done | bytes 262176 | tf_op jit(solution)/shard_map/ppermute | solution.py:98
  33.7 1.8 %collective-permute-start.3 = (f32[64,1024]{1,0:T(8,128)S(1)}, f32[64,1024]{1,0:T(8,128)S(1)}, u32[]{:S(2)}, u32[]{:S(2)}) collective-permute-start(f32[64,1024]{1,0:T(8,128)S(1)} %get-tuple-element.6), channel_id=1, source_target_pairs={{0,4},{4,8},{8,12},{12,16},{16,20},{20,24},{24,28},{28,0},{1,5},{5... | collective-permute-start | bytes 786440 | tf_op jit(solution)/shard_map/ppermute | solution.py:98
  35.5 1.5 %collective-permute-start.6 = (f32[64,1024]{1,0:T(8,128)S(1)}, f32[64,1024]{1,0:T(8,128)S(1)}, u32[]{:S(2)}, u32[]{:S(2)}) collective-permute-start(f32[64,1024]{1,0:T(8,128)S(1)} %get-tuple-element.7), channel_id=1, source_target_pairs={{0,28},{4,0},{8,4},{12,8},{16,12},{20,16},{24,20},{28,24},{1,29},{... | collective-permute-start | bytes 786440 | tf_op jit(solution)/shard_map/ppermute | solution.py:100
  37.0 4.3 %collective-permute-done.3 = f32[64,1024]{1,0:T(8,128)S(1)} collective-permute-done((f32[64,1024]{1,0:T(8,128)S(1)}, f32[64,1024]{1,0:T(8,128)S(1)}, u32[]{:S(2)}, u32[]{:S(2)}) %collective-permute-start.3) | collective-permute-done | bytes 262176 | tf_op jit(solution)/shard_map/ppermute | solution.py:98
  41.4 0.5 collective-permute-done.6
  41.9 1.0 add_add_fusion
  42.9 1.6 %collective-permute-start.7 = (f32[64,256]{1,0:T(8,128)S(1)}, f32[64,256]{1,0:T(8,128)S(1)}, u32[]{:S(2)}, u32[]{:S(2)}) collective-permute-start(f32[64,256]{1,0:T(8,128)S(1)} %get-tuple-element.12), channel_id=1, source_target_pairs={{0,1},{1,2},{2,3},{3,0},{4,5},{5,6},{6,7},{7,4},{8,9},{9,10},{10,1... | collective-permute-start | bytes 196616 | tf_op jit(solution)/shard_map/ppermute | solution.py:133
  44.6 1.7 %collective-permute-start.8 = (f32[64,256]{1,0:T(8,128)S(1)}, f32[64,256]{1,0:T(8,128)S(1)}, u32[]{:S(2)}, u32[]{:S(2)}) collective-permute-start(f32[64,256]{1,0:T(8,128)S(1)} %get-tuple-element.14), channel_id=1, source_target_pairs={{0,3},{1,0},{2,1},{3,2},{4,7},{5,4},{6,5},{7,6},{8,11},{9,8},{10,9... | collective-permute-start | bytes 196616 | tf_op jit(solution)/shard_map/ppermute | solution.py:133
  46.2 2.0 %collective-permute-start.9 = (f32[64,256]{1,0:T(8,128)S(1)}, f32[64,256]{1,0:T(8,128)S(1)}, u32[]{:S(2)}, u32[]{:S(2)}) collective-permute-start(f32[64,256]{1,0:T(8,128)S(1)} %get-tuple-element.13), channel_id=1, source_target_pairs={{0,2},{1,3},{2,0},{3,1},{4,6},{5,7},{6,4},{7,5},{8,10},{9,11},{10,... | collective-permute-start | bytes 196616 | tf_op jit(solution)/shard_map/ppermute | solution.py:133
  48.8 3.2 %collective-permute-done.9 = f32[64,256]{1,0:T(8,128)S(1)} collective-permute-done((f32[64,256]{1,0:T(8,128)S(1)}, f32[64,256]{1,0:T(8,128)S(1)}, u32[]{:S(2)}, u32[]{:S(2)}) %collective-permute-start.9) | collective-permute-done | bytes 65568 | tf_op jit(solution)/shard_map/ppermute | solution.py:133
  52.1 1.6 %collective-permute-start.10 = (f32[64,64]{1,0:T(8,128)S(1)}, f32[64,64]{1,0:T(8,128)S(1)}, u32[]{:S(2)}, u32[]{:S(2)}) collective-permute-start(f32[64,64]{1,0:T(8,128)S(1)} %get-tuple-element.15), channel_id=1, source_target_pairs={{0,32},{32,64},{64,96},{96,0},{1,33},{33,65},{65,97},{97,1},{2,34}... | collective-permute-start | bytes 49160 | tf_op jit(solution)/shard_map/ppermute | solution.py:133
  53.7 1.7 %collective-permute-start.11 = (f32[64,64]{1,0:T(8,128)S(1)}, f32[64,64]{1,0:T(8,128)S(1)}, u32[]{:S(2)}, u32[]{:S(2)}) collective-permute-start(f32[64,64]{1,0:T(8,128)S(1)} %get-tuple-element.17), channel_id=1, source_target_pairs={{0,96},{32,0},{64,32},{96,64},{1,97},{33,1},{65,33},{97,65},{2,98}... | collective-permute-start | bytes 49160 | tf_op jit(solution)/shard_map/ppermute | solution.py:133
  55.5 1.8 %collective-permute-start.12 = (f32[64,64]{1,0:T(8,128)S(1)}, f32[64,64]{1,0:T(8,128)S(1)}, u32[]{:S(2)}, u32[]{:S(2)}) collective-permute-start(f32[64,64]{1,0:T(8,128)S(1)} %get-tuple-element.16), channel_id=1, source_target_pairs={{0,64},{32,96},{64,0},{96,32},{1,65},{33,97},{65,1},{97,33},{2,66}... | collective-permute-start | bytes 49160 | tf_op jit(solution)/shard_map/ppermute | solution.py:133
  57.6 3.5 %collective-permute-done.12 = f32[64,64]{1,0:T(8,128)S(1)} collective-permute-done((f32[64,64]{1,0:T(8,128)S(1)}, f32[64,64]{1,0:T(8,128)S(1)}, u32[]{:S(2)}, u32[]{:S(2)}) %collective-permute-start.12) | collective-permute-done | bytes 16416 | tf_op jit(solution)/shard_map/ppermute | solution.py:133
  61.3 3.2 %collective-permute-start.14 = (f32[64,64]{1,0:T(8,128)S(1)}, f32[64,64]{1,0:T(8,128)S(1)}, u32[]{:S(2)}, u32[]{:S(2)}) collective-permute-start(f32[64,64]{1,0:T(8,128)S(1)} %add_add_fusion.2), channel_id=1, source_target_pairs={{0,96},{32,0},{64,32},{96,64},{1,97},{33,1},{65,33},{97,65},{2,98}... | collective-permute-start | bytes 49160 | tf_op jit(solution)/shard_map/ppermute | solution.py:143
  64.9 0.4 dynamic_update_slice.48
  65.3 1.1 collective-permute-done.13
  66.8 0.6 dynamic_update_slice.50
  67.4 2.5 %collective-permute-done.15 = f32[64,64]{1,0:T(8,128)S(1)} collective-permute-done((f32[64,64]{1,0:T(8,128)S(1)}, f32[64,64]{1,0:T(8,128)S(1)}, u32[]{:S(2)}, u32[]{:S(2)}) %collective-permute-start.15) | collective-permute-done | bytes 16416 | tf_op jit(solution)/shard_map/ppermute | solution.py:143
  70.5 3.0 %collective-permute-start.17 = (f32[64,256]{1,0:T(8,128)S(1)}, f32[64,256]{1,0:T(8,128)S(1)}, u32[]{:S(2)}, u32[]{:S(2)}) collective-permute-start(f32[64,256]{1,0:T(8,128)S(1)} %dynamic_update_slice.51), channel_id=1, source_target_pairs={{0,3},{1,0},{2,1},{3,2},{4,7},{5,4},{6,5},{7,6},{8,11},{9,8},{10,9... | collective-permute-start | bytes 196616 | tf_op jit(solution)/shard_map/ppermute | solution.py:143
  73.5 0.6 collective-permute-start.18
  74.2 1.6 %collective-permute-done.16 = f32[64,256]{1,0:T(8,128)S(1)} collective-permute-done((f32[64,256]{1,0:T(8,128)S(1)}, f32[64,256]{1,0:T(8,128)S(1)}, u32[]{:S(2)}, u32[]{:S(2)}) %collective-permute-start.16) | collective-permute-done | bytes 65568 | tf_op jit(solution)/shard_map/ppermute | solution.py:143
  75.8 3.5 %collective-permute-done.18 = f32[64,256]{1,0:T(8,128)S(1)} collective-permute-done((f32[64,256]{1,0:T(8,128)S(1)}, f32[64,256]{1,0:T(8,128)S(1)}, u32[]{:S(2)}, u32[]{:S(2)}) %collective-permute-start.18) | collective-permute-done | bytes 65568 | tf_op jit(solution)/shard_map/ppermute | solution.py:143
  79.3 1.8 %collective-permute-start.19 = (f32[64,1024]{1,0:T(8,128)S(1)}, f32[64,1024]{1,0:T(8,128)S(1)}, u32[]{:S(2)}, u32[]{:S(2)}) collective-permute-start(f32[64,1024]{1,0:T(8,128)S(1)} %constant_dynamic-update-slice_fusion.8), channel_id=1, source_target_pairs={{0,4},{4,8},{8,12},{12,16},{16,20},{20,24},{24,28},{28,0},{1,5},{5... | collective-permute-start | bytes 786440 | tf_op jit(solution)/shard_map/ppermute | solution.py:120
  81.1 1.5 %collective-permute-start.20 = (f32[64,1024]{1,0:T(8,128)S(1)}, f32[64,1024]{1,0:T(8,128)S(1)}, u32[]{:S(2)}, u32[]{:S(2)}) collective-permute-start(f32[64,1024]{1,0:T(8,128)S(1)} %constant_dynamic-update-slice_fusion.8), channel_id=1, source_target_pairs={{0,28},{4,0},{8,4},{12,8},{16,12},{20,16},{24,20},{28,24},{1,29},{... | collective-permute-start | bytes 786440 | tf_op jit(solution)/shard_map/ppermute | solution.py:123
  82.6 2.7 %copy.9 = f32[64,8192]{0,1:T(8,128)} copy(f32[64,8192]{1,0:T(8,128)S(1)} %copy-done.1) | data formatting | bytes 4194304 | tf_op args[0]
  85.4 2.8 %gather_fusion = f32[64,64]{1,0:T(8,128)S(1)} fusion(f32[64,8192]{0,1:T(8,128)} %copy.9, s32[1024]{0:T(1024)S(1)} %pad_clamp_fusion), kind=kCustom, calls=%fused_computation | custom fusion | bytes 33024 | tf_op jit(solution)/shard_map/jit(_take)/gather | solution.py:166
  88.2 1.1 collective-permute-start.21
  89.3 0.5 convert_bitcast_fusion.acc_ref
  89.8 2.2 %collective-permute-start.22 = (f32[64,1024]{1,0:T(8,128)S(1)}, f32[64,1024]{1,0:T(8,128)S(1)}, u32[]{:S(2)}, u32[]{:S(2)}) collective-permute-start(f32[64,1024]{1,0:T(8,128)S(1)} %collective-permute-done.20), channel_id=1, source_target_pairs={{0,28},{4,0},{8,4},{12,8},{16,12},{20,16},{24,20},{28,24},{1,29},{... | collective-permute-start | bytes 786440 | tf_op jit(solution)/shard_map/ppermute | solution.py:123
  92.2 5.6 %collective-permute-done.21 = f32[64,1024]{1,0:T(8,128)S(1)} collective-permute-done((f32[64,1024]{1,0:T(8,128)S(1)}, f32[64,1024]{1,0:T(8,128)S(1)}, u32[]{:S(2)}, u32[]{:S(2)}) %collective-permute-start.21) | collective-permute-done | bytes 262176 | tf_op jit(solution)/shard_map/ppermute | solution.py:120
  97.8 0.5 collective-permute-start.23
  98.3 2.9 %collective-permute-start.24 = (f32[64,1024]{1,0:T(8,128)S(1)}, f32[64,1024]{1,0:T(8,128)S(1)}, u32[]{:S(2)}, u32[]{:S(2)}) collective-permute-start(f32[64,1024]{1,0:T(8,128)S(1)} %collective-permute-done.22), channel_id=1, source_target_pairs={{0,28},{4,0},{8,4},{12,8},{16,12},{20,16},{24,20},{28,24},{1,29},{... | collective-permute-start | bytes 786440 | tf_op jit(solution)/shard_map/ppermute | solution.py:123
  101.2 4.2 %collective-permute-done.23 = f32[64,1024]{1,0:T(8,128)S(1)} collective-permute-done((f32[64,1024]{1,0:T(8,128)S(1)}, f32[64,1024]{1,0:T(8,128)S(1)}, u32[]{:S(2)}, u32[]{:S(2)}) %collective-permute-start.23) | collective-permute-done | bytes 262176 | tf_op jit(solution)/shard_map/ppermute | solution.py:120
  105.5 7.5 %collective-permute-done.25 = f32[64,1024]{1,0:T(8,128)S(1)} collective-permute-done((f32[64,1024]{1,0:T(8,128)S(1)}, f32[64,1024]{1,0:T(8,128)S(1)}, u32[]{:S(2)}, u32[]{:S(2)}) %collective-permute-start.25) | collective-permute-done | bytes 262176 | tf_op jit(solution)/shard_map/ppermute | solution.py:120
  113.0 1.4 %copy-done.2 = f32[64,8192]{1,0:T(8,128)} copy-done((f32[64,8192]{1,0:T(8,128)}, f32[64,8192]{1,0:T(8,128)S(1)}, u32[]{:S(2)}) %copy-start.2) | copy-done | bytes 2097176
  114.4 1.4 %fusion.m_ref = f32[64,64]{1,0:T(8,128)S(1)} fusion(f32[64,8192]{1,0:T(8,128)S(1)} %constant_dynamic-update-slice_fusion, s32[64]{0:T(128)S(1)} %copy-done.5), kind=kOutput, calls=%fused_computation.3 | convolution fusion | flops 403177472 | bytes 2113792 | tf_op jit(solution)/shard_map/dot_general | solution.py:171
  115.8 0.7 copy.10
  116.5 8.6 %shard_map.68 = (f32[64,64]{1,0:T(8,128)}, f32[1,64]{1,0:T(1,128)}) custom-call(f32[64,64]{1,0:T(8,128)} %copy-done.4, f32[64,64]{1,0:T(8,128)} %bitcast.17, f32[1,64]{1,0:T(1,128)} %convert_bitcast_fusion.acc_ref), custom_call_target="tpu_custom_call" | custom-call | tf_op jit(solution)/shard_map/pallas_call | solution.py:76
  125.2 1.1 fusion.2
  126.2 4.8 %convolution_subtract_fusion = f32[64,8192]{1,0:T(8,128)} fusion(f32[64,8192]{1,0:T(8,128)S(1)} %copy-done.1, f32[64,64]{1,0:T(8,128)S(1)} %fusion.2, f32[64,8192]{1,0:T(8,128)} %copy-done.2), kind=kOutput, calls=%fused_computation.1 | convolution fusion | flops 403177472 | bytes 6307840 | tf_op jit(solution)/shard_map/dot_general | solution.py:174
  (61 shorter events, 4.1 us)
Async XLA Ops:
  0.6 1.0 copy-start
  5.4 28.2 %copy-start.3 = (f32[64,8192]{1,0:T(8,128)}, f32[64,8192]{1,0:T(8,128)S(1)}, u32[]{:S(2)}) copy-start(f32[64,8192]{1,0:T(8,128)S(1)} %fusion.8) | copy-start | bytes 6291460
  5.5 10.5 %collective-permute-start = (f32[64,1024]{1,0:T(8,128)S(1)}, f32[64,1024]{1,0:T(8,128)S(1)}, u32[]{:S(2)}, u32[]{:S(2)}) collective-permute-start(f32[64,1024]{1,0:T(8,128)S(1)} %constant_dynamic-slice_fusion.7), channel_id=1, source_target_pairs={{0,4},{4,8},{8,12},{12,16},{16,20},{20,24},{24,28},{28,0},{1,5},{5... | collective-permute-start | bytes 786440 | tf_op jit(solution)/shard_map/ppermute | solution.py:98
  16.1 8.8 %collective-permute-start.1 = (f32[64,1024]{1,0:T(8,128)S(1)}, f32[64,1024]{1,0:T(8,128)S(1)}, u32[]{:S(2)}, u32[]{:S(2)}) collective-permute-start(f32[64,1024]{1,0:T(8,128)S(1)} %get-tuple-element.10), channel_id=1, source_target_pairs={{0,4},{4,8},{8,12},{12,16},{16,20},{20,24},{24,28},{28,0},{1,5},{5... | collective-permute-start | bytes 786440 | tf_op jit(solution)/shard_map/ppermute | solution.py:98
  16.2 8.7 %collective-permute-start.4 = (f32[64,1024]{1,0:T(8,128)S(1)}, f32[64,1024]{1,0:T(8,128)S(1)}, u32[]{:S(2)}, u32[]{:S(2)}) collective-permute-start(f32[64,1024]{1,0:T(8,128)S(1)} %get-tuple-element.11), channel_id=1, source_target_pairs={{0,28},{4,0},{8,4},{12,8},{16,12},{20,16},{24,20},{28,24},{1,29},{... | collective-permute-start | bytes 786440 | tf_op jit(solution)/shard_map/ppermute | solution.py:100
  25.6 39.3 %copy-start.5 = (s32[64]{0:T(128)S(1)}, s32[64]{0:T(128)}, u32[]{:S(2)}) copy-start(s32[64]{0:T(128)} %param.8) | copy-start | bytes 772
  25.6 8.0 %collective-permute-start.2 = (f32[64,1024]{1,0:T(8,128)}, f32[64,1024]{1,0:T(8,128)S(1)}, u32[]{:S(2)}, u32[]{:S(2)}) collective-permute-start(f32[64,1024]{1,0:T(8,128)} %get-tuple-element.8), channel_id=1, source_target_pairs={{0,4},{4,8},{8,12},{12,16},{16,20},{20,24},{24,28},{28,0},{1,5},{5... | collective-permute-start | bytes 786440 | tf_op jit(solution)/shard_map/ppermute | solution.py:98
  25.6 8.0 %collective-permute-start.5 = (f32[64,1024]{1,0:T(8,128)S(1)}, f32[64,1024]{1,0:T(8,128)S(1)}, u32[]{:S(2)}, u32[]{:S(2)}) collective-permute-start(f32[64,1024]{1,0:T(8,128)S(1)} %get-tuple-element.9), channel_id=1, source_target_pairs={{0,28},{4,0},{8,4},{12,8},{16,12},{20,16},{24,20},{28,24},{1,29},{... | collective-permute-start | bytes 786440 | tf_op jit(solution)/shard_map/ppermute | solution.py:100
  33.7 48.9 %copy-start.1 = (f32[64,8192]{1,0:T(8,128)S(1)}, f32[64,8192]{1,0:T(8,128)}, u32[]{:S(2)}) copy-start(f32[64,8192]{1,0:T(8,128)} %param.5) | copy-start | bytes 6291460
  33.7 7.7 %collective-permute-start.3 = (f32[64,1024]{1,0:T(8,128)S(1)}, f32[64,1024]{1,0:T(8,128)S(1)}, u32[]{:S(2)}, u32[]{:S(2)}) collective-permute-start(f32[64,1024]{1,0:T(8,128)S(1)} %get-tuple-element.6), channel_id=1, source_target_pairs={{0,4},{4,8},{8,12},{12,16},{16,20},{20,24},{24,28},{28,0},{1,5},{5... | collective-permute-start | bytes 786440 | tf_op jit(solution)/shard_map/ppermute | solution.py:98
  35.5 6.4 %collective-permute-start.6 = (f32[64,1024]{1,0:T(8,128)S(1)}, f32[64,1024]{1,0:T(8,128)S(1)}, u32[]{:S(2)}, u32[]{:S(2)}) collective-permute-start(f32[64,1024]{1,0:T(8,128)S(1)} %get-tuple-element.7), channel_id=1, source_target_pairs={{0,28},{4,0},{8,4},{12,8},{16,12},{20,16},{24,20},{28,24},{1,29},{... | collective-permute-start | bytes 786440 | tf_op jit(solution)/shard_map/ppermute | solution.py:100
  42.9 5.6 %collective-permute-start.7 = (f32[64,256]{1,0:T(8,128)S(1)}, f32[64,256]{1,0:T(8,128)S(1)}, u32[]{:S(2)}, u32[]{:S(2)}) collective-permute-start(f32[64,256]{1,0:T(8,128)S(1)} %get-tuple-element.12), channel_id=1, source_target_pairs={{0,1},{1,2},{2,3},{3,0},{4,5},{5,6},{6,7},{7,4},{8,9},{9,10},{10,1... | collective-permute-start | bytes 196616 | tf_op jit(solution)/shard_map/ppermute | solution.py:133
  44.6 4.3 %collective-permute-start.8 = (f32[64,256]{1,0:T(8,128)S(1)}, f32[64,256]{1,0:T(8,128)S(1)}, u32[]{:S(2)}, u32[]{:S(2)}) collective-permute-start(f32[64,256]{1,0:T(8,128)S(1)} %get-tuple-element.14), channel_id=1, source_target_pairs={{0,3},{1,0},{2,1},{3,2},{4,7},{5,4},{6,5},{7,6},{8,11},{9,8},{10,9... | collective-permute-start | bytes 196616 | tf_op jit(solution)/shard_map/ppermute | solution.py:133
  46.2 5.8 %collective-permute-start.9 = (f32[64,256]{1,0:T(8,128)S(1)}, f32[64,256]{1,0:T(8,128)S(1)}, u32[]{:S(2)}, u32[]{:S(2)}) collective-permute-start(f32[64,256]{1,0:T(8,128)S(1)} %get-tuple-element.13), channel_id=1, source_target_pairs={{0,2},{1,3},{2,0},{3,1},{4,6},{5,7},{6,4},{7,5},{8,10},{9,11},{10,... | collective-permute-start | bytes 196616 | tf_op jit(solution)/shard_map/ppermute | solution.py:133
  52.1 5.2 %collective-permute-start.10 = (f32[64,64]{1,0:T(8,128)S(1)}, f32[64,64]{1,0:T(8,128)S(1)}, u32[]{:S(2)}, u32[]{:S(2)}) collective-permute-start(f32[64,64]{1,0:T(8,128)S(1)} %get-tuple-element.15), channel_id=1, source_target_pairs={{0,32},{32,64},{64,96},{96,0},{1,33},{33,65},{65,97},{97,1},{2,34}... | collective-permute-start | bytes 49160 | tf_op jit(solution)/shard_map/ppermute | solution.py:133
  53.7 3.9 %collective-permute-start.11 = (f32[64,64]{1,0:T(8,128)S(1)}, f32[64,64]{1,0:T(8,128)S(1)}, u32[]{:S(2)}, u32[]{:S(2)}) collective-permute-start(f32[64,64]{1,0:T(8,128)S(1)} %get-tuple-element.17), channel_id=1, source_target_pairs={{0,96},{32,0},{64,32},{96,64},{1,97},{33,1},{65,33},{97,65},{2,98}... | collective-permute-start | bytes 49160 | tf_op jit(solution)/shard_map/ppermute | solution.py:133
  55.5 5.7 %collective-permute-start.12 = (f32[64,64]{1,0:T(8,128)S(1)}, f32[64,64]{1,0:T(8,128)S(1)}, u32[]{:S(2)}, u32[]{:S(2)}) collective-permute-start(f32[64,64]{1,0:T(8,128)S(1)} %get-tuple-element.16), channel_id=1, source_target_pairs={{0,64},{32,96},{64,0},{96,32},{1,65},{33,97},{65,1},{97,33},{2,66}... | collective-permute-start | bytes 49160 | tf_op jit(solution)/shard_map/ppermute | solution.py:133
  61.2 5.2 %collective-permute-start.13 = (f32[64,64]{1,0:T(8,128)S(1)}, f32[64,64]{1,0:T(8,128)S(1)}, u32[]{:S(2)}, u32[]{:S(2)}) collective-permute-start(f32[64,64]{1,0:T(8,128)S(1)} %add_add_fusion.2), channel_id=1, source_target_pairs={{0,32},{32,64},{64,96},{96,0},{1,33},{33,65},{65,97},{97,1},{2,34}... | collective-permute-start | bytes 49160 | tf_op jit(solution)/shard_map/ppermute | solution.py:143
  61.3 5.5 %collective-permute-start.14 = (f32[64,64]{1,0:T(8,128)S(1)}, f32[64,64]{1,0:T(8,128)S(1)}, u32[]{:S(2)}, u32[]{:S(2)}) collective-permute-start(f32[64,64]{1,0:T(8,128)S(1)} %add_add_fusion.2), channel_id=1, source_target_pairs={{0,96},{32,0},{64,32},{96,64},{1,97},{33,1},{65,33},{97,65},{2,98}... | collective-permute-start | bytes 49160 | tf_op jit(solution)/shard_map/ppermute | solution.py:143
  64.5 5.4 %collective-permute-start.15 = (f32[64,64]{1,0:T(8,128)S(1)}, f32[64,64]{1,0:T(8,128)S(1)}, u32[]{:S(2)}, u32[]{:S(2)}) collective-permute-start(f32[64,64]{1,0:T(8,128)S(1)} %add_add_fusion.2), channel_id=1, source_target_pairs={{0,64},{32,96},{64,0},{96,32},{1,65},{33,97},{65,1},{97,33},{2,66}... | collective-permute-start | bytes 49160 | tf_op jit(solution)/shard_map/ppermute | solution.py:143
  70.2 5.6 %collective-permute-start.16 = (f32[64,256]{1,0:T(8,128)S(1)}, f32[64,256]{1,0:T(8,128)S(1)}, u32[]{:S(2)}, u32[]{:S(2)}) collective-permute-start(f32[64,256]{1,0:T(8,128)S(1)} %dynamic_update_slice.51), channel_id=1, source_target_pairs={{0,1},{1,2},{2,3},{3,0},{4,5},{5,6},{6,7},{7,4},{8,9},{9,10},{10,1... | collective-permute-start | bytes 196616 | tf_op jit(solution)/shard_map/ppermute | solution.py:143
  70.5 5.3 %collective-permute-start.17 = (f32[64,256]{1,0:T(8,128)S(1)}, f32[64,256]{1,0:T(8,128)S(1)}, u32[]{:S(2)}, u32[]{:S(2)}) collective-permute-start(f32[64,256]{1,0:T(8,128)S(1)} %dynamic_update_slice.51), channel_id=1, source_target_pairs={{0,3},{1,0},{2,1},{3,2},{4,7},{5,4},{6,5},{7,6},{8,11},{9,8},{10,9... | collective-permute-start | bytes 196616 | tf_op jit(solution)/shard_map/ppermute | solution.py:143
  73.5 5.8 %collective-permute-start.18 = (f32[64,256]{1,0:T(8,128)S(1)}, f32[64,256]{1,0:T(8,128)S(1)}, u32[]{:S(2)}, u32[]{:S(2)}) collective-permute-start(f32[64,256]{1,0:T(8,128)S(1)} %dynamic_update_slice.51), channel_id=1, source_target_pairs={{0,2},{1,3},{2,0},{3,1},{4,6},{5,7},{6,4},{7,5},{8,10},{9,11},{10,... | collective-permute-start | bytes 196616 | tf_op jit(solution)/shard_map/ppermute | solution.py:143
  79.3 8.9 %collective-permute-start.19 = (f32[64,1024]{1,0:T(8,128)S(1)}, f32[64,1024]{1,0:T(8,128)S(1)}, u32[]{:S(2)}, u32[]{:S(2)}) collective-permute-start(f32[64,1024]{1,0:T(8,128)S(1)} %constant_dynamic-update-slice_fusion.8), channel_id=1, source_target_pairs={{0,4},{4,8},{8,12},{12,16},{16,20},{20,24},{24,28},{28,0},{1,5},{5... | collective-permute-start | bytes 786440 | tf_op jit(solution)/shard_map/ppermute | solution.py:120
  81.1 8.7 %collective-permute-start.20 = (f32[64,1024]{1,0:T(8,128)S(1)}, f32[64,1024]{1,0:T(8,128)S(1)}, u32[]{:S(2)}, u32[]{:S(2)}) collective-permute-start(f32[64,1024]{1,0:T(8,128)S(1)} %constant_dynamic-update-slice_fusion.8), channel_id=1, source_target_pairs={{0,28},{4,0},{8,4},{12,8},{16,12},{20,16},{24,20},{28,24},{1,29},{... | collective-permute-start | bytes 786440 | tf_op jit(solution)/shard_map/ppermute | solution.py:123
  82.6 6.6 %copy-start.6 = (s32[64]{0:T(128)S(1)}, s32[64]{0:T(128)}, u32[]{:S(2)}) copy-start(s32[64]{0:T(128)} %param.9) | copy-start | bytes 772
  88.2 9.6 %collective-permute-start.21 = (f32[64,1024]{1,0:T(8,128)S(1)}, f32[64,1024]{1,0:T(8,128)S(1)}, u32[]{:S(2)}, u32[]{:S(2)}) collective-permute-start(f32[64,1024]{1,0:T(8,128)S(1)} %collective-permute-done.19), channel_id=1, source_target_pairs={{0,4},{4,8},{8,12},{12,16},{16,20},{20,24},{24,28},{28,0},{1,5},{5... | collective-permute-start | bytes 786440 | tf_op jit(solution)/shard_map/ppermute | solution.py:120
  89.8 8.5 %collective-permute-start.22 = (f32[64,1024]{1,0:T(8,128)S(1)}, f32[64,1024]{1,0:T(8,128)S(1)}, u32[]{:S(2)}, u32[]{:S(2)}) collective-permute-start(f32[64,1024]{1,0:T(8,128)S(1)} %collective-permute-done.20), channel_id=1, source_target_pairs={{0,28},{4,0},{8,4},{12,8},{16,12},{20,16},{24,20},{28,24},{1,29},{... | collective-permute-start | bytes 786440 | tf_op jit(solution)/shard_map/ppermute | solution.py:123
  97.8 7.6 %collective-permute-start.23 = (f32[64,1024]{1,0:T(8,128)S(1)}, f32[64,1024]{1,0:T(8,128)S(1)}, u32[]{:S(2)}, u32[]{:S(2)}) collective-permute-start(f32[64,1024]{1,0:T(8,128)S(1)} %collective-permute-done.21), channel_id=1, source_target_pairs={{0,4},{4,8},{8,12},{12,16},{16,20},{20,24},{24,28},{28,0},{1,5},{5... | collective-permute-start | bytes 786440 | tf_op jit(solution)/shard_map/ppermute | solution.py:120
  98.3 7.1 %collective-permute-start.24 = (f32[64,1024]{1,0:T(8,128)S(1)}, f32[64,1024]{1,0:T(8,128)S(1)}, u32[]{:S(2)}, u32[]{:S(2)}) collective-permute-start(f32[64,1024]{1,0:T(8,128)S(1)} %collective-permute-done.22), channel_id=1, source_target_pairs={{0,28},{4,0},{8,4},{12,8},{16,12},{20,16},{24,20},{28,24},{1,29},{... | collective-permute-start | bytes 786440 | tf_op jit(solution)/shard_map/ppermute | solution.py:123
  105.4 7.6 %collective-permute-start.25 = (f32[64,1024]{1,0:T(8,128)S(1)}, f32[64,1024]{1,0:T(8,128)S(1)}, u32[]{:S(2)}, u32[]{:S(2)}) collective-permute-start(f32[64,1024]{1,0:T(8,128)S(1)} %collective-permute-done.23), channel_id=1, source_target_pairs={{0,4},{4,8},{8,12},{12,16},{16,20},{20,24},{24,28},{28,0},{1,5},{5... | collective-permute-start | bytes 786440 | tf_op jit(solution)/shard_map/ppermute | solution.py:120
  113.0 1.4 %copy-start.2 = (f32[64,8192]{1,0:T(8,128)}, f32[64,8192]{1,0:T(8,128)S(1)}, u32[]{:S(2)}) copy-start(f32[64,8192]{1,0:T(8,128)S(1)} %constant_dynamic-update-slice_fusion) | copy-start | bytes 6291460
  115.8 0.7 copy-start.4

commit v4 on v2

--- a/solution.py
+++ b/solution.py
@@ -156,6 +156,15 @@
     return x
 
 
+def butterfly_allreduce(x, axes):
+    for axis, n in axes:
+        bit = 1
+        while bit < n:
+            x = x + lax.ppermute(x, axis, [(j, j ^ bit) for j in range(n)])
+            bit *= 2
+    return x
+
+
 def on_device(inverse_rows, row_values, orbital_blocks, moved, accepted):
     row_count = inverse_rows.shape[0]
     block_width = row_values.shape[2]
@@ -166,7 +175,7 @@
     picked = jnp.take(inverse_rows, moved, axis=1)
     local_weights = jnp.dot(change, inverse_rows, precision=HI)
     full_weights = ring_allreduce(local_weights, PHASES)
-    intersection = jnp.take(full_weights, moved, axis=1)
+    intersection = butterfly_allreduce(jnp.dot(change, picked, precision=HI), PHASES)
     coupling, ratios = border(intersection, accepted)
     factor = jnp.dot(picked, coupling, precision=HI)
     new_inverse = inverse_rows - jnp.dot(factor, full_weights, precision=HI)

time: 156 us -> 140 us (0.90)
  local copies, waits for them, and re-layouts: 19.7 us -> 9.58 us
  waiting for transfers between devices: 68.9 us -> 61.1 us
  starting transfers between devices: 37.8 us -> 44.3 us
  matrix products: 13 us -> 8.36 us
    ppermute x0 -> x7, waiting for transfers between devices: none -> 16 us  [butterfly_allreduce(): x = x + lax.ppermute(x, axis, [(j, j ^ bit) for j in range(n)])]
    ppermute x4, waiting for transfers between devices: 25.2 us -> 13 us  [half_ring_ag(): cw = lax.ppermute(cw, axis, shift_perm(n, 1))]
    ppermute x6, waiting for transfers between devices: 7.7 us -> 1.13 us  [direct_rs(): total = total + lax.ppermute(chunk(i + d), axis, shift_perm(n, d))]
    ppermute x0 -> x7, starting transfers between devices: none -> 6.15 us  [butterfly_allreduce(): x = x + lax.ppermute(x, axis, [(j, j ^ bit) for j in range(n)])]
    dot_general x1, matrix products: 8.07 us -> 3.25 us  [on_device(): new_inverse = inverse_rows - jnp.dot(factor, full_weights, precision=HI)]
    ppermute x4, waiting for transfers between devices: 24.8 us -> 21.3 us  [half_ring_rs(): cw = lax.ppermute(cw, axis, shift_perm(n, 1))]
    dynamic_update_slice x3, local copies, waits for them, and re-layouts: 3.53 us -> 0.07 us  [half_ring_ag(): out = lax.dynamic_update_slice_in_dim(out, ccw, (i + s) % n * width, 1)]
    dynamic_update_slice x4, local copies, waits for them, and re-layouts: 3.33 us -> 0.09 us  [half_ring_ag(): out = lax.dynamic_update_slice_in_dim(out, cw, (i - s) % n * width, 1)]
  transfers between devices with their start and end apart: 26 -> 33, of which waited for: 20 -> 19; matrix products, arithmetic and copies ran while one was open for 10% -> 7% of each run, Pallas kernels for 0% -> 6%
where the time goes in v4:
time: 140 us; the launch traced here: 139 us
  waiting for transfers between devices  61.1 us (44%)
  starting transfers between devices  44.3 us (32%)
  local copies, waits for them, and re-layouts  9.58 us (7%)
  Pallas kernels  8.63 us (6%)
  matrix products  8.36 us (6%)
  other arithmetic  5.78 us (4%)
    ppermute x4, waiting for transfers between devices, half_ring_rs(): cw = lax.ppermute(cw, axis, shift_perm(n, 1))  21.3 us
    ppermute x7, waiting for transfers between devices, butterfly_allreduce(): x = x + lax.ppermute(x, axis, [(j, j ^ bit) for j in range(n)])  16 us
    ppermute x4, waiting for transfers between devices, half_ring_ag(): cw = lax.ppermute(cw, axis, shift_perm(n, 1))  13 us
    ppermute x6, starting transfers between devices, direct_rs(): total = total + lax.ppermute(chunk(i + d), axis, shift_perm(n, d))  10.6 us
    ppermute x3, starting transfers between devices, half_ring_rs(): ccw = lax.ppermute(ccw, axis, shift_perm(n, -1))  9.62 us
    pallas_call x1, Pallas kernels, border(): pl.pallas_call(_border_kernel, out_shape=(jax.ShapeDtypeStruct((n, n), jn...  8.63 us
    ppermute x6, waiting for transfers between devices, direct_ag(): got = lax.ppermute(x, axis, shift_perm(n, d))  8.3 us
    ppermute x3, starting transfers between devices, half_ring_ag(): ccw = lax.ppermute(ccw, axis, shift_perm(n, -1))  7.97 us
  transfers between devices with their start and end apart: 33, of which 19 were waited for; matrix products, arithmetic and copies ran while one was open for 7% of the time, Pallas kernels for 6%

profile of v4, /device:TPU:0, one launch (start us, length us, event | category | flops | bytes accessed | tf_op | source)
XLA Modules:
  0.0 138.8 jit_solution(10047098298877387721)
XLA Ops:
  0.7 0.7 compare_bitcast_fusion
  2.0 3.5 %fusion.11 = f32[64,8192]{1,0:T(8,128)S(1)} fusion(f32[64,64]{1,0:T(8,128)S(1)} %bitcast.16, f32[64,8192]{1,0:T(8,128)} %param.5), kind=kOutput, calls=%fused_computation.46 | convolution fusion | flops 402653184 | bytes 4210688 | tf_op jit(solution)/shard_map/dot_general | solution.py:176
  5.8 1.0 copy-done.2
  6.8 9.3 %collective-permute-done.7 = f32[64,1024]{1,0:T(8,128)S(1)} collective-permute-done((f32[64,1024]{1,0:T(8,128)S(1)}, f32[64,1024]{1,0:T(8,128)S(1)}, u32[]{:S(2)}, u32[]{:S(2)}) %collective-permute-start.7) | collective-permute-done | bytes 262176 | tf_op jit(solution)/shard_map/ppermute | solution.py:98
  16.0 1.1 dynamic-slice_add_fusion.4
  17.2 3.2 %collective-permute-start.11 = (f32[64,1024]{1,0:T(8,128)S(1)}, f32[64,1024]{1,0:T(8,128)}, u32[]{:S(2)}, u32[]{:S(2)}) collective-permute-start(f32[64,1024]{1,0:T(8,128)S(1)} %get-tuple-element.11), channel_id=1, source_target_pairs={{0,28},{4,0},{8,4},{12,8},{16,12},{20,16},{24,20},{28,24},{1,29},{... | collective-permute-start | bytes 786440 | tf_op jit(solution)/shard_map/ppermute | solution.py:100
  20.4 5.4 %collective-permute-done.8 = f32[64,1024]{1,0:T(8,128)S(1)} collective-permute-done((f32[64,1024]{1,0:T(8,128)S(1)}, f32[64,1024]{1,0:T(8,128)S(1)}, u32[]{:S(2)}, u32[]{:S(2)}) %collective-permute-start.8) | collective-permute-done | bytes 262176 | tf_op jit(solution)/shard_map/ppermute | solution.py:98
  25.9 1.2 dynamic-slice_add_fusion.3
  27.1 3.2 %collective-permute-start.12 = (f32[64,1024]{1,0:T(8,128)S(1)}, f32[64,1024]{1,0:T(8,128)}, u32[]{:S(2)}, u32[]{:S(2)}) collective-permute-start(f32[64,1024]{1,0:T(8,128)S(1)} %get-tuple-element.9), channel_id=1, source_target_pairs={{0,28},{4,0},{8,4},{12,8},{16,12},{20,16},{24,20},{28,24},{1,29},{... | collective-permute-start | bytes 786440 | tf_op jit(solution)/shard_map/ppermute | solution.py:100
  30.4 4.6 %collective-permute-done.9 = f32[64,1024]{1,0:T(8,128)S(1)} collective-permute-done((f32[64,1024]{1,0:T(8,128)S(1)}, f32[64,1024]{1,0:T(8,128)S(1)}, u32[]{:S(2)}, u32[]{:S(2)}) %collective-permute-start.9) | collective-permute-done | bytes 262176 | tf_op jit(solution)/shard_map/ppermute | solution.py:98
  35.0 1.2 dynamic-slice_add_fusion.2
  36.1 3.2 %collective-permute-start.13 = (f32[64,1024]{1,0:T(8,128)S(1)}, f32[64,1024]{1,0:T(8,128)S(1)}, u32[]{:S(2)}, u32[]{:S(2)}) collective-permute-start(f32[64,1024]{1,0:T(8,128)S(1)} %get-tuple-element.7), channel_id=1, source_target_pairs={{0,28},{4,0},{8,4},{12,8},{16,12},{20,16},{24,20},{28,24},{1,29},{... | collective-permute-start | bytes 786440 | tf_op jit(solution)/shard_map/ppermute | solution.py:100
  39.3 2.7 %copy.7 = f32[64,8192]{0,1:T(8,128)} copy(f32[64,8192]{1,0:T(8,128)S(1)} %copy-done.1) | data formatting | bytes 4194304 | tf_op args[0]
  42.1 2.8 %gather_fusion = f32[64,64]{1,0:T(8,128)S(1)} fusion(f32[64,8192]{0,1:T(8,128)} %copy.7, s32[1024]{0:T(1024)S(1)} %pad_clamp_fusion), kind=kCustom, calls=%fused_computation | custom fusion | bytes 33024 | tf_op jit(solution)/shard_map/jit(_take)/gather | solution.py:175
  44.9 2.0 %collective-permute-done.10 = f32[64,1024]{1,0:T(8,128)S(1)} collective-permute-done((f32[64,1024]{1,0:T(8,128)S(1)}, f32[64,1024]{1,0:T(8,128)S(1)}, u32[]{:S(2)}, u32[]{:S(2)}) %collective-permute-start.10) | collective-permute-done | bytes 262176 | tf_op jit(solution)/shard_map/ppermute | solution.py:98
  46.9 1.0 add_add_fusion
  47.9 3.3 %collective-permute-start.16 = (f32[64,256]{1,0:T(8,128)S(1)}, f32[64,256]{1,0:T(8,128)S(1)}, u32[]{:S(2)}, u32[]{:S(2)}) collective-permute-start(f32[64,256]{1,0:T(8,128)S(1)} %get-tuple-element.13), channel_id=1, source_target_pairs={{0,2},{1,3},{2,0},{3,1},{4,6},{5,7},{6,4},{7,5},{8,10},{9,11},{10,... | collective-permute-start | bytes 196616 | tf_op jit(solution)/shard_map/ppermute | solution.py:133
  51.2 1.1 collective-permute-start.15
  52.3 1.0 collective-permute-start.14
  53.6 3.8 %collective-permute-done = f32[64,64]{0,1:T(8,128)S(1)} collective-permute-done((f32[64,64]{0,1:T(8,128)S(1)}, f32[64,64]{0,1:T(8,128)S(1)}, u32[]{:S(2)}, u32[]{:S(2)}) %collective-permute-start) | collective-permute-done | bytes 16416 | tf_op jit(solution)/shard_map/ppermute | solution.py:163
  57.5 1.1 collective-permute-start.1
  58.8 3.3 %collective-permute-start.19 = (f32[64,64]{1,0:T(8,128)S(1)}, f32[64,64]{1,0:T(8,128)S(1)}, u32[]{:S(2)}, u32[]{:S(2)}) collective-permute-start(f32[64,64]{1,0:T(8,128)S(1)} %get-tuple-element.16), channel_id=1, source_target_pairs={{0,64},{32,96},{64,0},{96,32},{1,65},{33,97},{65,1},{97,33},{2,66}... | collective-permute-start | bytes 49160 | tf_op jit(solution)/shard_map/ppermute | solution.py:133
  62.0 1.1 collective-permute-start.18
  63.2 0.9 collective-permute-start.17
  64.1 3.2 %collective-permute-start.2 = (f32[64,64]{0,1:T(8,128)S(1)}, f32[64,64]{0,1:T(8,128)S(1)}, u32[]{:S(2)}, u32[]{:S(2)}) collective-permute-start(f32[64,64]{0,1:T(8,128)S(1)} %add.279), channel_id=1, source_target_pairs={{0,16},{4,20},{8,24},{12,28},{16,0},{20,4},{24,8},{28,12},{1,17},{... | collective-permute-start | bytes 49160 | tf_op jit(solution)/shard_map/ppermute | solution.py:163
  67.3 1.1 collective-permute-done.17
  68.6 3.2 %collective-permute-start.21 = (f32[64,64]{1,0:T(8,128)S(1)}, f32[64,64]{1,0:T(8,128)S(1)}, u32[]{:S(2)}, u32[]{:S(2)}) collective-permute-start(f32[64,64]{1,0:T(8,128)S(1)} %add_add_fusion.2), channel_id=1, source_target_pairs={{0,96},{32,0},{64,32},{96,64},{1,97},{33,1},{65,33},{97,65},{2,98}... | collective-permute-start | bytes 49160 | tf_op jit(solution)/shard_map/ppermute | solution.py:143
  72.0 0.7 collective-permute-start.3
  74.7 2.5 %collective-permute-done.22 = f32[64,64]{1,0:T(8,128)S(1)} collective-permute-done((f32[64,64]{1,0:T(8,128)S(1)}, f32[64,64]{1,0:T(8,128)S(1)}, u32[]{:S(2)}, u32[]{:S(2)}) %collective-permute-start.22) | collective-permute-done | bytes 16416 | tf_op jit(solution)/shard_map/ppermute | solution.py:143
  77.5 0.8 collective-permute-start.23
  78.2 2.6 %collective-permute-start.24 = (f32[64,256]{1,0:T(8,128)S(1)}, f32[64,256]{1,0:T(8,128)S(1)}, u32[]{:S(2)}, u32[]{:S(2)}) collective-permute-start(f32[64,256]{1,0:T(8,128)S(1)} %dynamic_update_slice.51), channel_id=1, source_target_pairs={{0,3},{1,0},{2,1},{3,2},{4,7},{5,4},{6,5},{7,6},{8,11},{9,8},{10,9... | collective-permute-start | bytes 196616 | tf_op jit(solution)/shard_map/ppermute | solution.py:143
  81.3 1.7 %collective-permute-done.23 = f32[64,256]{1,0:T(8,128)S(1)} collective-permute-done((f32[64,256]{1,0:T(8,128)S(1)}, f32[64,256]{1,0:T(8,128)S(1)}, u32[]{:S(2)}, u32[]{:S(2)}) %collective-permute-start.23) | collective-permute-done | bytes 65568 | tf_op jit(solution)/shard_map/ppermute | solution.py:143
  83.1 3.5 %collective-permute-done.25 = f32[64,256]{1,0:T(8,128)S(1)} collective-permute-done((f32[64,256]{1,0:T(8,128)S(1)}, f32[64,256]{1,0:T(8,128)S(1)}, u32[]{:S(2)}, u32[]{:S(2)}) %collective-permute-start.25) | collective-permute-done | bytes 65568 | tf_op jit(solution)/shard_map/ppermute | solution.py:143
  86.6 2.0 %collective-permute-start.26 = (f32[64,1024]{1,0:T(8,128)S(1)}, f32[64,1024]{1,0:T(8,128)S(1)}, u32[]{:S(2)}, u32[]{:S(2)}) collective-permute-start(f32[64,1024]{1,0:T(8,128)S(1)} %constant_dynamic-update-slice_fusion.8), channel_id=1, source_target_pairs={{0,4},{4,8},{8,12},{12,16},{16,20},{20,24},{24,28},{28,0},{1,5},{5... | collective-permute-start | bytes 786440 | tf_op jit(solution)/shard_map/ppermute | solution.py:120
  89.2 4.9 %collective-permute-done.4 = f32[64,64]{0,1:T(8,128)S(1)} collective-permute-done((f32[64,64]{0,1:T(8,128)S(1)}, f32[64,64]{0,1:T(8,128)S(1)}, u32[]{:S(2)}, u32[]{:S(2)}) %collective-permute-start.4) | collective-permute-done | bytes 16416 | tf_op jit(solution)/shard_map/ppermute | solution.py:163
  94.1 3.9 %collective-permute-done.5 = f32[64,64]{0,1:T(8,128)S(1)} collective-permute-done((f32[64,64]{0,1:T(8,128)S(1)}, f32[64,64]{0,1:T(8,128)S(1)}, u32[]{:S(2)}, u32[]{:S(2)}) %collective-permute-start.5) | collective-permute-done | bytes 16416 | tf_op jit(solution)/shard_map/ppermute | solution.py:163
  98.5 1.3 collective-permute-start.27
  100.3 3.2 %collective-permute-done.6 = f32[64,64]{0,1:T(8,128)S(1)} collective-permute-done((f32[64,64]{0,1:T(8,128)S(1)}, f32[64,64]{0,1:T(8,128)S(1)}, u32[]{:S(2)}, u32[]{:S(2)}) %collective-permute-start.6) | collective-permute-done | bytes 16416 | tf_op jit(solution)/shard_map/ppermute | solution.py:163
  103.5 0.7 copy.10.m_ref
  104.2 8.6 %shard_map.68 = (f32[64,64]{1,0:T(8,128)}, f32[1,64]{1,0:T(1,128)}) custom-call(f32[64,64]{1,0:T(8,128)} %copy.10.m_ref, f32[64,64]{1,0:T(8,128)} %bitcast.18, f32[1,64]{1,0:T(1,128)} %convert_bitcast_fusion.acc_ref), custom_call_target="tpu_custom_call" | custom-call | tf_op jit(solution)/shard_map/pallas_call | solution.py:76
  113.1 1.1 fusion.2
  114.2 3.0 %collective-permute-start.29 = (f32[64,1024]{1,0:T(8,128)S(1)}, f32[64,1024]{1,0:T(8,128)S(1)}, u32[]{:S(2)}, u32[]{:S(2)}) collective-permute-start(f32[64,1024]{1,0:T(8,128)S(1)} %collective-permute-done.27), channel_id=1, source_target_pairs={{0,28},{4,0},{8,4},{12,8},{16,12},{20,16},{24,20},{28,24},{1,29},{... | collective-permute-start | bytes 786440 | tf_op jit(solution)/shard_map/ppermute | solution.py:123
  117.4 3.0 %collective-permute-done.28 = f32[64,1024]{1,0:T(8,128)S(1)} collective-permute-done((f32[64,1024]{1,0:T(8,128)S(1)}, f32[64,1024]{1,0:T(8,128)S(1)}, u32[]{:S(2)}, u32[]{:S(2)}) %collective-permute-start.28) | collective-permute-done | bytes 262176 | tf_op jit(solution)/shard_map/ppermute | solution.py:120
  120.4 0.6 collective-permute-done.29
  121.1 3.7 %collective-permute-start.31 = (f32[64,1024]{1,0:T(8,128)S(1)}, f32[64,1024]{1,0:T(8,128)S(1)}, u32[]{:S(2)}, u32[]{:S(2)}) collective-permute-start(f32[64,1024]{1,0:T(8,128)S(1)} %collective-permute-done.29), channel_id=1, source_target_pairs={{0,28},{4,0},{8,4},{12,8},{16,12},{20,16},{24,20},{28,24},{1,29},{... | collective-permute-start | bytes 786440 | tf_op jit(solution)/shard_map/ppermute | solution.py:123
  124.8 3.2 %collective-permute-done.30 = f32[64,1024]{1,0:T(8,128)S(1)} collective-permute-done((f32[64,1024]{1,0:T(8,128)S(1)}, f32[64,1024]{1,0:T(8,128)S(1)}, u32[]{:S(2)}, u32[]{:S(2)}) %collective-permute-start.30) | collective-permute-done | bytes 262176 | tf_op jit(solution)/shard_map/ppermute | solution.py:120
  128.7 6.9 %collective-permute-done.32 = f32[64,1024]{1,0:T(8,128)S(1)} collective-permute-done((f32[64,1024]{1,0:T(8,128)S(1)}, f32[64,1024]{1,0:T(8,128)S(1)}, u32[]{:S(2)}, u32[]{:S(2)}) %collective-permute-start.32) | collective-permute-done | bytes 262176 | tf_op jit(solution)/shard_map/ppermute | solution.py:120
  135.6 3.2 %convolution_subtract_fusion = f32[64,8192]{1,0:T(8,128)} fusion(f32[64,8192]{1,0:T(8,128)S(1)} %copy-done.1, f32[64,64]{1,0:T(8,128)S(1)} %fusion.2, f32[64,8192]{1,0:T(8,128)S(1)} %constant_dynamic-update-slice_fusion), kind=kOutput, calls=%fused_computation.1 | convolution fusion | flops 403177472 | bytes 6307840 | tf_op jit(solution)/shard_map/dot_general | solution.py:181
  (80 shorter events, 7.6 us)
Async XLA Ops:
  0.6 1.0 copy-start
  5.4 1.3 copy-start.2
  5.5 24.9 %copy-start.4 = (s32[64]{0:T(128)S(1)}, s32[64]{0:T(128)}, u32[]{:S(2)}) copy-start(s32[64]{0:T(128)} %param.8) | copy-start | bytes 772
  5.5 10.5 %collective-permute-start.7 = (f32[64,1024]{1,0:T(8,128)S(1)}, f32[64,1024]{1,0:T(8,128)S(1)}, u32[]{:S(2)}, u32[]{:S(2)}) collective-permute-start(f32[64,1024]{1,0:T(8,128)S(1)} %constant_dynamic-slice_fusion.7), channel_id=1, source_target_pairs={{0,4},{4,8},{8,12},{12,16},{16,20},{20,24},{24,28},{28,0},{1,5},{5... | collective-permute-start | bytes 786440 | tf_op jit(solution)/shard_map/ppermute | solution.py:98
  6.8 32.6 %copy-start.1 = (f32[64,8192]{1,0:T(8,128)S(1)}, f32[64,8192]{1,0:T(8,128)}, u32[]{:S(2)}) copy-start(f32[64,8192]{1,0:T(8,128)} %param.5) | copy-start | bytes 6291460
  17.1 8.8 %collective-permute-start.8 = (f32[64,1024]{1,0:T(8,128)S(1)}, f32[64,1024]{1,0:T(8,128)S(1)}, u32[]{:S(2)}, u32[]{:S(2)}) collective-permute-start(f32[64,1024]{1,0:T(8,128)S(1)} %get-tuple-element.10), channel_id=1, source_target_pairs={{0,4},{4,8},{8,12},{12,16},{16,20},{20,24},{24,28},{28,0},{1,5},{5... | collective-permute-start | bytes 786440 | tf_op jit(solution)/shard_map/ppermute | solution.py:98
  17.2 8.7 %collective-permute-start.11 = (f32[64,1024]{1,0:T(8,128)S(1)}, f32[64,1024]{1,0:T(8,128)}, u32[]{:S(2)}, u32[]{:S(2)}) collective-permute-start(f32[64,1024]{1,0:T(8,128)S(1)} %get-tuple-element.11), channel_id=1, source_target_pairs={{0,28},{4,0},{8,4},{12,8},{16,12},{20,16},{24,20},{28,24},{1,29},{... | collective-permute-start | bytes 786440 | tf_op jit(solution)/shard_map/ppermute | solution.py:100
  27.1 7.9 %collective-permute-start.9 = (f32[64,1024]{1,0:T(8,128)S(1)}, f32[64,1024]{1,0:T(8,128)S(1)}, u32[]{:S(2)}, u32[]{:S(2)}) collective-permute-start(f32[64,1024]{1,0:T(8,128)S(1)} %get-tuple-element.8), channel_id=1, source_target_pairs={{0,4},{4,8},{8,12},{12,16},{16,20},{20,24},{24,28},{28,0},{1,5},{5... | collective-permute-start | bytes 786440 | tf_op jit(solution)/shard_map/ppermute | solution.py:98
  27.1 7.8 %collective-permute-start.12 = (f32[64,1024]{1,0:T(8,128)S(1)}, f32[64,1024]{1,0:T(8,128)}, u32[]{:S(2)}, u32[]{:S(2)}) collective-permute-start(f32[64,1024]{1,0:T(8,128)S(1)} %get-tuple-element.9), channel_id=1, source_target_pairs={{0,28},{4,0},{8,4},{12,8},{16,12},{20,16},{24,20},{28,24},{1,29},{... | collective-permute-start | bytes 786440 | tf_op jit(solution)/shard_map/ppermute | solution.py:100
  36.1 8.8 %collective-permute-start.13 = (f32[64,1024]{1,0:T(8,128)S(1)}, f32[64,1024]{1,0:T(8,128)S(1)}, u32[]{:S(2)}, u32[]{:S(2)}) collective-permute-start(f32[64,1024]{1,0:T(8,128)S(1)} %get-tuple-element.7), channel_id=1, source_target_pairs={{0,28},{4,0},{8,4},{12,8},{16,12},{20,16},{24,20},{28,24},{1,29},{... | collective-permute-start | bytes 786440 | tf_op jit(solution)/shard_map/ppermute | solution.py:100
  39.3 7.6 %collective-permute-start.10 = (f32[64,1024]{1,0:T(8,128)S(1)}, f32[64,1024]{1,0:T(8,128)S(1)}, u32[]{:S(2)}, u32[]{:S(2)}) collective-permute-start(f32[64,1024]{1,0:T(8,128)S(1)} %get-tuple-element.6), channel_id=1, source_target_pairs={{0,4},{4,8},{8,12},{12,16},{16,20},{20,24},{24,28},{28,0},{1,5},{5... | collective-permute-start | bytes 786440 | tf_op jit(solution)/shard_map/ppermute | solution.py:98
  44.9 54.9 %copy-start.5 = (s32[64]{0:T(128)S(1)}, s32[64]{0:T(128)}, u32[]{:S(2)}) copy-start(s32[64]{0:T(128)} %param.9) | copy-start | bytes 772
  47.9 10.7 %collective-permute-start.16 = (f32[64,256]{1,0:T(8,128)S(1)}, f32[64,256]{1,0:T(8,128)S(1)}, u32[]{:S(2)}, u32[]{:S(2)}) collective-permute-start(f32[64,256]{1,0:T(8,128)S(1)} %get-tuple-element.13), channel_id=1, source_target_pairs={{0,2},{1,3},{2,0},{3,1},{4,6},{5,7},{6,4},{7,5},{8,10},{9,11},{10,... | collective-permute-start | bytes 196616 | tf_op jit(solution)/shard_map/ppermute | solution.py:133
  51.2 7.4 %collective-permute-start.15 = (f32[64,256]{1,0:T(8,128)S(1)}, f32[64,256]{1,0:T(8,128)S(1)}, u32[]{:S(2)}, u32[]{:S(2)}) collective-permute-start(f32[64,256]{1,0:T(8,128)S(1)} %get-tuple-element.14), channel_id=1, source_target_pairs={{0,3},{1,0},{2,1},{3,2},{4,7},{5,4},{6,5},{7,6},{8,11},{9,8},{10,9... | collective-permute-start | bytes 196616 | tf_op jit(solution)/shard_map/ppermute | solution.py:133
  52.3 6.4 %collective-permute-start.14 = (f32[64,256]{1,0:T(8,128)S(1)}, f32[64,256]{1,0:T(8,128)S(1)}, u32[]{:S(2)}, u32[]{:S(2)}) collective-permute-start(f32[64,256]{1,0:T(8,128)S(1)} %get-tuple-element.12), channel_id=1, source_target_pairs={{0,1},{1,2},{2,3},{3,0},{4,5},{5,6},{6,7},{7,4},{8,9},{9,10},{10,1... | collective-permute-start | bytes 196616 | tf_op jit(solution)/shard_map/ppermute | solution.py:133
  53.5 4.0 %collective-permute-start = (f32[64,64]{0,1:T(8,128)S(1)}, f32[64,64]{0,1:T(8,128)S(1)}, u32[]{:S(2)}, u32[]{:S(2)}) collective-permute-start(f32[64,64]{0,1:T(8,128)S(1)} %fusion), channel_id=1, source_target_pairs={{0,4},{4,0},{8,12},{12,8},{16,20},{20,16},{24,28},{28,24},{1,5},{5... | collective-permute-start | bytes 49160 | tf_op jit(solution)/shard_map/ppermute | solution.py:163
  57.5 6.6 %collective-permute-start.1 = (f32[64,64]{0,1:T(8,128)S(1)}, f32[64,64]{0,1:T(8,128)S(1)}, u32[]{:S(2)}, u32[]{:S(2)}) collective-permute-start(f32[64,64]{0,1:T(8,128)S(1)} %add.278), channel_id=1, source_target_pairs={{0,8},{4,12},{8,0},{12,4},{16,24},{20,28},{24,16},{28,20},{1,9},{5... | collective-permute-start | bytes 49160 | tf_op jit(solution)/shard_map/ppermute | solution.py:163
  58.8 8.5 %collective-permute-start.19 = (f32[64,64]{1,0:T(8,128)S(1)}, f32[64,64]{1,0:T(8,128)S(1)}, u32[]{:S(2)}, u32[]{:S(2)}) collective-permute-start(f32[64,64]{1,0:T(8,128)S(1)} %get-tuple-element.16), channel_id=1, source_target_pairs={{0,64},{32,96},{64,0},{96,32},{1,65},{33,97},{65,1},{97,33},{2,66}... | collective-permute-start | bytes 49160 | tf_op jit(solution)/shard_map/ppermute | solution.py:133
  62.0 5.2 %collective-permute-start.18 = (f32[64,64]{1,0:T(8,128)S(1)}, f32[64,64]{1,0:T(8,128)S(1)}, u32[]{:S(2)}, u32[]{:S(2)}) collective-permute-start(f32[64,64]{1,0:T(8,128)S(1)} %get-tuple-element.17), channel_id=1, source_target_pairs={{0,96},{32,0},{64,32},{96,64},{1,97},{33,1},{65,33},{97,65},{2,98}... | collective-permute-start | bytes 49160 | tf_op jit(solution)/shard_map/ppermute | solution.py:133
  63.2 5.2 %collective-permute-start.17 = (f32[64,64]{1,0:T(8,128)S(1)}, f32[64,64]{1,0:T(8,128)S(1)}, u32[]{:S(2)}, u32[]{:S(2)}) collective-permute-start(f32[64,64]{1,0:T(8,128)S(1)} %get-tuple-element.15), channel_id=1, source_target_pairs={{0,32},{32,64},{64,96},{96,0},{1,33},{33,65},{65,97},{97,1},{2,34}... | collective-permute-start | bytes 49160 | tf_op jit(solution)/shard_map/ppermute | solution.py:133
  64.1 7.9 %collective-permute-start.2 = (f32[64,64]{0,1:T(8,128)S(1)}, f32[64,64]{0,1:T(8,128)S(1)}, u32[]{:S(2)}, u32[]{:S(2)}) collective-permute-start(f32[64,64]{0,1:T(8,128)S(1)} %add.279), channel_id=1, source_target_pairs={{0,16},{4,20},{8,24},{12,28},{16,0},{20,4},{24,8},{28,12},{1,17},{... | collective-permute-start | bytes 49160 | tf_op jit(solution)/shard_map/ppermute | solution.py:163
  68.5 5.2 %collective-permute-start.20 = (f32[64,64]{1,0:T(8,128)S(1)}, f32[64,64]{1,0:T(8,128)S(1)}, u32[]{:S(2)}, u32[]{:S(2)}) collective-permute-start(f32[64,64]{1,0:T(8,128)S(1)} %add_add_fusion.2), channel_id=1, source_target_pairs={{0,32},{32,64},{64,96},{96,0},{1,33},{33,65},{65,97},{97,1},{2,34}... | collective-permute-start | bytes 49160 | tf_op jit(solution)/shard_map/ppermute | solution.py:143
  68.6 5.5 %collective-permute-start.21 = (f32[64,64]{1,0:T(8,128)S(1)}, f32[64,64]{1,0:T(8,128)S(1)}, u32[]{:S(2)}, u32[]{:S(2)}) collective-permute-start(f32[64,64]{1,0:T(8,128)S(1)} %add_add_fusion.2), channel_id=1, source_target_pairs={{0,96},{32,0},{64,32},{96,64},{1,97},{33,1},{65,33},{97,65},{2,98}... | collective-permute-start | bytes 49160 | tf_op jit(solution)/shard_map/ppermute | solution.py:143
  71.8 5.4 %collective-permute-start.22 = (f32[64,64]{1,0:T(8,128)S(1)}, f32[64,64]{1,0:T(8,128)S(1)}, u32[]{:S(2)}, u32[]{:S(2)}) collective-permute-start(f32[64,64]{1,0:T(8,128)S(1)} %add_add_fusion.2), channel_id=1, source_target_pairs={{0,64},{32,96},{64,0},{96,32},{1,65},{33,97},{65,1},{97,33},{2,66}... | collective-permute-start | bytes 49160 | tf_op jit(solution)/shard_map/ppermute | solution.py:143
  72.0 16.6 %collective-permute-start.3 = (f32[64,64]{0,1:T(8,128)S(1)}, f32[64,64]{0,1:T(8,128)S(1)}, u32[]{:S(2)}, u32[]{:S(2)}) collective-permute-start(f32[64,64]{0,1:T(8,128)S(1)} %add.280), channel_id=1, source_target_pairs={{0,1},{1,0},{2,3},{3,2},{4,5},{5,4},{6,7},{7,6},{8,9},{9,8},{10,11... | collective-permute-start | bytes 49160 | tf_op jit(solution)/shard_map/ppermute | solution.py:163
  77.5 5.6 %collective-permute-start.23 = (f32[64,256]{1,0:T(8,128)S(1)}, f32[64,256]{1,0:T(8,128)S(1)}, u32[]{:S(2)}, u32[]{:S(2)}) collective-permute-start(f32[64,256]{1,0:T(8,128)S(1)} %dynamic_update_slice.51), channel_id=1, source_target_pairs={{0,1},{1,2},{2,3},{3,0},{4,5},{5,6},{6,7},{7,4},{8,9},{9,10},{10,1... | collective-permute-start | bytes 196616 | tf_op jit(solution)/shard_map/ppermute | solution.py:143
  78.2 4.8 %collective-permute-start.24 = (f32[64,256]{1,0:T(8,128)S(1)}, f32[64,256]{1,0:T(8,128)S(1)}, u32[]{:S(2)}, u32[]{:S(2)}) collective-permute-start(f32[64,256]{1,0:T(8,128)S(1)} %dynamic_update_slice.51), channel_id=1, source_target_pairs={{0,3},{1,0},{2,1},{3,2},{4,7},{5,4},{6,5},{7,6},{8,11},{9,8},{10,9... | collective-permute-start | bytes 196616 | tf_op jit(solution)/shard_map/ppermute | solution.py:143
  80.8 5.8 %collective-permute-start.25 = (f32[64,256]{1,0:T(8,128)S(1)}, f32[64,256]{1,0:T(8,128)S(1)}, u32[]{:S(2)}, u32[]{:S(2)}) collective-permute-start(f32[64,256]{1,0:T(8,128)S(1)} %dynamic_update_slice.51), channel_id=1, source_target_pairs={{0,2},{1,3},{2,0},{3,1},{4,6},{5,7},{6,4},{7,5},{8,10},{9,11},{10,... | collective-permute-start | bytes 196616 | tf_op jit(solution)/shard_map/ppermute | solution.py:143
  86.6 26.2 %collective-permute-start.26 = (f32[64,1024]{1,0:T(8,128)S(1)}, f32[64,1024]{1,0:T(8,128)S(1)}, u32[]{:S(2)}, u32[]{:S(2)}) collective-permute-start(f32[64,1024]{1,0:T(8,128)S(1)} %constant_dynamic-update-slice_fusion.8), channel_id=1, source_target_pairs={{0,4},{4,8},{8,12},{12,16},{16,20},{20,24},{24,28},{28,0},{1,5},{5... | collective-permute-start | bytes 786440 | tf_op jit(solution)/shard_map/ppermute | solution.py:120
  88.6 5.5 %collective-permute-start.4 = (f32[64,64]{0,1:T(8,128)S(1)}, f32[64,64]{0,1:T(8,128)S(1)}, u32[]{:S(2)}, u32[]{:S(2)}) collective-permute-start(f32[64,64]{0,1:T(8,128)S(1)} %add.281), channel_id=1, source_target_pairs={{0,2},{1,3},{2,0},{3,1},{4,6},{5,7},{6,4},{7,5},{8,10},{9,11},{10,... | collective-permute-start | bytes 49160 | tf_op jit(solution)/shard_map/ppermute | solution.py:163
  94.1 3.9 %collective-permute-start.5 = (f32[64,64]{0,1:T(8,128)S(1)}, f32[64,64]{0,1:T(8,128)S(1)}, u32[]{:S(2)}, u32[]{:S(2)}) collective-permute-start(f32[64,64]{0,1:T(8,128)S(1)} %add.282), channel_id=1, source_target_pairs={{0,32},{32,0},{64,96},{96,64},{1,33},{33,1},{65,97},{97,65},{2,34}... | collective-permute-start | bytes 49160 | tf_op jit(solution)/shard_map/ppermute | solution.py:163
  98.0 5.4 %collective-permute-start.6 = (f32[64,64]{0,1:T(8,128)S(1)}, f32[64,64]{0,1:T(8,128)S(1)}, u32[]{:S(2)}, u32[]{:S(2)}) collective-permute-start(f32[64,64]{0,1:T(8,128)S(1)} %add.283), channel_id=1, source_target_pairs={{0,64},{32,96},{64,0},{96,32},{1,65},{33,97},{65,1},{97,33},{2,66}... | collective-permute-start | bytes 49160 | tf_op jit(solution)/shard_map/ppermute | solution.py:163
  98.5 15.7 %collective-permute-start.27 = (f32[64,1024]{1,0:T(8,128)S(1)}, f32[64,1024]{1,0:T(8,128)S(1)}, u32[]{:S(2)}, u32[]{:S(2)}) collective-permute-start(f32[64,1024]{1,0:T(8,128)S(1)} %constant_dynamic-update-slice_fusion.8), channel_id=1, source_target_pairs={{0,28},{4,0},{8,4},{12,8},{16,12},{20,16},{24,20},{28,24},{1,29},{... | collective-permute-start | bytes 786440 | tf_op jit(solution)/shard_map/ppermute | solution.py:123
  103.5 0.7 copy-start.3
  112.8 7.6 %collective-permute-start.28 = (f32[64,1024]{1,0:T(8,128)S(1)}, f32[64,1024]{1,0:T(8,128)S(1)}, u32[]{:S(2)}, u32[]{:S(2)}) collective-permute-start(f32[64,1024]{1,0:T(8,128)S(1)} %collective-permute-done.26), channel_id=1, source_target_pairs={{0,4},{4,8},{8,12},{12,16},{16,20},{20,24},{24,28},{28,0},{1,5},{5... | collective-permute-start | bytes 786440 | tf_op jit(solution)/shard_map/ppermute | solution.py:120
  114.2 6.9 %collective-permute-start.29 = (f32[64,1024]{1,0:T(8,128)S(1)}, f32[64,1024]{1,0:T(8,128)S(1)}, u32[]{:S(2)}, u32[]{:S(2)}) collective-permute-start(f32[64,1024]{1,0:T(8,128)S(1)} %collective-permute-done.27), channel_id=1, source_target_pairs={{0,28},{4,0},{8,4},{12,8},{16,12},{20,16},{24,20},{28,24},{1,29},{... | collective-permute-start | bytes 786440 | tf_op jit(solution)/shard_map/ppermute | solution.py:123
  120.4 7.6 %collective-permute-start.30 = (f32[64,1024]{1,0:T(8,128)S(1)}, f32[64,1024]{1,0:T(8,128)S(1)}, u32[]{:S(2)}, u32[]{:S(2)}) collective-permute-start(f32[64,1024]{1,0:T(8,128)S(1)} %collective-permute-done.28), channel_id=1, source_target_pairs={{0,4},{4,8},{8,12},{12,16},{16,20},{20,24},{24,28},{28,0},{1,5},{5... | collective-permute-start | bytes 786440 | tf_op jit(solution)/shard_map/ppermute | solution.py:120
  121.1 7.6 %collective-permute-start.31 = (f32[64,1024]{1,0:T(8,128)S(1)}, f32[64,1024]{1,0:T(8,128)S(1)}, u32[]{:S(2)}, u32[]{:S(2)}) collective-permute-start(f32[64,1024]{1,0:T(8,128)S(1)} %collective-permute-done.29), channel_id=1, source_target_pairs={{0,28},{4,0},{8,4},{12,8},{16,12},{20,16},{24,20},{28,24},{1,29},{... | collective-permute-start | bytes 786440 | tf_op jit(solution)/shard_map/ppermute | solution.py:123
  128.0 7.6 %collective-permute-start.32 = (f32[64,1024]{1,0:T(8,128)S(1)}, f32[64,1024]{1,0:T(8,128)S(1)}, u32[]{:S(2)}, u32[]{:S(2)}) collective-permute-start(f32[64,1024]{1,0:T(8,128)S(1)} %collective-permute-done.30), channel_id=1, source_target_pairs={{0,4},{4,8},{8,12},{12,16},{16,20},{20,24},{24,28},{28,0},{1,5},{5... | collective-permute-start | bytes 786440 | tf_op jit(solution)/shard_map/ppermute | solution.py:120

commit v5 on v3

--- a/solution.py
+++ b/solution.py
@@ -86,18 +86,28 @@
     return [(j, (j + d) % n) for j in range(n)]
 
 
+def mirrored(axis, n):
+    walker = lax.axis_index("walker")
+    i = lax.axis_index(axis)
+    virtual = (i + walker * (n - 2 * i)) % n
+    ahead = [(j, (j + 1) % n) for j in range(n)] + [(n + j, n + (j - 1) % n) for j in range(n)]
+    behind = [(t, f) for f, t in ahead]
+    send = lambda v, pairs: lax.ppermute(v, ("walker", axis), pairs)
+    return virtual, lambda v: send(v, ahead), lambda v: send(v, behind)
+
+
 def half_ring_rs(x, axis, n):
     if n == 1:
         return x
-    i = lax.axis_index(axis)
+    i, forward, backward = mirrored(axis, n)
     width = x.shape[1] // n
     chunk = lambda c: lax.dynamic_slice_in_dim(x, (c % n) * width, width, 1)
     up, down = n // 2, n - 1 - n // 2
     cw, ccw = chunk(i + up), chunk(i - down)
     for s in range(1, up + 1):
-        cw = lax.ppermute(cw, axis, shift_perm(n, 1))
+        cw = forward(cw)
         if s <= down:
-            ccw = lax.ppermute(ccw, axis, shift_perm(n, -1))
+            ccw = backward(ccw)
         if s < up:
             cw = cw + chunk(i + up - s)
         if s < down:
@@ -110,19 +120,20 @@
 def half_ring_ag(x, axis, n):
     if n == 1:
         return x
-    i = lax.axis_index(axis)
+    i, forward, backward = mirrored(axis, n)
     width = x.shape[1]
     up, down = n // 2, n - 1 - n // 2
     out = jnp.zeros(x.shape[:1] + (n * width,), x.dtype)
     out = lax.dynamic_update_slice_in_dim(out, x, i * width, 1)
     cw, ccw = x, x
     for s in range(1, up + 1):
-        cw = lax.ppermute(cw, axis, shift_perm(n, 1))
+        cw = forward(cw)
         out = lax.dynamic_update_slice_in_dim(out, cw, ((i - s) % n) * width, 1)
         if s <= down:
-            ccw = lax.ppermute(ccw, axis, shift_perm(n, -1))
+            ccw = backward(ccw)
             out = lax.dynamic_update_slice_in_dim(out, ccw, ((i + s) % n) * width, 1)
     return out
+
 
 def direct_rs(x, axis, n):
     i = lax.axis_index(axis)

time: 131 us -> 135 us (1.031)
  waiting for transfers between devices: 59 us -> 62.2 us
    ppermute x14, waiting for transfers between devices: 42.6 us -> 46 us  [mirrored(): send = lambda v, pairs: lax.ppermute(v, ('walker', axis), pairs)]
where the time goes in v5:
time: 135 us; the launch traced here: 134 us
  waiting for transfers between devices  62.2 us (46%)
  starting transfers between devices  38.1 us (28%)
  matrix products  11.1 us (8%)
  local copies, waits for them, and re-layouts  9.99 us (7%)
  Pallas kernels  8.64 us (6%)
  other arithmetic  3.23 us (2%)
    ppermute x14, waiting for transfers between devices, mirrored(): send = lambda v, pairs: lax.ppermute(v, ('walker', axis), pairs)  46 us
    ppermute x14, starting transfers between devices, mirrored(): send = lambda v, pairs: lax.ppermute(v, ('walker', axis), pairs)  20 us
    ppermute x6, starting transfers between devices, direct_rs(): total = total + lax.ppermute(chunk(i + d), axis, shift_perm(n, d))  10.4 us
    pallas_call x1, Pallas kernels, border(): pl.pallas_call(_border_kernel, out_shape=(jax.ShapeDtypeStruct((n, n), jn...  8.64 us
    ppermute x6, waiting for transfers between devices, direct_ag(): got = lax.ppermute(x, axis, shift_perm(n, d))  8.6 us
    ppermute x6, starting transfers between devices, direct_ag(): got = lax.ppermute(x, axis, shift_perm(n, d))  7.65 us
    ppermute x6, waiting for transfers between devices, direct_rs(): total = total + lax.ppermute(chunk(i + d), axis, shift_perm(n, d))  7.57 us
    dot_general x1, matrix products, on_device(): new_inverse = inverse_rows - jnp.dot(factor, full_weights, precision=HI)  4.8 us
  transfers between devices with their start and end apart: 26, of which 18 were waited for; matrix products, arithmetic and copies ran while one was open for 6% of the time, Pallas kernels for 0%

profile of v5, /device:TPU:0, one launch (start us, length us, event | category | flops | bytes accessed | tf_op | source)
XLA Modules:
  0.0 134.2 jit_solution(1859261381954469454)
XLA Ops:
  0.7 0.7 compare_bitcast_fusion
  1.6 0.3 fusion.7
  1.9 3.5 %fusion.8 = f32[64,8192]{1,0:T(8,128)S(1)} fusion(f32[64,64]{1,0:T(8,128)S(1)} %bitcast.16, f32[64,8192]{1,0:T(8,128)} %param.5), kind=kOutput, calls=%fused_computation.44 | convolution fusion | flops 402653184 | bytes 4210688 | tf_op jit(solution)/shard_map/dot_general | solution.py:178
  5.8 8.3 %collective-permute-done = f32[64,1024]{1,0:T(8,128)S(1)} collective-permute-done((f32[64,1024]{1,0:T(8,128)S(1)}, f32[64,1024]{1,0:T(8,128)S(1)}, u32[]{:S(2)}, u32[]{:S(2)}) %collective-permute-start) | collective-permute-done | bytes 262176 | tf_op jit(solution)/shard_map/ppermute | solution.py:95
  14.2 3.2 %collective-permute-start.4 = (f32[64,1024]{1,0:T(8,128)S(1)}, f32[64,1024]{1,0:T(8,128)S(1)}, u32[]{:S(2)}, u32[]{:S(2)}) collective-permute-start(f32[64,1024]{1,0:T(8,128)S(1)} %get-tuple-element.11), channel_id=1, source_target_pairs={{4,0},{8,4},{12,8},{16,12},{20,16},{24,20},{28,24},{0,28},{156,128... | collective-permute-start | bytes 786440 | tf_op jit(solution)/shard_map/ppermute | solution.py:95
  17.4 6.5 %collective-permute-done.1 = f32[64,1024]{1,0:T(8,128)S(1)} collective-permute-done((f32[64,1024]{1,0:T(8,128)S(1)}, f32[64,1024]{1,0:T(8,128)S(1)}, u32[]{:S(2)}, u32[]{:S(2)}) %collective-permute-start.1) | collective-permute-done | bytes 262176 | tf_op jit(solution)/shard_map/ppermute | solution.py:95
  23.9 0.8 dynamic-slice_add_fusion.3
  24.7 3.2 %collective-permute-start.5 = (f32[64,1024]{1,0:T(8,128)S(1)}, f32[64,1024]{1,0:T(8,128)S(1)}, u32[]{:S(2)}, u32[]{:S(2)}) collective-permute-start(f32[64,1024]{1,0:T(8,128)S(1)} %get-tuple-element.9), channel_id=1, source_target_pairs={{4,0},{8,4},{12,8},{16,12},{20,16},{24,20},{28,24},{0,28},{156,128... | collective-permute-start | bytes 786440 | tf_op jit(solution)/shard_map/ppermute | solution.py:95
  27.9 6.7 %collective-permute-done.2 = f32[64,1024]{1,0:T(8,128)S(1)} collective-permute-done((f32[64,1024]{1,0:T(8,128)}, f32[64,1024]{1,0:T(8,128)S(1)}, u32[]{:S(2)}, u32[]{:S(2)}) %collective-permute-start.2) | collective-permute-done | bytes 262176 | tf_op jit(solution)/shard_map/ppermute | solution.py:95
  34.8 3.2 %collective-permute-start.6 = (f32[64,1024]{1,0:T(8,128)S(1)}, f32[64,1024]{1,0:T(8,128)S(1)}, u32[]{:S(2)}, u32[]{:S(2)}) collective-permute-start(f32[64,1024]{1,0:T(8,128)S(1)} %get-tuple-element.7), channel_id=1, source_target_pairs={{4,0},{8,4},{12,8},{16,12},{20,16},{24,20},{28,24},{0,28},{156,128... | collective-permute-start | bytes 786440 | tf_op jit(solution)/shard_map/ppermute | solution.py:95
  38.0 5.7 %collective-permute-done.3 = f32[64,1024]{1,0:T(8,128)S(1)} collective-permute-done((f32[64,1024]{1,0:T(8,128)S(1)}, f32[64,1024]{1,0:T(8,128)S(1)}, u32[]{:S(2)}, u32[]{:S(2)}) %collective-permute-start.3) | collective-permute-done | bytes 262176 | tf_op jit(solution)/shard_map/ppermute | solution.py:95
  43.7 1.0 add_add_fusion
  44.7 1.7 %collective-permute-start.7 = (f32[64,256]{1,0:T(8,128)S(1)}, f32[64,256]{1,0:T(8,128)S(1)}, u32[]{:S(2)}, u32[]{:S(2)}) collective-permute-start(f32[64,256]{1,0:T(8,128)S(1)} %get-tuple-element.12), channel_id=1, source_target_pairs={{0,1},{1,2},{2,3},{3,0},{4,5},{5,6},{6,7},{7,4},{8,9},{9,10},{10,1... | collective-permute-start | bytes 196616 | tf_op jit(solution)/shard_map/ppermute | solution.py:144
  46.4 1.7 %collective-permute-start.8 = (f32[64,256]{1,0:T(8,128)S(1)}, f32[64,256]{1,0:T(8,128)S(1)}, u32[]{:S(2)}, u32[]{:S(2)}) collective-permute-start(f32[64,256]{1,0:T(8,128)S(1)} %get-tuple-element.14), channel_id=1, source_target_pairs={{0,3},{1,0},{2,1},{3,2},{4,7},{5,4},{6,5},{7,6},{8,11},{9,8},{10,9... | collective-permute-start | bytes 196616 | tf_op jit(solution)/shard_map/ppermute | solution.py:144
  48.0 2.0 %collective-permute-start.9 = (f32[64,256]{1,0:T(8,128)S(1)}, f32[64,256]{1,0:T(8,128)S(1)}, u32[]{:S(2)}, u32[]{:S(2)}) collective-permute-start(f32[64,256]{1,0:T(8,128)S(1)} %get-tuple-element.13), channel_id=1, source_target_pairs={{0,2},{1,3},{2,0},{3,1},{4,6},{5,7},{6,4},{7,5},{8,10},{9,11},{10,... | collective-permute-start | bytes 196616 | tf_op jit(solution)/shard_map/ppermute | solution.py:144
  50.3 0.5 collective-permute-done.8
  50.7 3.1 %collective-permute-done.9 = f32[64,256]{1,0:T(8,128)S(1)} collective-permute-done((f32[64,256]{1,0:T(8,128)S(1)}, f32[64,256]{1,0:T(8,128)S(1)}, u32[]{:S(2)}, u32[]{:S(2)}) %collective-permute-start.9) | collective-permute-done | bytes 65568 | tf_op jit(solution)/shard_map/ppermute | solution.py:144
  53.9 1.6 %collective-permute-start.10 = (f32[64,64]{1,0:T(8,128)S(1)}, f32[64,64]{1,0:T(8,128)S(1)}, u32[]{:S(2)}, u32[]{:S(2)}) collective-permute-start(f32[64,64]{1,0:T(8,128)S(1)} %get-tuple-element.15), channel_id=1, source_target_pairs={{0,32},{32,64},{64,96},{96,0},{1,33},{33,65},{65,97},{97,1},{2,34}... | collective-permute-start | bytes 49160 | tf_op jit(solution)/shard_map/ppermute | solution.py:144
  55.5 1.7 %collective-permute-start.11 = (f32[64,64]{1,0:T(8,128)S(1)}, f32[64,64]{1,0:T(8,128)S(1)}, u32[]{:S(2)}, u32[]{:S(2)}) collective-permute-start(f32[64,64]{1,0:T(8,128)S(1)} %get-tuple-element.17), channel_id=1, source_target_pairs={{0,96},{32,0},{64,32},{96,64},{1,97},{33,1},{65,33},{97,65},{2,98}... | collective-permute-start | bytes 49160 | tf_op jit(solution)/shard_map/ppermute | solution.py:144
  57.2 1.8 %collective-permute-start.12 = (f32[64,64]{1,0:T(8,128)S(1)}, f32[64,64]{1,0:T(8,128)S(1)}, u32[]{:S(2)}, u32[]{:S(2)}) collective-permute-start(f32[64,64]{1,0:T(8,128)S(1)} %get-tuple-element.16), channel_id=1, source_target_pairs={{0,64},{32,96},{64,0},{96,32},{1,65},{33,97},{65,1},{97,33},{2,66}... | collective-permute-start | bytes 49160 | tf_op jit(solution)/shard_map/ppermute | solution.py:144
  59.4 3.4 %collective-permute-done.12 = f32[64,64]{1,0:T(8,128)S(1)} collective-permute-done((f32[64,64]{1,0:T(8,128)S(1)}, f32[64,64]{1,0:T(8,128)S(1)}, u32[]{:S(2)}, u32[]{:S(2)}) %collective-permute-start.12) | collective-permute-done | bytes 16416 | tf_op jit(solution)/shard_map/ppermute | solution.py:144
  63.2 3.0 %collective-permute-start.14 = (f32[64,64]{1,0:T(8,128)S(1)}, f32[64,64]{1,0:T(8,128)S(1)}, u32[]{:S(2)}, u32[]{:S(2)}) collective-permute-start(f32[64,64]{1,0:T(8,128)S(1)} %add_add_fusion.2), channel_id=1, source_target_pairs={{0,96},{32,0},{64,32},{96,64},{1,97},{33,1},{65,33},{97,65},{2,98}... | collective-permute-start | bytes 49160 | tf_op jit(solution)/shard_map/ppermute | solution.py:154
  66.2 0.4 collective-permute-start.15
  66.7 0.4 dynamic_update_slice.48
  67.1 1.0 collective-permute-done.13
  68.1 0.4 dynamic_update_slice.49
  68.5 0.6 dynamic_update_slice.50
  69.1 2.5 %collective-permute-done.15 = f32[64,64]{1,0:T(8,128)S(1)} collective-permute-done((f32[64,64]{1,0:T(8,128)S(1)}, f32[64,64]{1,0:T(8,128)S(1)}, u32[]{:S(2)}, u32[]{:S(2)}) %collective-permute-start.15) | collective-permute-done | bytes 16416 | tf_op jit(solution)/shard_map/ppermute | solution.py:154
  72.2 3.0 %collective-permute-start.17 = (f32[64,256]{1,0:T(8,128)S(1)}, f32[64,256]{1,0:T(8,128)S(1)}, u32[]{:S(2)}, u32[]{:S(2)}) collective-permute-start(f32[64,256]{1,0:T(8,128)S(1)} %dynamic_update_slice.51), channel_id=1, source_target_pairs={{0,3},{1,0},{2,1},{3,2},{4,7},{5,4},{6,5},{7,6},{8,11},{9,8},{10,9... | collective-permute-start | bytes 196616 | tf_op jit(solution)/shard_map/ppermute | solution.py:154
  75.2 0.6 collective-permute-start.18
  75.9 1.6 %collective-permute-done.16 = f32[64,256]{1,0:T(8,128)S(1)} collective-permute-done((f32[64,256]{1,0:T(8,128)S(1)}, f32[64,256]{1,0:T(8,128)S(1)}, u32[]{:S(2)}, u32[]{:S(2)}) %collective-permute-start.16) | collective-permute-done | bytes 65568 | tf_op jit(solution)/shard_map/ppermute | solution.py:154
  77.5 3.5 %collective-permute-done.18 = f32[64,256]{1,0:T(8,128)S(1)} collective-permute-done((f32[64,256]{1,0:T(8,128)S(1)}, f32[64,256]{1,0:T(8,128)S(1)}, u32[]{:S(2)}, u32[]{:S(2)}) %collective-permute-start.18) | collective-permute-done | bytes 65568 | tf_op jit(solution)/shard_map/ppermute | solution.py:154
  81.1 3.2 %collective-permute-start.20 = (f32[64,1024]{1,0:T(8,128)S(1)}, f32[64,1024]{1,0:T(8,128)S(1)}, u32[]{:S(2)}, u32[]{:S(2)}) collective-permute-start(f32[64,1024]{1,0:T(8,128)S(1)} %constant_dynamic-update-slice_fusion.8), channel_id=1, source_target_pairs={{4,0},{8,4},{12,8},{16,12},{20,16},{24,20},{28,24},{0,28},{156,128... | collective-permute-start | bytes 786440 | tf_op jit(solution)/shard_map/ppermute | solution.py:95
  84.3 2.7 %copy.9 = f32[64,8192]{0,1:T(8,128)} copy(f32[64,8192]{1,0:T(8,128)S(1)} %copy-done.1) | data formatting | bytes 4194304 | tf_op args[0]
  87.1 2.8 %gather_fusion = f32[64,64]{1,0:T(8,128)S(1)} fusion(f32[64,8192]{0,1:T(8,128)} %copy.9, s32[1024]{0:T(1024)S(1)} %pad_clamp_fusion), kind=kCustom, calls=%fused_computation | custom fusion | bytes 33024 | tf_op jit(solution)/shard_map/jit(_take)/gather | solution.py:177
  89.9 1.6 %collective-permute-done.19 = f32[64,1024]{1,0:T(8,128)S(1)} collective-permute-done((f32[64,1024]{1,0:T(8,128)S(1)}, f32[64,1024]{1,0:T(8,128)S(1)}, u32[]{:S(2)}, u32[]{:S(2)}) %collective-permute-start.19) | collective-permute-done | bytes 262176 | tf_op jit(solution)/shard_map/ppermute | solution.py:95
  91.5 0.5 convert_bitcast_fusion.acc_ref
  92.0 3.2 %collective-permute-start.22 = (f32[64,1024]{1,0:T(8,128)S(1)}, f32[64,1024]{1,0:T(8,128)S(1)}, u32[]{:S(2)}, u32[]{:S(2)}) collective-permute-start(f32[64,1024]{1,0:T(8,128)S(1)} %collective-permute-done.20), channel_id=1, source_target_pairs={{4,0},{8,4},{12,8},{16,12},{20,16},{24,20},{28,24},{0,28},{156,128... | collective-permute-start | bytes 786440 | tf_op jit(solution)/shard_map/ppermute | solution.py:95
  95.4 5.6 %collective-permute-done.21 = f32[64,1024]{1,0:T(8,128)S(1)} collective-permute-done((f32[64,1024]{1,0:T(8,128)S(1)}, f32[64,1024]{1,0:T(8,128)S(1)}, u32[]{:S(2)}, u32[]{:S(2)}) %collective-permute-start.21) | collective-permute-done | bytes 262176 | tf_op jit(solution)/shard_map/ppermute | solution.py:95
  101.1 3.3 %collective-permute-start.24 = (f32[64,1024]{1,0:T(8,128)S(1)}, f32[64,1024]{1,0:T(8,128)S(1)}, u32[]{:S(2)}, u32[]{:S(2)}) collective-permute-start(f32[64,1024]{1,0:T(8,128)S(1)} %collective-permute-done.22), channel_id=1, source_target_pairs={{4,0},{8,4},{12,8},{16,12},{20,16},{24,20},{28,24},{0,28},{156,128... | collective-permute-start | bytes 786440 | tf_op jit(solution)/shard_map/ppermute | solution.py:95
  104.4 4.2 %collective-permute-done.23 = f32[64,1024]{1,0:T(8,128)S(1)} collective-permute-done((f32[64,1024]{1,0:T(8,128)S(1)}, f32[64,1024]{1,0:T(8,128)S(1)}, u32[]{:S(2)}, u32[]{:S(2)}) %collective-permute-start.23) | collective-permute-done | bytes 262176 | tf_op jit(solution)/shard_map/ppermute | solution.py:95
  108.7 7.5 %collective-permute-done.25 = f32[64,1024]{1,0:T(8,128)S(1)} collective-permute-done((f32[64,1024]{1,0:T(8,128)S(1)}, f32[64,1024]{1,0:T(8,128)S(1)}, u32[]{:S(2)}, u32[]{:S(2)}) %collective-permute-start.25) | collective-permute-done | bytes 262176 | tf_op jit(solution)/shard_map/ppermute | solution.py:95
  116.2 1.4 %copy-done.2 = f32[64,8192]{1,0:T(8,128)} copy-done((f32[64,8192]{1,0:T(8,128)}, f32[64,8192]{1,0:T(8,128)S(1)}, u32[]{:S(2)}) %copy-start.2) | copy-done | bytes 2097176
  117.6 1.4 %fusion.m_ref = f32[64,64]{1,0:T(8,128)S(1)} fusion(f32[64,8192]{1,0:T(8,128)S(1)} %constant_dynamic-update-slice_fusion, s32[64]{0:T(128)S(1)} %copy-done.5), kind=kOutput, calls=%fused_computation.3 | convolution fusion | flops 403177472 | bytes 2113792 | tf_op jit(solution)/shard_map/dot_general | solution.py:182
  119.0 0.7 copy.10
  119.7 8.6 %shard_map.68 = (f32[64,64]{1,0:T(8,128)}, f32[1,64]{1,0:T(1,128)}) custom-call(f32[64,64]{1,0:T(8,128)} %copy-done.4, f32[64,64]{1,0:T(8,128)} %bitcast.17, f32[1,64]{1,0:T(1,128)} %convert_bitcast_fusion.acc_ref), custom_call_target="tpu_custom_call" | custom-call | tf_op jit(solution)/shard_map/pallas_call | solution.py:76
  128.3 1.1 fusion.2
  129.4 4.8 %convolution_subtract_fusion = f32[64,8192]{1,0:T(8,128)} fusion(f32[64,8192]{1,0:T(8,128)S(1)} %copy-done.1, f32[64,64]{1,0:T(8,128)S(1)} %fusion.2, f32[64,8192]{1,0:T(8,128)} %copy-done.2), kind=kOutput, calls=%fused_computation.1 | convolution fusion | flops 403177472 | bytes 6307840 | tf_op jit(solution)/shard_map/dot_general | solution.py:185
  (61 shorter events, 2.9 us)
Async XLA Ops:
  0.6 1.0 copy-start
  5.4 29.2 %copy-start.3 = (f32[64,8192]{1,0:T(8,128)}, f32[64,8192]{1,0:T(8,128)S(1)}, u32[]{:S(2)}) copy-start(f32[64,8192]{1,0:T(8,128)S(1)} %fusion.8) | copy-start | bytes 6291460
  5.5 8.6 %collective-permute-start = (f32[64,1024]{1,0:T(8,128)S(1)}, f32[64,1024]{1,0:T(8,128)S(1)}, u32[]{:S(2)}, u32[]{:S(2)}) collective-permute-start(f32[64,1024]{1,0:T(8,128)S(1)} %constant_dynamic-slice_fusion.7), channel_id=1, source_target_pairs={{0,4},{4,8},{8,12},{12,16},{16,20},{20,24},{24,28},{28,0},{128,156... | collective-permute-start | bytes 786440 | tf_op jit(solution)/shard_map/ppermute | solution.py:95
  14.1 9.8 %collective-permute-start.1 = (f32[64,1024]{1,0:T(8,128)S(1)}, f32[64,1024]{1,0:T(8,128)S(1)}, u32[]{:S(2)}, u32[]{:S(2)}) collective-permute-start(f32[64,1024]{1,0:T(8,128)S(1)} %get-tuple-element.10), channel_id=1, source_target_pairs={{0,4},{4,8},{8,12},{12,16},{16,20},{20,24},{24,28},{28,0},{128,156... | collective-permute-start | bytes 786440 | tf_op jit(solution)/shard_map/ppermute | solution.py:95
  14.2 9.7 %collective-permute-start.4 = (f32[64,1024]{1,0:T(8,128)S(1)}, f32[64,1024]{1,0:T(8,128)S(1)}, u32[]{:S(2)}, u32[]{:S(2)}) collective-permute-start(f32[64,1024]{1,0:T(8,128)S(1)} %get-tuple-element.11), channel_id=1, source_target_pairs={{4,0},{8,4},{12,8},{16,12},{20,16},{24,20},{28,24},{0,28},{156,128... | collective-permute-start | bytes 786440 | tf_op jit(solution)/shard_map/ppermute | solution.py:95
  24.7 42.0 %copy-start.5 = (s32[64]{0:T(128)S(1)}, s32[64]{0:T(128)}, u32[]{:S(2)}) copy-start(s32[64]{0:T(128)} %param.8) | copy-start | bytes 772
  24.7 9.9 %collective-permute-start.2 = (f32[64,1024]{1,0:T(8,128)}, f32[64,1024]{1,0:T(8,128)S(1)}, u32[]{:S(2)}, u32[]{:S(2)}) collective-permute-start(f32[64,1024]{1,0:T(8,128)} %get-tuple-element.8), channel_id=1, source_target_pairs={{0,4},{4,8},{8,12},{12,16},{16,20},{20,24},{24,28},{28,0},{128,156... | collective-permute-start | bytes 786440 | tf_op jit(solution)/shard_map/ppermute | solution.py:95
  24.7 9.9 %collective-permute-start.5 = (f32[64,1024]{1,0:T(8,128)S(1)}, f32[64,1024]{1,0:T(8,128)S(1)}, u32[]{:S(2)}, u32[]{:S(2)}) collective-permute-start(f32[64,1024]{1,0:T(8,128)S(1)} %get-tuple-element.9), channel_id=1, source_target_pairs={{4,0},{8,4},{12,8},{16,12},{20,16},{24,20},{28,24},{0,28},{156,128... | collective-permute-start | bytes 786440 | tf_op jit(solution)/shard_map/ppermute | solution.py:95
  34.7 49.7 %copy-start.1 = (f32[64,8192]{1,0:T(8,128)S(1)}, f32[64,8192]{1,0:T(8,128)}, u32[]{:S(2)}) copy-start(f32[64,8192]{1,0:T(8,128)} %param.5) | copy-start | bytes 6291460
  34.7 9.0 %collective-permute-start.3 = (f32[64,1024]{1,0:T(8,128)S(1)}, f32[64,1024]{1,0:T(8,128)S(1)}, u32[]{:S(2)}, u32[]{:S(2)}) collective-permute-start(f32[64,1024]{1,0:T(8,128)S(1)} %get-tuple-element.6), channel_id=1, source_target_pairs={{0,4},{4,8},{8,12},{12,16},{16,20},{20,24},{24,28},{28,0},{128,156... | collective-permute-start | bytes 786440 | tf_op jit(solution)/shard_map/ppermute | solution.py:95
  34.8 8.9 %collective-permute-start.6 = (f32[64,1024]{1,0:T(8,128)S(1)}, f32[64,1024]{1,0:T(8,128)S(1)}, u32[]{:S(2)}, u32[]{:S(2)}) collective-permute-start(f32[64,1024]{1,0:T(8,128)S(1)} %get-tuple-element.7), channel_id=1, source_target_pairs={{4,0},{8,4},{12,8},{16,12},{20,16},{24,20},{28,24},{0,28},{156,128... | collective-permute-start | bytes 786440 | tf_op jit(solution)/shard_map/ppermute | solution.py:95
  44.7 5.6 %collective-permute-start.7 = (f32[64,256]{1,0:T(8,128)S(1)}, f32[64,256]{1,0:T(8,128)S(1)}, u32[]{:S(2)}, u32[]{:S(2)}) collective-permute-start(f32[64,256]{1,0:T(8,128)S(1)} %get-tuple-element.12), channel_id=1, source_target_pairs={{0,1},{1,2},{2,3},{3,0},{4,5},{5,6},{6,7},{7,4},{8,9},{9,10},{10,1... | collective-permute-start | bytes 196616 | tf_op jit(solution)/shard_map/ppermute | solution.py:144
  46.4 4.4 %collective-permute-start.8 = (f32[64,256]{1,0:T(8,128)S(1)}, f32[64,256]{1,0:T(8,128)S(1)}, u32[]{:S(2)}, u32[]{:S(2)}) collective-permute-start(f32[64,256]{1,0:T(8,128)S(1)} %get-tuple-element.14), channel_id=1, source_target_pairs={{0,3},{1,0},{2,1},{3,2},{4,7},{5,4},{6,5},{7,6},{8,11},{9,8},{10,9... | collective-permute-start | bytes 196616 | tf_op jit(solution)/shard_map/ppermute | solution.py:144
  48.0 5.8 %collective-permute-start.9 = (f32[64,256]{1,0:T(8,128)S(1)}, f32[64,256]{1,0:T(8,128)S(1)}, u32[]{:S(2)}, u32[]{:S(2)}) collective-permute-start(f32[64,256]{1,0:T(8,128)S(1)} %get-tuple-element.13), channel_id=1, source_target_pairs={{0,2},{1,3},{2,0},{3,1},{4,6},{5,7},{6,4},{7,5},{8,10},{9,11},{10,... | collective-permute-start | bytes 196616 | tf_op jit(solution)/shard_map/ppermute | solution.py:144
  53.9 5.2 %collective-permute-start.10 = (f32[64,64]{1,0:T(8,128)S(1)}, f32[64,64]{1,0:T(8,128)S(1)}, u32[]{:S(2)}, u32[]{:S(2)}) collective-permute-start(f32[64,64]{1,0:T(8,128)S(1)} %get-tuple-element.15), channel_id=1, source_target_pairs={{0,32},{32,64},{64,96},{96,0},{1,33},{33,65},{65,97},{97,1},{2,34}... | collective-permute-start | bytes 49160 | tf_op jit(solution)/shard_map/ppermute | solution.py:144
  55.5 3.9 %collective-permute-start.11 = (f32[64,64]{1,0:T(8,128)S(1)}, f32[64,64]{1,0:T(8,128)S(1)}, u32[]{:S(2)}, u32[]{:S(2)}) collective-permute-start(f32[64,64]{1,0:T(8,128)S(1)} %get-tuple-element.17), channel_id=1, source_target_pairs={{0,96},{32,0},{64,32},{96,64},{1,97},{33,1},{65,33},{97,65},{2,98}... | collective-permute-start | bytes 49160 | tf_op jit(solution)/shard_map/ppermute | solution.py:144
  57.2 5.6 %collective-permute-start.12 = (f32[64,64]{1,0:T(8,128)S(1)}, f32[64,64]{1,0:T(8,128)S(1)}, u32[]{:S(2)}, u32[]{:S(2)}) collective-permute-start(f32[64,64]{1,0:T(8,128)S(1)} %get-tuple-element.16), channel_id=1, source_target_pairs={{0,64},{32,96},{64,0},{96,32},{1,65},{33,97},{65,1},{97,33},{2,66}... | collective-permute-start | bytes 49160 | tf_op jit(solution)/shard_map/ppermute | solution.py:144
  62.9 5.2 %collective-permute-start.13 = (f32[64,64]{1,0:T(8,128)S(1)}, f32[64,64]{1,0:T(8,128)S(1)}, u32[]{:S(2)}, u32[]{:S(2)}) collective-permute-start(f32[64,64]{1,0:T(8,128)S(1)} %add_add_fusion.2), channel_id=1, source_target_pairs={{0,32},{32,64},{64,96},{96,0},{1,33},{33,65},{65,97},{97,1},{2,34}... | collective-permute-start | bytes 49160 | tf_op jit(solution)/shard_map/ppermute | solution.py:154
  63.2 5.3 %collective-permute-start.14 = (f32[64,64]{1,0:T(8,128)S(1)}, f32[64,64]{1,0:T(8,128)S(1)}, u32[]{:S(2)}, u32[]{:S(2)}) collective-permute-start(f32[64,64]{1,0:T(8,128)S(1)} %add_add_fusion.2), channel_id=1, source_target_pairs={{0,96},{32,0},{64,32},{96,64},{1,97},{33,1},{65,33},{97,65},{2,98}... | collective-permute-start | bytes 49160 | tf_op jit(solution)/shard_map/ppermute | solution.py:154
  66.2 5.4 %collective-permute-start.15 = (f32[64,64]{1,0:T(8,128)S(1)}, f32[64,64]{1,0:T(8,128)S(1)}, u32[]{:S(2)}, u32[]{:S(2)}) collective-permute-start(f32[64,64]{1,0:T(8,128)S(1)} %add_add_fusion.2), channel_id=1, source_target_pairs={{0,64},{32,96},{64,0},{96,32},{1,65},{33,97},{65,1},{97,33},{2,66}... | collective-permute-start | bytes 49160 | tf_op jit(solution)/shard_map/ppermute | solution.py:154
  71.9 5.6 %collective-permute-start.16 = (f32[64,256]{1,0:T(8,128)S(1)}, f32[64,256]{1,0:T(8,128)S(1)}, u32[]{:S(2)}, u32[]{:S(2)}) collective-permute-start(f32[64,256]{1,0:T(8,128)S(1)} %dynamic_update_slice.51), channel_id=1, source_target_pairs={{0,1},{1,2},{2,3},{3,0},{4,5},{5,6},{6,7},{7,4},{8,9},{9,10},{10,1... | collective-permute-start | bytes 196616 | tf_op jit(solution)/shard_map/ppermute | solution.py:154
  72.2 5.3 %collective-permute-start.17 = (f32[64,256]{1,0:T(8,128)S(1)}, f32[64,256]{1,0:T(8,128)S(1)}, u32[]{:S(2)}, u32[]{:S(2)}) collective-permute-start(f32[64,256]{1,0:T(8,128)S(1)} %dynamic_update_slice.51), channel_id=1, source_target_pairs={{0,3},{1,0},{2,1},{3,2},{4,7},{5,4},{6,5},{7,6},{8,11},{9,8},{10,9... | collective-permute-start | bytes 196616 | tf_op jit(solution)/shard_map/ppermute | solution.py:154
  75.2 5.8 %collective-permute-start.18 = (f32[64,256]{1,0:T(8,128)S(1)}, f32[64,256]{1,0:T(8,128)S(1)}, u32[]{:S(2)}, u32[]{:S(2)}) collective-permute-start(f32[64,256]{1,0:T(8,128)S(1)} %dynamic_update_slice.51), channel_id=1, source_target_pairs={{0,2},{1,3},{2,0},{3,1},{4,6},{5,7},{6,4},{7,5},{8,10},{9,11},{10,... | collective-permute-start | bytes 196616 | tf_op jit(solution)/shard_map/ppermute | solution.py:154
  81.0 10.5 %collective-permute-start.19 = (f32[64,1024]{1,0:T(8,128)S(1)}, f32[64,1024]{1,0:T(8,128)S(1)}, u32[]{:S(2)}, u32[]{:S(2)}) collective-permute-start(f32[64,1024]{1,0:T(8,128)S(1)} %constant_dynamic-update-slice_fusion.8), channel_id=1, source_target_pairs={{0,4},{4,8},{8,12},{12,16},{16,20},{20,24},{24,28},{28,0},{128,156... | collective-permute-start | bytes 786440 | tf_op jit(solution)/shard_map/ppermute | solution.py:95
  81.1 10.9 %collective-permute-start.20 = (f32[64,1024]{1,0:T(8,128)S(1)}, f32[64,1024]{1,0:T(8,128)S(1)}, u32[]{:S(2)}, u32[]{:S(2)}) collective-permute-start(f32[64,1024]{1,0:T(8,128)S(1)} %constant_dynamic-update-slice_fusion.8), channel_id=1, source_target_pairs={{4,0},{8,4},{12,8},{16,12},{20,16},{24,20},{28,24},{0,28},{156,128... | collective-permute-start | bytes 786440 | tf_op jit(solution)/shard_map/ppermute | solution.py:95
  84.3 7.1 %copy-start.6 = (s32[64]{0:T(128)S(1)}, s32[64]{0:T(128)}, u32[]{:S(2)}) copy-start(s32[64]{0:T(128)} %param.9) | copy-start | bytes 772
  91.5 9.5 %collective-permute-start.21 = (f32[64,1024]{1,0:T(8,128)S(1)}, f32[64,1024]{1,0:T(8,128)S(1)}, u32[]{:S(2)}, u32[]{:S(2)}) collective-permute-start(f32[64,1024]{1,0:T(8,128)S(1)} %collective-permute-done.19), channel_id=1, source_target_pairs={{0,4},{4,8},{8,12},{12,16},{16,20},{20,24},{24,28},{28,0},{128,156... | collective-permute-start | bytes 786440 | tf_op jit(solution)/shard_map/ppermute | solution.py:95
  92.0 9.1 %collective-permute-start.22 = (f32[64,1024]{1,0:T(8,128)S(1)}, f32[64,1024]{1,0:T(8,128)S(1)}, u32[]{:S(2)}, u32[]{:S(2)}) collective-permute-start(f32[64,1024]{1,0:T(8,128)S(1)} %collective-permute-done.20), channel_id=1, source_target_pairs={{4,0},{8,4},{12,8},{16,12},{20,16},{24,20},{28,24},{0,28},{156,128... | collective-permute-start | bytes 786440 | tf_op jit(solution)/shard_map/ppermute | solution.py:95
  101.0 7.6 %collective-permute-start.23 = (f32[64,1024]{1,0:T(8,128)S(1)}, f32[64,1024]{1,0:T(8,128)S(1)}, u32[]{:S(2)}, u32[]{:S(2)}) collective-permute-start(f32[64,1024]{1,0:T(8,128)S(1)} %collective-permute-done.21), channel_id=1, source_target_pairs={{0,4},{4,8},{8,12},{12,16},{16,20},{20,24},{24,28},{28,0},{128,156... | collective-permute-start | bytes 786440 | tf_op jit(solution)/shard_map/ppermute | solution.py:95
  101.1 7.6 %collective-permute-start.24 = (f32[64,1024]{1,0:T(8,128)S(1)}, f32[64,1024]{1,0:T(8,128)S(1)}, u32[]{:S(2)}, u32[]{:S(2)}) collective-permute-start(f32[64,1024]{1,0:T(8,128)S(1)} %collective-permute-done.22), channel_id=1, source_target_pairs={{4,0},{8,4},{12,8},{16,12},{20,16},{24,20},{28,24},{0,28},{156,128... | collective-permute-start | bytes 786440 | tf_op jit(solution)/shard_map/ppermute | solution.py:95
  108.6 7.6 %collective-permute-start.25 = (f32[64,1024]{1,0:T(8,128)S(1)}, f32[64,1024]{1,0:T(8,128)S(1)}, u32[]{:S(2)}, u32[]{:S(2)}) collective-permute-start(f32[64,1024]{1,0:T(8,128)S(1)} %collective-permute-done.23), channel_id=1, source_target_pairs={{0,4},{4,8},{8,12},{12,16},{16,20},{20,24},{24,28},{28,0},{128,156... | collective-permute-start | bytes 786440 | tf_op jit(solution)/shard_map/ppermute | solution.py:95
  116.2 1.4 %copy-start.2 = (f32[64,8192]{1,0:T(8,128)}, f32[64,8192]{1,0:T(8,128)S(1)}, u32[]{:S(2)}) copy-start(f32[64,8192]{1,0:T(8,128)S(1)} %constant_dynamic-update-slice_fusion) | copy-start | bytes 6291460
  119.0 0.7 copy-start.4

commit v6 on v3

--- a/solution.py
+++ b/solution.py
@@ -145,7 +145,7 @@
     return out
 
 
-SHIFTS = {2: (1,), 4: (1, -1, 2)}
+SHIFTS = {2: (1,), 4: (2, 1, -1)}
 
 
 def ring_allreduce(x, phases):

time: 131 us -> 129 us (0.985)
  waiting for transfers between devices: 59 us -> 52.3 us
  starting transfers between devices: 38.1 us -> 42.5 us
    ppermute x6, waiting for transfers between devices: 7.66 us -> 4.13 us  [direct_rs(): total = total + lax.ppermute(chunk(i + d), axis, shift_perm(n, d))]
    ppermute x6, waiting for transfers between devices: 8.67 us -> 5.78 us  [direct_ag(): got = lax.ppermute(x, axis, shift_perm(n, d))]
    ppermute x6, starting transfers between devices: 10.4 us -> 12.9 us  [direct_rs(): total = total + lax.ppermute(chunk(i + d), axis, shift_perm(n, d))]
    ppermute x6, starting transfers between devices: 7.59 us -> 9.57 us  [direct_ag(): got = lax.ppermute(x, axis, shift_perm(n, d))]
  transfers between devices with their start and end apart: 26 -> 26, of which waited for: 18 -> 16; matrix products, arithmetic and copies ran while one was open for 6% -> 6% of each run, Pallas kernels for 0% -> 0%
where the time goes in v6:
time: 129 us
  waiting for transfers between devices  52.3 us (41%)
  starting transfers between devices  42.5 us (33%)
  matrix products  11.1 us (9%)
  local copies, waits for them, and re-layouts  9.96 us (8%)
  Pallas kernels  8.64 us (7%)
  other arithmetic  3.23 us (3%)
    ppermute x4, waiting for transfers between devices, half_ring_rs(): cw = lax.ppermute(cw, axis, shift_perm(n, 1))  24.8 us
    ppermute x4, waiting for transfers between devices, half_ring_ag(): cw = lax.ppermute(cw, axis, shift_perm(n, 1))  17 us
    ppermute x6, starting transfers between devices, direct_rs(): total = total + lax.ppermute(chunk(i + d), axis, shift_perm(n, d))  12.9 us
    ppermute x6, starting transfers between devices, direct_ag(): got = lax.ppermute(x, axis, shift_perm(n, d))  9.57 us
    pallas_call x1, Pallas kernels, border(): pl.pallas_call(_border_kernel, out_shape=(jax.ShapeDtypeStruct((n, n), jn...  8.64 us
    ppermute x3, starting transfers between devices, half_ring_rs(): ccw = lax.ppermute(ccw, axis, shift_perm(n, -1))  7.97 us
    ppermute x6, waiting for transfers between devices, direct_ag(): got = lax.ppermute(x, axis, shift_perm(n, d))  5.78 us
    ppermute x3, starting transfers between devices, half_ring_ag(): ccw = lax.ppermute(ccw, axis, shift_perm(n, -1))  5.6 us
  transfers between devices with their start and end apart: 26, of which 16 were waited for; matrix products, arithmetic and copies ran while one was open for 6% of the time, Pallas kernels for 0%

profile of v6, /device:TPU:0, one launch (start us, length us, event | category | flops | bytes accessed | tf_op | source)
XLA Modules:
  0.0 128.7 jit_solution(13450853889623330832)
XLA Ops:
  0.7 0.7 compare_bitcast_fusion
  2.0 3.5 %fusion.8 = f32[64,8192]{1,0:T(8,128)S(1)} fusion(f32[64,64]{1,0:T(8,128)S(1)} %bitcast.16, f32[64,8192]{1,0:T(8,128)} %param.5), kind=kOutput, calls=%fused_computation.44 | convolution fusion | flops 402653184 | bytes 4210688 | tf_op jit(solution)/shard_map/dot_general | solution.py:167
  5.8 10.2 %collective-permute-done = f32[64,1024]{1,0:T(8,128)S(1)} collective-permute-done((f32[64,1024]{1,0:T(8,128)S(1)}, f32[64,1024]{1,0:T(8,128)S(1)}, u32[]{:S(2)}, u32[]{:S(2)}) %collective-permute-start) | collective-permute-done | bytes 262176 | tf_op jit(solution)/shard_map/ppermute | solution.py:98
  16.2 3.2 %collective-permute-start.4 = (f32[64,1024]{1,0:T(8,128)S(1)}, f32[64,1024]{1,0:T(8,128)S(1)}, u32[]{:S(2)}, u32[]{:S(2)}) collective-permute-start(f32[64,1024]{1,0:T(8,128)S(1)} %get-tuple-element.11), channel_id=1, source_target_pairs={{0,28},{4,0},{8,4},{12,8},{16,12},{20,16},{24,20},{28,24},{1,29},{... | collective-permute-start | bytes 786440 | tf_op jit(solution)/shard_map/ppermute | solution.py:100
  19.4 5.4 %collective-permute-done.1 = f32[64,1024]{1,0:T(8,128)S(1)} collective-permute-done((f32[64,1024]{1,0:T(8,128)S(1)}, f32[64,1024]{1,0:T(8,128)S(1)}, u32[]{:S(2)}, u32[]{:S(2)}) %collective-permute-start.1) | collective-permute-done | bytes 262176 | tf_op jit(solution)/shard_map/ppermute | solution.py:98
  24.8 0.8 dynamic-slice_add_fusion.3
  25.6 3.2 %collective-permute-start.5 = (f32[64,1024]{1,0:T(8,128)S(1)}, f32[64,1024]{1,0:T(8,128)S(1)}, u32[]{:S(2)}, u32[]{:S(2)}) collective-permute-start(f32[64,1024]{1,0:T(8,128)S(1)} %get-tuple-element.9), channel_id=1, source_target_pairs={{0,28},{4,0},{8,4},{12,8},{16,12},{20,16},{24,20},{28,24},{1,29},{... | collective-permute-start | bytes 786440 | tf_op jit(solution)/shard_map/ppermute | solution.py:100
  28.8 4.8 %collective-permute-done.2 = f32[64,1024]{1,0:T(8,128)S(1)} collective-permute-done((f32[64,1024]{1,0:T(8,128)}, f32[64,1024]{1,0:T(8,128)S(1)}, u32[]{:S(2)}, u32[]{:S(2)}) %collective-permute-start.2) | collective-permute-done | bytes 262176 | tf_op jit(solution)/shard_map/ppermute | solution.py:98
  33.7 1.8 %collective-permute-start.3 = (f32[64,1024]{1,0:T(8,128)S(1)}, f32[64,1024]{1,0:T(8,128)S(1)}, u32[]{:S(2)}, u32[]{:S(2)}) collective-permute-start(f32[64,1024]{1,0:T(8,128)S(1)} %get-tuple-element.6), channel_id=1, source_target_pairs={{0,4},{4,8},{8,12},{12,16},{16,20},{20,24},{24,28},{28,0},{1,5},{5... | collective-permute-start | bytes 786440 | tf_op jit(solution)/shard_map/ppermute | solution.py:98
  35.5 1.5 %collective-permute-start.6 = (f32[64,1024]{1,0:T(8,128)S(1)}, f32[64,1024]{1,0:T(8,128)S(1)}, u32[]{:S(2)}, u32[]{:S(2)}) collective-permute-start(f32[64,1024]{1,0:T(8,128)S(1)} %get-tuple-element.7), channel_id=1, source_target_pairs={{0,28},{4,0},{8,4},{12,8},{16,12},{20,16},{24,20},{28,24},{1,29},{... | collective-permute-start | bytes 786440 | tf_op jit(solution)/shard_map/ppermute | solution.py:100
  37.0 4.3 %collective-permute-done.3 = f32[64,1024]{1,0:T(8,128)S(1)} collective-permute-done((f32[64,1024]{1,0:T(8,128)S(1)}, f32[64,1024]{1,0:T(8,128)S(1)}, u32[]{:S(2)}, u32[]{:S(2)}) %collective-permute-start.3) | collective-permute-done | bytes 262176 | tf_op jit(solution)/shard_map/ppermute | solution.py:98
  41.9 1.0 add_add_fusion
  42.9 3.3 %collective-permute-start.7 = (f32[64,256]{1,0:T(8,128)S(1)}, f32[64,256]{1,0:T(8,128)S(1)}, u32[]{:S(2)}, u32[]{:S(2)}) collective-permute-start(f32[64,256]{1,0:T(8,128)S(1)} %get-tuple-element.12), channel_id=1, source_target_pairs={{0,2},{1,3},{2,0},{3,1},{4,6},{5,7},{6,4},{7,5},{8,10},{9,11},{10,... | collective-permute-start | bytes 196616 | tf_op jit(solution)/shard_map/ppermute | solution.py:133
  46.2 0.7 collective-permute-start.8
  46.9 2.6 %collective-permute-start.9 = (f32[64,256]{1,0:T(8,128)S(1)}, f32[64,256]{1,0:T(8,128)S(1)}, u32[]{:S(2)}, u32[]{:S(2)}) collective-permute-start(f32[64,256]{1,0:T(8,128)S(1)} %get-tuple-element.13), channel_id=1, source_target_pairs={{0,3},{1,0},{2,1},{3,2},{4,7},{5,4},{6,5},{7,6},{8,11},{9,8},{10,9... | collective-permute-start | bytes 196616 | tf_op jit(solution)/shard_map/ppermute | solution.py:133
  49.4 2.2 %collective-permute-done.8 = f32[64,256]{1,0:T(8,128)S(1)} collective-permute-done((f32[64,256]{1,0:T(8,128)S(1)}, f32[64,256]{1,0:T(8,128)S(1)}, u32[]{:S(2)}, u32[]{:S(2)}) %collective-permute-start.8) | collective-permute-done | bytes 65568 | tf_op jit(solution)/shard_map/ppermute | solution.py:133
  51.8 3.1 %collective-permute-start.10 = (f32[64,64]{1,0:T(8,128)S(1)}, f32[64,64]{1,0:T(8,128)S(1)}, u32[]{:S(2)}, u32[]{:S(2)}) collective-permute-start(f32[64,64]{1,0:T(8,128)S(1)} %get-tuple-element.15), channel_id=1, source_target_pairs={{0,64},{32,96},{64,0},{96,32},{1,65},{33,97},{65,1},{97,33},{2,66}... | collective-permute-start | bytes 49160 | tf_op jit(solution)/shard_map/ppermute | solution.py:133
  54.9 0.6 collective-permute-start.11
  55.5 2.6 %collective-permute-start.12 = (f32[64,64]{1,0:T(8,128)S(1)}, f32[64,64]{1,0:T(8,128)S(1)}, u32[]{:S(2)}, u32[]{:S(2)}) collective-permute-start(f32[64,64]{1,0:T(8,128)S(1)} %get-tuple-element.16), channel_id=1, source_target_pairs={{0,96},{32,0},{64,32},{96,64},{1,97},{33,1},{65,33},{97,65},{2,98}... | collective-permute-start | bytes 49160 | tf_op jit(solution)/shard_map/ppermute | solution.py:133
  58.2 1.9 %collective-permute-done.11 = f32[64,64]{1,0:T(8,128)S(1)} collective-permute-done((f32[64,64]{1,0:T(8,128)S(1)}, f32[64,64]{1,0:T(8,128)S(1)}, u32[]{:S(2)}, u32[]{:S(2)}) %collective-permute-start.11) | collective-permute-done | bytes 16416 | tf_op jit(solution)/shard_map/ppermute | solution.py:133
  60.1 1.5 %collective-permute-start.13 = (f32[64,64]{1,0:T(8,128)S(1)}, f32[64,64]{1,0:T(8,128)S(1)}, u32[]{:S(2)}, u32[]{:S(2)}) collective-permute-start(f32[64,64]{1,0:T(8,128)S(1)} %add_add_fusion.2), channel_id=1, source_target_pairs={{0,64},{32,96},{64,0},{96,32},{1,65},{33,97},{65,1},{97,33},{2,66}... | collective-permute-start | bytes 49160 | tf_op jit(solution)/shard_map/ppermute | solution.py:143
  61.7 2.6 %collective-permute-start.14 = (f32[64,64]{1,0:T(8,128)S(1)}, f32[64,64]{1,0:T(8,128)S(1)}, u32[]{:S(2)}, u32[]{:S(2)}) collective-permute-start(f32[64,64]{1,0:T(8,128)S(1)} %add_add_fusion.2), channel_id=1, source_target_pairs={{0,32},{32,64},{64,96},{96,0},{1,33},{33,65},{65,97},{97,1},{2,34}... | collective-permute-start | bytes 49160 | tf_op jit(solution)/shard_map/ppermute | solution.py:143
  64.3 0.6 collective-permute-start.15
  65.9 0.9 collective-permute-done.14
  67.2 1.0 collective-permute-done.15
  68.8 1.5 %collective-permute-start.16 = (f32[64,256]{1,0:T(8,128)S(1)}, f32[64,256]{1,0:T(8,128)S(1)}, u32[]{:S(2)}, u32[]{:S(2)}) collective-permute-start(f32[64,256]{1,0:T(8,128)S(1)} %dynamic_update_slice.51), channel_id=1, source_target_pairs={{0,2},{1,3},{2,0},{3,1},{4,6},{5,7},{6,4},{7,5},{8,10},{9,11},{10,... | collective-permute-start | bytes 196616 | tf_op jit(solution)/shard_map/ppermute | solution.py:143
  70.3 2.6 %collective-permute-start.17 = (f32[64,256]{1,0:T(8,128)S(1)}, f32[64,256]{1,0:T(8,128)S(1)}, u32[]{:S(2)}, u32[]{:S(2)}) collective-permute-start(f32[64,256]{1,0:T(8,128)S(1)} %dynamic_update_slice.51), channel_id=1, source_target_pairs={{0,1},{1,2},{2,3},{3,0},{4,5},{5,6},{6,7},{7,4},{8,9},{9,10},{10,1... | collective-permute-start | bytes 196616 | tf_op jit(solution)/shard_map/ppermute | solution.py:143
  73.0 0.6 collective-permute-start.18
  73.6 1.0 collective-permute-done.16
  74.6 1.2 collective-permute-done.17
  75.8 1.4 %collective-permute-done.18 = f32[64,256]{1,0:T(8,128)S(1)} collective-permute-done((f32[64,256]{1,0:T(8,128)S(1)}, f32[64,256]{1,0:T(8,128)S(1)}, u32[]{:S(2)}, u32[]{:S(2)}) %collective-permute-start.18) | collective-permute-done | bytes 65568 | tf_op jit(solution)/shard_map/ppermute | solution.py:143
  77.2 2.1 %collective-permute-start.19 = (f32[64,1024]{1,0:T(8,128)S(1)}, f32[64,1024]{1,0:T(8,128)S(1)}, u32[]{:S(2)}, u32[]{:S(2)}) collective-permute-start(f32[64,1024]{1,0:T(8,128)S(1)} %constant_dynamic-update-slice_fusion.8), channel_id=1, source_target_pairs={{0,4},{4,8},{8,12},{12,16},{16,20},{20,24},{24,28},{28,0},{1,5},{5... | collective-permute-start | bytes 786440 | tf_op jit(solution)/shard_map/ppermute | solution.py:120
  79.3 1.2 collective-permute-start.20
  80.6 2.7 %copy.9 = f32[64,8192]{0,1:T(8,128)} copy(f32[64,8192]{1,0:T(8,128)S(1)} %copy-done.1) | data formatting | bytes 4194304 | tf_op args[0]
  83.3 2.8 %gather_fusion = f32[64,64]{1,0:T(8,128)S(1)} fusion(f32[64,8192]{0,1:T(8,128)} %copy.9, s32[1024]{0:T(1024)S(1)} %pad_clamp_fusion), kind=kCustom, calls=%fused_computation | custom fusion | bytes 33024 | tf_op jit(solution)/shard_map/jit(_take)/gather | solution.py:166
  86.1 1.3 %collective-permute-start.21 = (f32[64,1024]{1,0:T(8,128)S(1)}, f32[64,1024]{1,0:T(8,128)S(1)}, u32[]{:S(2)}, u32[]{:S(2)}) collective-permute-start(f32[64,1024]{1,0:T(8,128)S(1)} %collective-permute-done.19), channel_id=1, source_target_pairs={{0,4},{4,8},{8,12},{12,16},{16,20},{20,24},{24,28},{28,0},{1,5},{5... | collective-permute-start | bytes 786440 | tf_op jit(solution)/shard_map/ppermute | solution.py:120
  88.0 2.0 %collective-permute-start.22 = (f32[64,1024]{1,0:T(8,128)S(1)}, f32[64,1024]{1,0:T(8,128)S(1)}, u32[]{:S(2)}, u32[]{:S(2)}) collective-permute-start(f32[64,1024]{1,0:T(8,128)S(1)} %collective-permute-done.20), channel_id=1, source_target_pairs={{0,28},{4,0},{8,4},{12,8},{16,12},{20,16},{24,20},{28,24},{1,29},{... | collective-permute-start | bytes 786440 | tf_op jit(solution)/shard_map/ppermute | solution.py:123
  90.1 5.3 %collective-permute-done.21 = f32[64,1024]{1,0:T(8,128)S(1)} collective-permute-done((f32[64,1024]{1,0:T(8,128)S(1)}, f32[64,1024]{1,0:T(8,128)S(1)}, u32[]{:S(2)}, u32[]{:S(2)}) %collective-permute-start.21) | collective-permute-done | bytes 262176 | tf_op jit(solution)/shard_map/ppermute | solution.py:120
  95.5 0.9 collective-permute-start.23
  96.4 2.4 %collective-permute-start.24 = (f32[64,1024]{1,0:T(8,128)S(1)}, f32[64,1024]{1,0:T(8,128)S(1)}, u32[]{:S(2)}, u32[]{:S(2)}) collective-permute-start(f32[64,1024]{1,0:T(8,128)S(1)} %collective-permute-done.22), channel_id=1, source_target_pairs={{0,28},{4,0},{8,4},{12,8},{16,12},{20,16},{24,20},{28,24},{1,29},{... | collective-permute-start | bytes 786440 | tf_op jit(solution)/shard_map/ppermute | solution.py:123
  98.9 4.2 %collective-permute-done.23 = f32[64,1024]{1,0:T(8,128)S(1)} collective-permute-done((f32[64,1024]{1,0:T(8,128)S(1)}, f32[64,1024]{1,0:T(8,128)S(1)}, u32[]{:S(2)}, u32[]{:S(2)}) %collective-permute-start.23) | collective-permute-done | bytes 262176 | tf_op jit(solution)/shard_map/ppermute | solution.py:120
  103.1 7.5 %collective-permute-done.25 = f32[64,1024]{1,0:T(8,128)S(1)} collective-permute-done((f32[64,1024]{1,0:T(8,128)S(1)}, f32[64,1024]{1,0:T(8,128)S(1)}, u32[]{:S(2)}, u32[]{:S(2)}) %collective-permute-start.25) | collective-permute-done | bytes 262176 | tf_op jit(solution)/shard_map/ppermute | solution.py:120
  110.7 1.4 %copy-done.2 = f32[64,8192]{1,0:T(8,128)} copy-done((f32[64,8192]{1,0:T(8,128)}, f32[64,8192]{1,0:T(8,128)S(1)}, u32[]{:S(2)}) %copy-start.2) | copy-done | bytes 2097176
  112.0 1.4 %fusion.m_ref = f32[64,64]{1,0:T(8,128)S(1)} fusion(f32[64,8192]{1,0:T(8,128)S(1)} %constant_dynamic-update-slice_fusion, s32[64]{0:T(128)S(1)} %copy-done.5), kind=kOutput, calls=%fused_computation.3 | convolution fusion | flops 403177472 | bytes 2113792 | tf_op jit(solution)/shard_map/dot_general | solution.py:171
  113.5 0.7 copy.10
  114.2 8.6 %shard_map.68 = (f32[64,64]{1,0:T(8,128)}, f32[1,64]{1,0:T(1,128)}) custom-call(f32[64,64]{1,0:T(8,128)} %copy-done.4, f32[64,64]{1,0:T(8,128)} %bitcast.17, f32[1,64]{1,0:T(1,128)} %convert_bitcast_fusion.acc_ref), custom_call_target="tpu_custom_call" | custom-call | tf_op jit(solution)/shard_map/pallas_call | solution.py:76
  122.8 1.1 fusion.2
  123.9 4.8 %convolution_subtract_fusion = f32[64,8192]{1,0:T(8,128)} fusion(f32[64,8192]{1,0:T(8,128)S(1)} %copy-done.1, f32[64,64]{1,0:T(8,128)S(1)} %fusion.2, f32[64,8192]{1,0:T(8,128)} %copy-done.2), kind=kOutput, calls=%fused_computation.1 | convolution fusion | flops 403177472 | bytes 6307840 | tf_op jit(solution)/shard_map/dot_general | solution.py:174
  (61 shorter events, 4.6 us)
Async XLA Ops:
  0.6 1.0 copy-start
  5.4 28.2 %copy-start.3 = (f32[64,8192]{1,0:T(8,128)}, f32[64,8192]{1,0:T(8,128)S(1)}, u32[]{:S(2)}) copy-start(f32[64,8192]{1,0:T(8,128)S(1)} %fusion.8) | copy-start | bytes 6291460
  5.5 10.5 %collective-permute-start = (f32[64,1024]{1,0:T(8,128)S(1)}, f32[64,1024]{1,0:T(8,128)S(1)}, u32[]{:S(2)}, u32[]{:S(2)}) collective-permute-start(f32[64,1024]{1,0:T(8,128)S(1)} %constant_dynamic-slice_fusion.7), channel_id=1, source_target_pairs={{0,4},{4,8},{8,12},{12,16},{16,20},{20,24},{24,28},{28,0},{1,5},{5... | collective-permute-start | bytes 786440 | tf_op jit(solution)/shard_map/ppermute | solution.py:98
  16.1 8.8 %collective-permute-start.1 = (f32[64,1024]{1,0:T(8,128)S(1)}, f32[64,1024]{1,0:T(8,128)S(1)}, u32[]{:S(2)}, u32[]{:S(2)}) collective-permute-start(f32[64,1024]{1,0:T(8,128)S(1)} %get-tuple-element.10), channel_id=1, source_target_pairs={{0,4},{4,8},{8,12},{12,16},{16,20},{20,24},{24,28},{28,0},{1,5},{5... | collective-permute-start | bytes 786440 | tf_op jit(solution)/shard_map/ppermute | solution.py:98
  16.2 8.7 %collective-permute-start.4 = (f32[64,1024]{1,0:T(8,128)S(1)}, f32[64,1024]{1,0:T(8,128)S(1)}, u32[]{:S(2)}, u32[]{:S(2)}) collective-permute-start(f32[64,1024]{1,0:T(8,128)S(1)} %get-tuple-element.11), channel_id=1, source_target_pairs={{0,28},{4,0},{8,4},{12,8},{16,12},{20,16},{24,20},{28,24},{1,29},{... | collective-permute-start | bytes 786440 | tf_op jit(solution)/shard_map/ppermute | solution.py:100
  25.6 39.3 %copy-start.5 = (s32[64]{0:T(128)S(1)}, s32[64]{0:T(128)}, u32[]{:S(2)}) copy-start(s32[64]{0:T(128)} %param.8) | copy-start | bytes 772
  25.6 8.0 %collective-permute-start.2 = (f32[64,1024]{1,0:T(8,128)}, f32[64,1024]{1,0:T(8,128)S(1)}, u32[]{:S(2)}, u32[]{:S(2)}) collective-permute-start(f32[64,1024]{1,0:T(8,128)} %get-tuple-element.8), channel_id=1, source_target_pairs={{0,4},{4,8},{8,12},{12,16},{16,20},{20,24},{24,28},{28,0},{1,5},{5... | collective-permute-start | bytes 786440 | tf_op jit(solution)/shard_map/ppermute | solution.py:98
  25.6 8.0 %collective-permute-start.5 = (f32[64,1024]{1,0:T(8,128)S(1)}, f32[64,1024]{1,0:T(8,128)S(1)}, u32[]{:S(2)}, u32[]{:S(2)}) collective-permute-start(f32[64,1024]{1,0:T(8,128)S(1)} %get-tuple-element.9), channel_id=1, source_target_pairs={{0,28},{4,0},{8,4},{12,8},{16,12},{20,16},{24,20},{28,24},{1,29},{... | collective-permute-start | bytes 786440 | tf_op jit(solution)/shard_map/ppermute | solution.py:100
  33.7 46.8 %copy-start.1 = (f32[64,8192]{1,0:T(8,128)S(1)}, f32[64,8192]{1,0:T(8,128)}, u32[]{:S(2)}) copy-start(f32[64,8192]{1,0:T(8,128)} %param.5) | copy-start | bytes 6291460
  33.7 7.7 %collective-permute-start.3 = (f32[64,1024]{1,0:T(8,128)S(1)}, f32[64,1024]{1,0:T(8,128)S(1)}, u32[]{:S(2)}, u32[]{:S(2)}) collective-permute-start(f32[64,1024]{1,0:T(8,128)S(1)} %get-tuple-element.6), channel_id=1, source_target_pairs={{0,4},{4,8},{8,12},{12,16},{16,20},{20,24},{24,28},{28,0},{1,5},{5... | collective-permute-start | bytes 786440 | tf_op jit(solution)/shard_map/ppermute | solution.py:98
  35.5 6.4 %collective-permute-start.6 = (f32[64,1024]{1,0:T(8,128)S(1)}, f32[64,1024]{1,0:T(8,128)S(1)}, u32[]{:S(2)}, u32[]{:S(2)}) collective-permute-start(f32[64,1024]{1,0:T(8,128)S(1)} %get-tuple-element.7), channel_id=1, source_target_pairs={{0,28},{4,0},{8,4},{12,8},{16,12},{20,16},{24,20},{28,24},{1,29},{... | collective-permute-start | bytes 786440 | tf_op jit(solution)/shard_map/ppermute | solution.py:100
  42.9 6.5 %collective-permute-start.7 = (f32[64,256]{1,0:T(8,128)S(1)}, f32[64,256]{1,0:T(8,128)S(1)}, u32[]{:S(2)}, u32[]{:S(2)}) collective-permute-start(f32[64,256]{1,0:T(8,128)S(1)} %get-tuple-element.12), channel_id=1, source_target_pairs={{0,2},{1,3},{2,0},{3,1},{4,6},{5,7},{6,4},{7,5},{8,10},{9,11},{10,... | collective-permute-start | bytes 196616 | tf_op jit(solution)/shard_map/ppermute | solution.py:133
  46.2 5.5 %collective-permute-start.8 = (f32[64,256]{1,0:T(8,128)S(1)}, f32[64,256]{1,0:T(8,128)S(1)}, u32[]{:S(2)}, u32[]{:S(2)}) collective-permute-start(f32[64,256]{1,0:T(8,128)S(1)} %get-tuple-element.14), channel_id=1, source_target_pairs={{0,1},{1,2},{2,3},{3,0},{4,5},{5,6},{6,7},{7,4},{8,9},{9,10},{10,1... | collective-permute-start | bytes 196616 | tf_op jit(solution)/shard_map/ppermute | solution.py:133
  46.9 4.8 %collective-permute-start.9 = (f32[64,256]{1,0:T(8,128)S(1)}, f32[64,256]{1,0:T(8,128)S(1)}, u32[]{:S(2)}, u32[]{:S(2)}) collective-permute-start(f32[64,256]{1,0:T(8,128)S(1)} %get-tuple-element.13), channel_id=1, source_target_pairs={{0,3},{1,0},{2,1},{3,2},{4,7},{5,4},{6,5},{7,6},{8,11},{9,8},{10,9... | collective-permute-start | bytes 196616 | tf_op jit(solution)/shard_map/ppermute | solution.py:133
  51.8 6.3 %collective-permute-start.10 = (f32[64,64]{1,0:T(8,128)S(1)}, f32[64,64]{1,0:T(8,128)S(1)}, u32[]{:S(2)}, u32[]{:S(2)}) collective-permute-start(f32[64,64]{1,0:T(8,128)S(1)} %get-tuple-element.15), channel_id=1, source_target_pairs={{0,64},{32,96},{64,0},{96,32},{1,65},{33,97},{65,1},{97,33},{2,66}... | collective-permute-start | bytes 49160 | tf_op jit(solution)/shard_map/ppermute | solution.py:133
  54.9 5.1 %collective-permute-start.11 = (f32[64,64]{1,0:T(8,128)S(1)}, f32[64,64]{1,0:T(8,128)S(1)}, u32[]{:S(2)}, u32[]{:S(2)}) collective-permute-start(f32[64,64]{1,0:T(8,128)S(1)} %get-tuple-element.17), channel_id=1, source_target_pairs={{0,32},{32,64},{64,96},{96,0},{1,33},{33,65},{65,97},{97,1},{2,34}... | collective-permute-start | bytes 49160 | tf_op jit(solution)/shard_map/ppermute | solution.py:133
  55.5 4.5 %collective-permute-start.12 = (f32[64,64]{1,0:T(8,128)S(1)}, f32[64,64]{1,0:T(8,128)S(1)}, u32[]{:S(2)}, u32[]{:S(2)}) collective-permute-start(f32[64,64]{1,0:T(8,128)S(1)} %get-tuple-element.16), channel_id=1, source_target_pairs={{0,96},{32,0},{64,32},{96,64},{1,97},{33,1},{65,33},{97,65},{2,98}... | collective-permute-start | bytes 49160 | tf_op jit(solution)/shard_map/ppermute | solution.py:133
  60.1 5.5 %collective-permute-start.13 = (f32[64,64]{1,0:T(8,128)S(1)}, f32[64,64]{1,0:T(8,128)S(1)}, u32[]{:S(2)}, u32[]{:S(2)}) collective-permute-start(f32[64,64]{1,0:T(8,128)S(1)} %add_add_fusion.2), channel_id=1, source_target_pairs={{0,64},{32,96},{64,0},{96,32},{1,65},{33,97},{65,1},{97,33},{2,66}... | collective-permute-start | bytes 49160 | tf_op jit(solution)/shard_map/ppermute | solution.py:143
  61.7 5.1 %collective-permute-start.14 = (f32[64,64]{1,0:T(8,128)S(1)}, f32[64,64]{1,0:T(8,128)S(1)}, u32[]{:S(2)}, u32[]{:S(2)}) collective-permute-start(f32[64,64]{1,0:T(8,128)S(1)} %add_add_fusion.2), channel_id=1, source_target_pairs={{0,32},{32,64},{64,96},{96,0},{1,33},{33,65},{65,97},{97,1},{2,34}... | collective-permute-start | bytes 49160 | tf_op jit(solution)/shard_map/ppermute | solution.py:143
  64.3 3.9 %collective-permute-start.15 = (f32[64,64]{1,0:T(8,128)S(1)}, f32[64,64]{1,0:T(8,128)S(1)}, u32[]{:S(2)}, u32[]{:S(2)}) collective-permute-start(f32[64,64]{1,0:T(8,128)S(1)} %add_add_fusion.2), channel_id=1, source_target_pairs={{0,96},{32,0},{64,32},{96,64},{1,97},{33,1},{65,33},{97,65},{2,98}... | collective-permute-start | bytes 49160 | tf_op jit(solution)/shard_map/ppermute | solution.py:143
  68.8 5.9 %collective-permute-start.16 = (f32[64,256]{1,0:T(8,128)S(1)}, f32[64,256]{1,0:T(8,128)S(1)}, u32[]{:S(2)}, u32[]{:S(2)}) collective-permute-start(f32[64,256]{1,0:T(8,128)S(1)} %dynamic_update_slice.51), channel_id=1, source_target_pairs={{0,2},{1,3},{2,0},{3,1},{4,6},{5,7},{6,4},{7,5},{8,10},{9,11},{10,... | collective-permute-start | bytes 196616 | tf_op jit(solution)/shard_map/ppermute | solution.py:143
  70.3 5.5 %collective-permute-start.17 = (f32[64,256]{1,0:T(8,128)S(1)}, f32[64,256]{1,0:T(8,128)S(1)}, u32[]{:S(2)}, u32[]{:S(2)}) collective-permute-start(f32[64,256]{1,0:T(8,128)S(1)} %dynamic_update_slice.51), channel_id=1, source_target_pairs={{0,1},{1,2},{2,3},{3,0},{4,5},{5,6},{6,7},{7,4},{8,9},{9,10},{10,1... | collective-permute-start | bytes 196616 | tf_op jit(solution)/shard_map/ppermute | solution.py:143
  73.0 4.3 %collective-permute-start.18 = (f32[64,256]{1,0:T(8,128)S(1)}, f32[64,256]{1,0:T(8,128)S(1)}, u32[]{:S(2)}, u32[]{:S(2)}) collective-permute-start(f32[64,256]{1,0:T(8,128)S(1)} %dynamic_update_slice.51), channel_id=1, source_target_pairs={{0,3},{1,0},{2,1},{3,2},{4,7},{5,4},{6,5},{7,6},{8,11},{9,8},{10,9... | collective-permute-start | bytes 196616 | tf_op jit(solution)/shard_map/ppermute | solution.py:143
  77.2 8.9 %collective-permute-start.19 = (f32[64,1024]{1,0:T(8,128)S(1)}, f32[64,1024]{1,0:T(8,128)S(1)}, u32[]{:S(2)}, u32[]{:S(2)}) collective-permute-start(f32[64,1024]{1,0:T(8,128)S(1)} %constant_dynamic-update-slice_fusion.8), channel_id=1, source_target_pairs={{0,4},{4,8},{8,12},{12,16},{16,20},{20,24},{24,28},{28,0},{1,5},{5... | collective-permute-start | bytes 786440 | tf_op jit(solution)/shard_map/ppermute | solution.py:120
  79.3 8.6 %collective-permute-start.20 = (f32[64,1024]{1,0:T(8,128)S(1)}, f32[64,1024]{1,0:T(8,128)S(1)}, u32[]{:S(2)}, u32[]{:S(2)}) collective-permute-start(f32[64,1024]{1,0:T(8,128)S(1)} %constant_dynamic-update-slice_fusion.8), channel_id=1, source_target_pairs={{0,28},{4,0},{8,4},{12,8},{16,12},{20,16},{24,20},{28,24},{1,29},{... | collective-permute-start | bytes 786440 | tf_op jit(solution)/shard_map/ppermute | solution.py:123
  80.6 6.9 %copy-start.6 = (s32[64]{0:T(128)S(1)}, s32[64]{0:T(128)}, u32[]{:S(2)}) copy-start(s32[64]{0:T(128)} %param.9) | copy-start | bytes 772
  86.1 9.4 %collective-permute-start.21 = (f32[64,1024]{1,0:T(8,128)S(1)}, f32[64,1024]{1,0:T(8,128)S(1)}, u32[]{:S(2)}, u32[]{:S(2)}) collective-permute-start(f32[64,1024]{1,0:T(8,128)S(1)} %collective-permute-done.19), channel_id=1, source_target_pairs={{0,4},{4,8},{8,12},{12,16},{16,20},{20,24},{24,28},{28,0},{1,5},{5... | collective-permute-start | bytes 786440 | tf_op jit(solution)/shard_map/ppermute | solution.py:120
  88.0 8.5 %collective-permute-start.22 = (f32[64,1024]{1,0:T(8,128)S(1)}, f32[64,1024]{1,0:T(8,128)S(1)}, u32[]{:S(2)}, u32[]{:S(2)}) collective-permute-start(f32[64,1024]{1,0:T(8,128)S(1)} %collective-permute-done.20), channel_id=1, source_target_pairs={{0,28},{4,0},{8,4},{12,8},{16,12},{20,16},{24,20},{28,24},{1,29},{... | collective-permute-start | bytes 786440 | tf_op jit(solution)/shard_map/ppermute | solution.py:123
  95.5 7.6 %collective-permute-start.23 = (f32[64,1024]{1,0:T(8,128)S(1)}, f32[64,1024]{1,0:T(8,128)S(1)}, u32[]{:S(2)}, u32[]{:S(2)}) collective-permute-start(f32[64,1024]{1,0:T(8,128)S(1)} %collective-permute-done.21), channel_id=1, source_target_pairs={{0,4},{4,8},{8,12},{12,16},{16,20},{20,24},{24,28},{28,0},{1,5},{5... | collective-permute-start | bytes 786440 | tf_op jit(solution)/shard_map/ppermute | solution.py:120
  96.4 6.7 %collective-permute-start.24 = (f32[64,1024]{1,0:T(8,128)S(1)}, f32[64,1024]{1,0:T(8,128)S(1)}, u32[]{:S(2)}, u32[]{:S(2)}) collective-permute-start(f32[64,1024]{1,0:T(8,128)S(1)} %collective-permute-done.22), channel_id=1, source_target_pairs={{0,28},{4,0},{8,4},{12,8},{16,12},{20,16},{24,20},{28,24},{1,29},{... | collective-permute-start | bytes 786440 | tf_op jit(solution)/shard_map/ppermute | solution.py:123
  103.0 7.6 %collective-permute-start.25 = (f32[64,1024]{1,0:T(8,128)S(1)}, f32[64,1024]{1,0:T(8,128)S(1)}, u32[]{:S(2)}, u32[]{:S(2)}) collective-permute-start(f32[64,1024]{1,0:T(8,128)S(1)} %collective-permute-done.23), channel_id=1, source_target_pairs={{0,4},{4,8},{8,12},{12,16},{16,20},{20,24},{24,28},{28,0},{1,5},{5... | collective-permute-start | bytes 786440 | tf_op jit(solution)/shard_map/ppermute | solution.py:120
  110.7 1.4 %copy-start.2 = (f32[64,8192]{1,0:T(8,128)}, f32[64,8192]{1,0:T(8,128)S(1)}, u32[]{:S(2)}) copy-start(f32[64,8192]{1,0:T(8,128)S(1)} %constant_dynamic-update-slice_fusion) | copy-start | bytes 6291460
  113.4 0.7 copy-start.4

commit v7 on v6

--- a/solution.py
+++ b/solution.py
@@ -86,12 +86,11 @@
     return [(j, (j + d) % n) for j in range(n)]
 
 
-def half_ring_rs(x, axis, n):
-    if n == 1:
-        return x
-    i = lax.axis_index(axis)
-    width = x.shape[1] // n
-    chunk = lambda c: lax.dynamic_slice_in_dim(x, (c % n) * width, width, 1)
+def half_ring_rs(x, axis, n, chunk=None):
+    i = lax.axis_index(axis)
+    if chunk is None:
+        width = x.shape[1] // n
+        chunk = lambda c: lax.dynamic_slice_in_dim(x, (c % n) * width, width, 1)
     up, down = n // 2, n - 1 - n // 2
     cw, ccw = chunk(i + up), chunk(i - down)
     for s in range(1, up + 1):
@@ -148,8 +147,10 @@
 SHIFTS = {2: (1,), 4: (2, 1, -1)}
 
 
-def ring_allreduce(x, phases):
-    for axis, n in phases:
+def ring_allreduce(make_chunk, phases):
+    axis, n = phases[0]
+    x = half_ring_rs(None, axis, n, lambda c: make_chunk(c % n, n))
+    for axis, n in phases[1:]:
         x = direct_rs(x, axis, n) if n in SHIFTS else half_ring_rs(x, axis, n)
     for axis, n in reversed(phases):
         x = direct_ag(x, axis, n) if n in SHIFTS else half_ring_ag(x, axis, n)
@@ -164,9 +165,13 @@
     onehot = (orbital_blocks[:, :, None] == owned_blocks[None, None, :]).astype(jnp.float32)
     change = jnp.einsum("ksb,kst->kbt", onehot, row_values, precision=HI).reshape(MOVES, row_count)
     picked = jnp.take(inverse_rows, moved, axis=1)
-    local_weights = jnp.dot(change, inverse_rows, precision=HI)
-    full_weights = ring_allreduce(local_weights, PHASES)
-    electrons = full_weights.shape[1]
+    electrons = inverse_rows.shape[1]
+
+    def local_chunk(c, n):
+        width = electrons // n
+        return jnp.dot(change, lax.dynamic_slice_in_dim(inverse_rows, c * width, width, 1), precision=HI)
+
+    full_weights = ring_allreduce(local_chunk, PHASES)
     pick = (lax.broadcasted_iota(jnp.int32, (electrons, MOVES), 0) == moved[None, :]).astype(jnp.float32)
     intersection = jnp.dot(full_weights, pick, precision=HI)
     coupling, ratios = border(intersection, accepted)

time: 129 us -> 129 us (level)
  waiting for transfers between devices: 52.3 us -> 46 us
  matrix products: 11.1 us -> 14.8 us
    ppermute x4, waiting for transfers between devices: 24.8 us -> 19.7 us  [half_ring_rs(): cw = lax.ppermute(cw, axis, shift_perm(n, 1))]
    ppermute x4, starting transfers between devices: 4.34 us -> 0.17 us  [half_ring_ag(): cw = lax.ppermute(cw, axis, shift_perm(n, 1))]
    ppermute x3, starting transfers between devices: 5.6 us -> 9.74 us  [half_ring_ag(): ccw = lax.ppermute(ccw, axis, shift_perm(n, -1))]
    dot_general x1 -> x8, matrix products: 3.48 us -> 7.15 us  [local_chunk(): jnp.dot(change, lax.dynamic_slice_in_dim(inverse_rows, c * width, width,...]
    ppermute x3, starting transfers between devices: 7.97 us -> 10.9 us  [half_ring_rs(): ccw = lax.ppermute(ccw, axis, shift_perm(n, -1))]
    ppermute x4, starting transfers between devices: 2.17 us -> 0.46 us  [half_ring_rs(): cw = lax.ppermute(cw, axis, shift_perm(n, 1))]
    unnamed x15 -> x13, local copies, waits for them, and re-layouts: 4.21 us -> 4.1 us
  transfers between devices with their start and end apart: 26 -> 26, of which waited for: 16 -> 15; matrix products, arithmetic and copies ran while one was open for 6% -> 11% of each run, Pallas kernels for 0% -> 0%
where the time goes in v7:
time: 129 us; the launch traced here: 128 us
  waiting for transfers between devices  46 us (36%)
  starting transfers between devices  43.7 us (34%)
  matrix products  14.8 us (11%)
  local copies, waits for them, and re-layouts  9.81 us (8%)
  Pallas kernels  8.64 us (7%)
  other arithmetic  3.6 us (3%)
    ppermute x4, waiting for transfers between devices, half_ring_rs(): cw = lax.ppermute(cw, axis, shift_perm(n, 1))  19.7 us
    ppermute x4, waiting for transfers between devices, half_ring_ag(): cw = lax.ppermute(cw, axis, shift_perm(n, 1))  16.4 us
    ppermute x6, starting transfers between devices, direct_rs(): total = total + lax.ppermute(chunk(i + d), axis, shift_perm(n, d))  12.9 us
    ppermute x3, starting transfers between devices, half_ring_rs(): ccw = lax.ppermute(ccw, axis, shift_perm(n, -1))  10.9 us
    ppermute x3, starting transfers between devices, half_ring_ag(): ccw = lax.ppermute(ccw, axis, shift_perm(n, -1))  9.74 us
    ppermute x6, starting transfers between devices, direct_ag(): got = lax.ppermute(x, axis, shift_perm(n, d))  9.57 us
    pallas_call x1, Pallas kernels, border(): pl.pallas_call(_border_kernel, out_shape=(jax.ShapeDtypeStruct((n, n), jn...  8.64 us
    dot_general x8, matrix products, local_chunk(): jnp.dot(change, lax.dynamic_slice_in_dim(inverse_rows, c * width, width,...  7.15 us
  transfers between devices with their start and end apart: 26, of which 15 were waited for; matrix products, arithmetic and copies ran while one was open for 11% of the time, Pallas kernels for 0%

profile of v7, /device:TPU:0, one launch (start us, length us, event | category | flops | bytes accessed | tf_op | source)
XLA Modules:
  0.0 127.7 jit_solution(7088574385083116942)
XLA Ops:
  0.7 0.8 compare_bitcast_fusion
  2.0 1.3 %fusion.12 = f32[64,1024]{1,0:T(8,128)S(1)} fusion(f32[64,64]{1,0:T(8,128)S(1)} %bitcast.22, f32[64,8192]{1,0:T(8,128)} %param.5, s32[]{:T(128)S(6)} %select_n.189), kind=kOutput, calls=%fused_computation.18 | convolution fusion | flops 50331648 | bytes 540676 | tf_op jit(solution)/shard_map/dot_general | solution.py:172
  3.6 1.3 %fusion.5 = f32[64,1024]{1,0:T(8,128)S(1)} fusion(f32[64,64]{1,0:T(8,128)S(1)} %bitcast.23, f32[64,8192]{1,0:T(8,128)} %param.5, s32[]{:T(128)S(6)} %select_n.197), kind=kOutput, calls=%fused_computation.10 | convolution fusion | flops 50331648 | bytes 540676 | tf_op jit(solution)/shard_map/dot_general | solution.py:172
  5.0 4.1 %collective-permute-start.4 = (f32[64,1024]{1,0:T(8,128)S(1)}, f32[64,1024]{1,0:T(8,128)S(1)}, u32[]{:S(2)}, u32[]{:S(2)}) collective-permute-start(f32[64,1024]{1,0:T(8,128)S(1)} %fusion.5), channel_id=1, source_target_pairs={{0,28},{4,0},{8,4},{12,8},{16,12},{20,16},{24,20},{28,24},{1,29},{... | collective-permute-start | bytes 786440 | tf_op jit(solution)/shard_map/ppermute | solution.py:99
  9.0 4.9 %collective-permute-done = f32[64,1024]{1,0:T(8,128)S(1)} collective-permute-done((f32[64,1024]{1,0:T(8,128)S(1)}, f32[64,1024]{1,0:T(8,128)S(1)}, u32[]{:S(2)}, u32[]{:S(2)}) %collective-permute-start) | collective-permute-done | bytes 262176 | tf_op jit(solution)/shard_map/ppermute | solution.py:97
  13.9 2.0 %convolution_add_fusion.1 = f32[64,1024]{1,0:T(8,128)} fusion(f32[64,1024]{1,0:T(8,128)S(1)} %collective-permute-done, f32[64,64]{1,0:T(8,128)S(1)} %bitcast.24, f32[64,8192]{1,0:T(8,128)} %param.5, s32[]{:T(128)S(6)} %select_n.191), kind=kOutput, calls=%fused_computation.5 | convolution fusion | flops 50397184 | bytes 802820 | tf_op jit(solution)/shard_map/dot_general | solution.py:172
  16.3 1.1 convolution_add_fusion
  17.4 3.2 %collective-permute-start.5 = (f32[64,1024]{1,0:T(8,128)}, f32[64,1024]{1,0:T(8,128)S(1)}, u32[]{:S(2)}, u32[]{:S(2)}) collective-permute-start(f32[64,1024]{1,0:T(8,128)} %convolution_add_fusion), channel_id=1, source_target_pairs={{0,28},{4,0},{8,4},{12,8},{16,12},{20,16},{24,20},{28,24},{1,29},{... | collective-permute-start | bytes 786440 | tf_op jit(solution)/shard_map/ppermute | solution.py:99
  20.6 4.2 %collective-permute-done.1 = f32[64,1024]{1,0:T(8,128)S(1)} collective-permute-done((f32[64,1024]{1,0:T(8,128)}, f32[64,1024]{1,0:T(8,128)S(1)}, u32[]{:S(2)}, u32[]{:S(2)}) %collective-permute-start.1) | collective-permute-done | bytes 262176 | tf_op jit(solution)/shard_map/ppermute | solution.py:97
  25.7 3.6 %collective-permute-start.6 = (f32[64,1024]{1,0:T(8,128)S(1)}, f32[64,1024]{1,0:T(8,128)S(1)}, u32[]{:S(2)}, u32[]{:S(2)}) collective-permute-start(f32[64,1024]{1,0:T(8,128)S(1)} %add.281), channel_id=1, source_target_pairs={{0,28},{4,0},{8,4},{12,8},{16,12},{20,16},{24,20},{28,24},{1,29},{... | collective-permute-start | bytes 786440 | tf_op jit(solution)/shard_map/ppermute | solution.py:99
  29.3 3.5 %collective-permute-done.2 = f32[64,1024]{1,0:T(8,128)} collective-permute-done((f32[64,1024]{1,0:T(8,128)S(1)}, f32[64,1024]{1,0:T(8,128)}, u32[]{:S(2)}, u32[]{:S(2)}) %collective-permute-start.2) | collective-permute-done | bytes 262176 | tf_op jit(solution)/shard_map/ppermute | solution.py:97
  32.8 1.0 add.270
  34.3 7.2 %collective-permute-done.3 = f32[64,1024]{1,0:T(8,128)} collective-permute-done((f32[64,1024]{1,0:T(8,128)S(1)}, f32[64,1024]{1,0:T(8,128)}, u32[]{:S(2)}, u32[]{:S(2)}) %collective-permute-start.3) | collective-permute-done | bytes 262176 | tf_op jit(solution)/shard_map/ppermute | solution.py:97
  41.5 1.0 add_add_fusion
  42.6 3.3 %collective-permute-start.7 = (f32[64,256]{1,0:T(8,128)S(1)}, f32[64,256]{1,0:T(8,128)S(1)}, u32[]{:S(2)}, u32[]{:S(2)}) collective-permute-start(f32[64,256]{1,0:T(8,128)S(1)} %get-tuple-element.6), channel_id=1, source_target_pairs={{0,2},{1,3},{2,0},{3,1},{4,6},{5,7},{6,4},{7,5},{8,10},{9,11},{10,... | collective-permute-start | bytes 196616 | tf_op jit(solution)/shard_map/ppermute | solution.py:132
  45.9 0.7 collective-permute-start.8
  46.6 2.6 %collective-permute-start.9 = (f32[64,256]{1,0:T(8,128)S(1)}, f32[64,256]{1,0:T(8,128)S(1)}, u32[]{:S(2)}, u32[]{:S(2)}) collective-permute-start(f32[64,256]{1,0:T(8,128)S(1)} %get-tuple-element.7), channel_id=1, source_target_pairs={{0,3},{1,0},{2,1},{3,2},{4,7},{5,4},{6,5},{7,6},{8,11},{9,8},{10,9... | collective-permute-start | bytes 196616 | tf_op jit(solution)/shard_map/ppermute | solution.py:132
  49.1 2.2 %collective-permute-done.8 = f32[64,256]{1,0:T(8,128)S(1)} collective-permute-done((f32[64,256]{1,0:T(8,128)S(1)}, f32[64,256]{1,0:T(8,128)S(1)}, u32[]{:S(2)}, u32[]{:S(2)}) %collective-permute-start.8) | collective-permute-done | bytes 65568 | tf_op jit(solution)/shard_map/ppermute | solution.py:132
  51.5 3.1 %collective-permute-start.10 = (f32[64,64]{1,0:T(8,128)S(1)}, f32[64,64]{1,0:T(8,128)S(1)}, u32[]{:S(2)}, u32[]{:S(2)}) collective-permute-start(f32[64,64]{1,0:T(8,128)S(1)} %get-tuple-element.9), channel_id=1, source_target_pairs={{0,64},{32,96},{64,0},{96,32},{1,65},{33,97},{65,1},{97,33},{2,66}... | collective-permute-start | bytes 49160 | tf_op jit(solution)/shard_map/ppermute | solution.py:132
  54.6 0.6 collective-permute-start.11
  55.2 2.6 %collective-permute-start.12 = (f32[64,64]{1,0:T(8,128)S(1)}, f32[64,64]{1,0:T(8,128)S(1)}, u32[]{:S(2)}, u32[]{:S(2)}) collective-permute-start(f32[64,64]{1,0:T(8,128)S(1)} %get-tuple-element.10), channel_id=1, source_target_pairs={{0,96},{32,0},{64,32},{96,64},{1,97},{33,1},{65,33},{97,65},{2,98}... | collective-permute-start | bytes 49160 | tf_op jit(solution)/shard_map/ppermute | solution.py:132
  57.8 1.9 %collective-permute-done.11 = f32[64,64]{1,0:T(8,128)S(1)} collective-permute-done((f32[64,64]{1,0:T(8,128)S(1)}, f32[64,64]{1,0:T(8,128)S(1)}, u32[]{:S(2)}, u32[]{:S(2)}) %collective-permute-start.11) | collective-permute-done | bytes 16416 | tf_op jit(solution)/shard_map/ppermute | solution.py:132
  59.8 1.5 %collective-permute-start.13 = (f32[64,64]{1,0:T(8,128)S(1)}, f32[64,64]{1,0:T(8,128)S(1)}, u32[]{:S(2)}, u32[]{:S(2)}) collective-permute-start(f32[64,64]{1,0:T(8,128)S(1)} %add_add_fusion.2), channel_id=1, source_target_pairs={{0,64},{32,96},{64,0},{96,32},{1,65},{33,97},{65,1},{97,33},{2,66}... | collective-permute-start | bytes 49160 | tf_op jit(solution)/shard_map/ppermute | solution.py:142
  61.4 2.6 %collective-permute-start.14 = (f32[64,64]{1,0:T(8,128)S(1)}, f32[64,64]{1,0:T(8,128)S(1)}, u32[]{:S(2)}, u32[]{:S(2)}) collective-permute-start(f32[64,64]{1,0:T(8,128)S(1)} %add_add_fusion.2), channel_id=1, source_target_pairs={{0,32},{32,64},{64,96},{96,0},{1,33},{33,65},{65,97},{97,1},{2,34}... | collective-permute-start | bytes 49160 | tf_op jit(solution)/shard_map/ppermute | solution.py:142
  64.0 0.6 collective-permute-start.15
  65.6 0.9 collective-permute-done.14
  66.9 1.0 collective-permute-done.15
  68.5 1.5 %collective-permute-start.16 = (f32[64,256]{1,0:T(8,128)S(1)}, f32[64,256]{1,0:T(8,128)S(1)}, u32[]{:S(2)}, u32[]{:S(2)}) collective-permute-start(f32[64,256]{1,0:T(8,128)S(1)} %dynamic_update_slice.51), channel_id=1, source_target_pairs={{0,2},{1,3},{2,0},{3,1},{4,6},{5,7},{6,4},{7,5},{8,10},{9,11},{10,... | collective-permute-start | bytes 196616 | tf_op jit(solution)/shard_map/ppermute | solution.py:142
  70.0 2.6 %collective-permute-start.17 = (f32[64,256]{1,0:T(8,128)S(1)}, f32[64,256]{1,0:T(8,128)S(1)}, u32[]{:S(2)}, u32[]{:S(2)}) collective-permute-start(f32[64,256]{1,0:T(8,128)S(1)} %dynamic_update_slice.51), channel_id=1, source_target_pairs={{0,1},{1,2},{2,3},{3,0},{4,5},{5,6},{6,7},{7,4},{8,9},{9,10},{10,1... | collective-permute-start | bytes 196616 | tf_op jit(solution)/shard_map/ppermute | solution.py:142
  72.6 0.6 collective-permute-start.18
  73.3 1.0 collective-permute-done.16
  74.3 1.2 collective-permute-done.17
  75.5 1.4 %collective-permute-done.18 = f32[64,256]{1,0:T(8,128)S(1)} collective-permute-done((f32[64,256]{1,0:T(8,128)S(1)}, f32[64,256]{1,0:T(8,128)S(1)}, u32[]{:S(2)}, u32[]{:S(2)}) %collective-permute-start.18) | collective-permute-done | bytes 65568 | tf_op jit(solution)/shard_map/ppermute | solution.py:142
  77.0 3.2 %collective-permute-start.20 = (f32[64,1024]{1,0:T(8,128)S(1)}, f32[64,1024]{1,0:T(8,128)S(1)}, u32[]{:S(2)}, u32[]{:S(2)}) collective-permute-start(f32[64,1024]{1,0:T(8,128)S(1)} %constant_dynamic-update-slice_fusion.8), channel_id=1, source_target_pairs={{0,28},{4,0},{8,4},{12,8},{16,12},{20,16},{24,20},{28,24},{1,29},{... | collective-permute-start | bytes 786440 | tf_op jit(solution)/shard_map/ppermute | solution.py:122
  80.2 2.7 %copy.9 = f32[64,8192]{0,1:T(8,128)} copy(f32[64,8192]{1,0:T(8,128)S(1)} %copy-done.1) | data formatting | bytes 4194304 | tf_op args[0]
  83.0 2.8 %gather_fusion = f32[64,64]{1,0:T(8,128)S(1)} fusion(f32[64,8192]{0,1:T(8,128)} %copy.9, s32[1024]{0:T(1024)S(1)} %pad_clamp_fusion), kind=kCustom, calls=%fused_computation | custom fusion | bytes 33024 | tf_op jit(solution)/shard_map/jit(_take)/gather | solution.py:167
  85.9 0.6 convert_bitcast_fusion.acc_ref
  86.5 3.2 %collective-permute-start.22 = (f32[64,1024]{1,0:T(8,128)S(1)}, f32[64,1024]{1,0:T(8,128)S(1)}, u32[]{:S(2)}, u32[]{:S(2)}) collective-permute-start(f32[64,1024]{1,0:T(8,128)S(1)} %collective-permute-done.20), channel_id=1, source_target_pairs={{0,28},{4,0},{8,4},{12,8},{16,12},{20,16},{24,20},{28,24},{1,29},{... | collective-permute-start | bytes 786440 | tf_op jit(solution)/shard_map/ppermute | solution.py:122
  89.8 4.7 %collective-permute-done.21 = f32[64,1024]{1,0:T(8,128)S(1)} collective-permute-done((f32[64,1024]{1,0:T(8,128)S(1)}, f32[64,1024]{1,0:T(8,128)S(1)}, u32[]{:S(2)}, u32[]{:S(2)}) %collective-permute-start.21) | collective-permute-done | bytes 262176 | tf_op jit(solution)/shard_map/ppermute | solution.py:119
  94.6 3.3 %collective-permute-start.24 = (f32[64,1024]{1,0:T(8,128)S(1)}, f32[64,1024]{1,0:T(8,128)S(1)}, u32[]{:S(2)}, u32[]{:S(2)}) collective-permute-start(f32[64,1024]{1,0:T(8,128)S(1)} %collective-permute-done.22), channel_id=1, source_target_pairs={{0,28},{4,0},{8,4},{12,8},{16,12},{20,16},{24,20},{28,24},{1,29},{... | collective-permute-start | bytes 786440 | tf_op jit(solution)/shard_map/ppermute | solution.py:122
  98.0 4.2 %collective-permute-done.23 = f32[64,1024]{1,0:T(8,128)S(1)} collective-permute-done((f32[64,1024]{1,0:T(8,128)S(1)}, f32[64,1024]{1,0:T(8,128)S(1)}, u32[]{:S(2)}, u32[]{:S(2)}) %collective-permute-start.23) | collective-permute-done | bytes 262176 | tf_op jit(solution)/shard_map/ppermute | solution.py:119
  102.2 7.5 %collective-permute-done.25 = f32[64,1024]{1,0:T(8,128)S(1)} collective-permute-done((f32[64,1024]{1,0:T(8,128)S(1)}, f32[64,1024]{1,0:T(8,128)S(1)}, u32[]{:S(2)}, u32[]{:S(2)}) %collective-permute-start.25) | collective-permute-done | bytes 262176 | tf_op jit(solution)/shard_map/ppermute | solution.py:119
  109.8 1.3 %copy-done.2 = f32[64,8192]{1,0:T(8,128)} copy-done((f32[64,8192]{1,0:T(8,128)}, f32[64,8192]{1,0:T(8,128)S(1)}, u32[]{:S(2)}) %copy-start.2) | copy-done | bytes 2097176
  111.1 1.4 %fusion.m_ref = f32[64,64]{1,0:T(8,128)S(1)} fusion(f32[64,8192]{1,0:T(8,128)S(1)} %constant_dynamic-update-slice_fusion, s32[64]{0:T(128)S(1)} %copy-done.4), kind=kOutput, calls=%fused_computation.3 | convolution fusion | flops 403177472 | bytes 2113792 | tf_op jit(solution)/shard_map/dot_general | solution.py:176
  112.5 0.7 copy.10
  113.2 8.6 %shard_map.68 = (f32[64,64]{1,0:T(8,128)}, f32[1,64]{1,0:T(1,128)}) custom-call(f32[64,64]{1,0:T(8,128)} %copy-done.3, f32[64,64]{1,0:T(8,128)} %bitcast.30, f32[1,64]{1,0:T(1,128)} %convert_bitcast_fusion.acc_ref), custom_call_target="tpu_custom_call" | custom-call | tf_op jit(solution)/shard_map/pallas_call | solution.py:76
  121.9 1.1 fusion.16
  122.9 4.8 %convolution_subtract_fusion = f32[64,8192]{1,0:T(8,128)} fusion(f32[64,8192]{1,0:T(8,128)S(1)} %copy-done.1, f32[64,64]{1,0:T(8,128)S(1)} %fusion.16, f32[64,8192]{1,0:T(8,128)} %copy-done.2), kind=kOutput, calls=%fused_computation.1 | convolution fusion | flops 403177472 | bytes 6307840 | tf_op jit(solution)/shard_map/dot_general | solution.py:179
  (65 shorter events, 5.1 us)
Async XLA Ops:
  0.6 1.0 copy-start
  0.6 15.2 %copy-start.1 = (f32[64,8192]{1,0:T(8,128)S(1)}, f32[64,8192]{1,0:T(8,128)}, u32[]{:S(2)}) copy-start(f32[64,8192]{1,0:T(8,128)} %param.5) | copy-start | bytes 6291460
  3.4 10.5 %collective-permute-start = (f32[64,1024]{1,0:T(8,128)S(1)}, f32[64,1024]{1,0:T(8,128)S(1)}, u32[]{:S(2)}, u32[]{:S(2)}) collective-permute-start(f32[64,1024]{1,0:T(8,128)S(1)} %fusion.12), channel_id=1, source_target_pairs={{0,4},{4,8},{8,12},{12,16},{16,20},{20,24},{24,28},{28,0},{1,5},{5... | collective-permute-start | bytes 786440 | tf_op jit(solution)/shard_map/ppermute | solution.py:97
  5.0 11.3 %collective-permute-start.4 = (f32[64,1024]{1,0:T(8,128)S(1)}, f32[64,1024]{1,0:T(8,128)S(1)}, u32[]{:S(2)}, u32[]{:S(2)}) collective-permute-start(f32[64,1024]{1,0:T(8,128)S(1)} %fusion.5), channel_id=1, source_target_pairs={{0,28},{4,0},{8,4},{12,8},{16,12},{20,16},{24,20},{28,24},{1,29},{... | collective-permute-start | bytes 786440 | tf_op jit(solution)/shard_map/ppermute | solution.py:99
  15.9 8.9 %collective-permute-start.1 = (f32[64,1024]{1,0:T(8,128)}, f32[64,1024]{1,0:T(8,128)S(1)}, u32[]{:S(2)}, u32[]{:S(2)}) collective-permute-start(f32[64,1024]{1,0:T(8,128)} %convolution_add_fusion.1), channel_id=1, source_target_pairs={{0,4},{4,8},{8,12},{12,16},{16,20},{20,24},{24,28},{28,0},{1,5},{5... | collective-permute-start | bytes 786440 | tf_op jit(solution)/shard_map/ppermute | solution.py:97
  17.4 8.3 %collective-permute-start.5 = (f32[64,1024]{1,0:T(8,128)}, f32[64,1024]{1,0:T(8,128)S(1)}, u32[]{:S(2)}, u32[]{:S(2)}) collective-permute-start(f32[64,1024]{1,0:T(8,128)} %convolution_add_fusion), channel_id=1, source_target_pairs={{0,28},{4,0},{8,4},{12,8},{16,12},{20,16},{24,20},{28,24},{1,29},{... | collective-permute-start | bytes 786440 | tf_op jit(solution)/shard_map/ppermute | solution.py:99
  24.8 8.0 %collective-permute-start.2 = (f32[64,1024]{1,0:T(8,128)S(1)}, f32[64,1024]{1,0:T(8,128)}, u32[]{:S(2)}, u32[]{:S(2)}) collective-permute-start(f32[64,1024]{1,0:T(8,128)S(1)} %add.267), channel_id=1, source_target_pairs={{0,4},{4,8},{8,12},{12,16},{16,20},{20,24},{24,28},{28,0},{1,5},{5... | collective-permute-start | bytes 786440 | tf_op jit(solution)/shard_map/ppermute | solution.py:97
  25.7 39.0 %copy-start.4 = (s32[64]{0:T(128)S(1)}, s32[64]{0:T(128)}, u32[]{:S(2)}) copy-start(s32[64]{0:T(128)} %param.8) | copy-start | bytes 772
  25.7 8.6 %collective-permute-start.6 = (f32[64,1024]{1,0:T(8,128)S(1)}, f32[64,1024]{1,0:T(8,128)S(1)}, u32[]{:S(2)}, u32[]{:S(2)}) collective-permute-start(f32[64,1024]{1,0:T(8,128)S(1)} %add.281), channel_id=1, source_target_pairs={{0,28},{4,0},{8,4},{12,8},{16,12},{20,16},{24,20},{28,24},{1,29},{... | collective-permute-start | bytes 786440 | tf_op jit(solution)/shard_map/ppermute | solution.py:99
  33.8 7.8 %collective-permute-start.3 = (f32[64,1024]{1,0:T(8,128)S(1)}, f32[64,1024]{1,0:T(8,128)}, u32[]{:S(2)}, u32[]{:S(2)}) collective-permute-start(f32[64,1024]{1,0:T(8,128)S(1)} %add.270), channel_id=1, source_target_pairs={{0,4},{4,8},{8,12},{12,16},{16,20},{20,24},{24,28},{28,0},{1,5},{5... | collective-permute-start | bytes 786440 | tf_op jit(solution)/shard_map/ppermute | solution.py:97
  42.6 6.5 %collective-permute-start.7 = (f32[64,256]{1,0:T(8,128)S(1)}, f32[64,256]{1,0:T(8,128)S(1)}, u32[]{:S(2)}, u32[]{:S(2)}) collective-permute-start(f32[64,256]{1,0:T(8,128)S(1)} %get-tuple-element.6), channel_id=1, source_target_pairs={{0,2},{1,3},{2,0},{3,1},{4,6},{5,7},{6,4},{7,5},{8,10},{9,11},{10,... | collective-permute-start | bytes 196616 | tf_op jit(solution)/shard_map/ppermute | solution.py:132
  45.9 5.5 %collective-permute-start.8 = (f32[64,256]{1,0:T(8,128)S(1)}, f32[64,256]{1,0:T(8,128)S(1)}, u32[]{:S(2)}, u32[]{:S(2)}) collective-permute-start(f32[64,256]{1,0:T(8,128)S(1)} %get-tuple-element.8), channel_id=1, source_target_pairs={{0,1},{1,2},{2,3},{3,0},{4,5},{5,6},{6,7},{7,4},{8,9},{9,10},{10,1... | collective-permute-start | bytes 196616 | tf_op jit(solution)/shard_map/ppermute | solution.py:132
  46.6 4.8 %collective-permute-start.9 = (f32[64,256]{1,0:T(8,128)S(1)}, f32[64,256]{1,0:T(8,128)S(1)}, u32[]{:S(2)}, u32[]{:S(2)}) collective-permute-start(f32[64,256]{1,0:T(8,128)S(1)} %get-tuple-element.7), channel_id=1, source_target_pairs={{0,3},{1,0},{2,1},{3,2},{4,7},{5,4},{6,5},{7,6},{8,11},{9,8},{10,9... | collective-permute-start | bytes 196616 | tf_op jit(solution)/shard_map/ppermute | solution.py:132
  51.5 6.4 %collective-permute-start.10 = (f32[64,64]{1,0:T(8,128)S(1)}, f32[64,64]{1,0:T(8,128)S(1)}, u32[]{:S(2)}, u32[]{:S(2)}) collective-permute-start(f32[64,64]{1,0:T(8,128)S(1)} %get-tuple-element.9), channel_id=1, source_target_pairs={{0,64},{32,96},{64,0},{96,32},{1,65},{33,97},{65,1},{97,33},{2,66}... | collective-permute-start | bytes 49160 | tf_op jit(solution)/shard_map/ppermute | solution.py:132
  54.6 5.1 %collective-permute-start.11 = (f32[64,64]{1,0:T(8,128)S(1)}, f32[64,64]{1,0:T(8,128)S(1)}, u32[]{:S(2)}, u32[]{:S(2)}) collective-permute-start(f32[64,64]{1,0:T(8,128)S(1)} %get-tuple-element.11), channel_id=1, source_target_pairs={{0,32},{32,64},{64,96},{96,0},{1,33},{33,65},{65,97},{97,1},{2,34}... | collective-permute-start | bytes 49160 | tf_op jit(solution)/shard_map/ppermute | solution.py:132
  55.2 4.5 %collective-permute-start.12 = (f32[64,64]{1,0:T(8,128)S(1)}, f32[64,64]{1,0:T(8,128)S(1)}, u32[]{:S(2)}, u32[]{:S(2)}) collective-permute-start(f32[64,64]{1,0:T(8,128)S(1)} %get-tuple-element.10), channel_id=1, source_target_pairs={{0,96},{32,0},{64,32},{96,64},{1,97},{33,1},{65,33},{97,65},{2,98}... | collective-permute-start | bytes 49160 | tf_op jit(solution)/shard_map/ppermute | solution.py:132
  59.8 5.5 %collective-permute-start.13 = (f32[64,64]{1,0:T(8,128)S(1)}, f32[64,64]{1,0:T(8,128)S(1)}, u32[]{:S(2)}, u32[]{:S(2)}) collective-permute-start(f32[64,64]{1,0:T(8,128)S(1)} %add_add_fusion.2), channel_id=1, source_target_pairs={{0,64},{32,96},{64,0},{96,32},{1,65},{33,97},{65,1},{97,33},{2,66}... | collective-permute-start | bytes 49160 | tf_op jit(solution)/shard_map/ppermute | solution.py:142
  61.4 5.1 %collective-permute-start.14 = (f32[64,64]{1,0:T(8,128)S(1)}, f32[64,64]{1,0:T(8,128)S(1)}, u32[]{:S(2)}, u32[]{:S(2)}) collective-permute-start(f32[64,64]{1,0:T(8,128)S(1)} %add_add_fusion.2), channel_id=1, source_target_pairs={{0,32},{32,64},{64,96},{96,0},{1,33},{33,65},{65,97},{97,1},{2,34}... | collective-permute-start | bytes 49160 | tf_op jit(solution)/shard_map/ppermute | solution.py:142
  64.0 3.9 %collective-permute-start.15 = (f32[64,64]{1,0:T(8,128)S(1)}, f32[64,64]{1,0:T(8,128)S(1)}, u32[]{:S(2)}, u32[]{:S(2)}) collective-permute-start(f32[64,64]{1,0:T(8,128)S(1)} %add_add_fusion.2), channel_id=1, source_target_pairs={{0,96},{32,0},{64,32},{96,64},{1,97},{33,1},{65,33},{97,65},{2,98}... | collective-permute-start | bytes 49160 | tf_op jit(solution)/shard_map/ppermute | solution.py:142
  68.5 5.9 %collective-permute-start.16 = (f32[64,256]{1,0:T(8,128)S(1)}, f32[64,256]{1,0:T(8,128)S(1)}, u32[]{:S(2)}, u32[]{:S(2)}) collective-permute-start(f32[64,256]{1,0:T(8,128)S(1)} %dynamic_update_slice.51), channel_id=1, source_target_pairs={{0,2},{1,3},{2,0},{3,1},{4,6},{5,7},{6,4},{7,5},{8,10},{9,11},{10,... | collective-permute-start | bytes 196616 | tf_op jit(solution)/shard_map/ppermute | solution.py:142
  70.0 5.5 %collective-permute-start.17 = (f32[64,256]{1,0:T(8,128)S(1)}, f32[64,256]{1,0:T(8,128)S(1)}, u32[]{:S(2)}, u32[]{:S(2)}) collective-permute-start(f32[64,256]{1,0:T(8,128)S(1)} %dynamic_update_slice.51), channel_id=1, source_target_pairs={{0,1},{1,2},{2,3},{3,0},{4,5},{5,6},{6,7},{7,4},{8,9},{9,10},{10,1... | collective-permute-start | bytes 196616 | tf_op jit(solution)/shard_map/ppermute | solution.py:142
  72.6 4.3 %collective-permute-start.18 = (f32[64,256]{1,0:T(8,128)S(1)}, f32[64,256]{1,0:T(8,128)S(1)}, u32[]{:S(2)}, u32[]{:S(2)}) collective-permute-start(f32[64,256]{1,0:T(8,128)S(1)} %dynamic_update_slice.51), channel_id=1, source_target_pairs={{0,3},{1,0},{2,1},{3,2},{4,7},{5,4},{6,5},{7,6},{8,11},{9,8},{10,9... | collective-permute-start | bytes 196616 | tf_op jit(solution)/shard_map/ppermute | solution.py:142
  76.9 8.8 %collective-permute-start.19 = (f32[64,1024]{1,0:T(8,128)S(1)}, f32[64,1024]{1,0:T(8,128)S(1)}, u32[]{:S(2)}, u32[]{:S(2)}) collective-permute-start(f32[64,1024]{1,0:T(8,128)S(1)} %constant_dynamic-update-slice_fusion.8), channel_id=1, source_target_pairs={{0,4},{4,8},{8,12},{12,16},{16,20},{20,24},{24,28},{28,0},{1,5},{5... | collective-permute-start | bytes 786440 | tf_op jit(solution)/shard_map/ppermute | solution.py:119
  77.0 9.4 %collective-permute-start.20 = (f32[64,1024]{1,0:T(8,128)S(1)}, f32[64,1024]{1,0:T(8,128)S(1)}, u32[]{:S(2)}, u32[]{:S(2)}) collective-permute-start(f32[64,1024]{1,0:T(8,128)S(1)} %constant_dynamic-update-slice_fusion.8), channel_id=1, source_target_pairs={{0,28},{4,0},{8,4},{12,8},{16,12},{20,16},{24,20},{28,24},{1,29},{... | collective-permute-start | bytes 786440 | tf_op jit(solution)/shard_map/ppermute | solution.py:122
  80.2 5.6 %copy-start.5 = (s32[64]{0:T(128)S(1)}, s32[64]{0:T(128)}, u32[]{:S(2)}) copy-start(s32[64]{0:T(128)} %param.9) | copy-start | bytes 772
  85.8 8.8 %collective-permute-start.21 = (f32[64,1024]{1,0:T(8,128)S(1)}, f32[64,1024]{1,0:T(8,128)S(1)}, u32[]{:S(2)}, u32[]{:S(2)}) collective-permute-start(f32[64,1024]{1,0:T(8,128)S(1)} %collective-permute-done.19), channel_id=1, source_target_pairs={{0,4},{4,8},{8,12},{12,16},{16,20},{20,24},{24,28},{28,0},{1,5},{5... | collective-permute-start | bytes 786440 | tf_op jit(solution)/shard_map/ppermute | solution.py:119
  86.5 8.2 %collective-permute-start.22 = (f32[64,1024]{1,0:T(8,128)S(1)}, f32[64,1024]{1,0:T(8,128)S(1)}, u32[]{:S(2)}, u32[]{:S(2)}) collective-permute-start(f32[64,1024]{1,0:T(8,128)S(1)} %collective-permute-done.20), channel_id=1, source_target_pairs={{0,28},{4,0},{8,4},{12,8},{16,12},{20,16},{24,20},{28,24},{1,29},{... | collective-permute-start | bytes 786440 | tf_op jit(solution)/shard_map/ppermute | solution.py:122
  94.6 7.6 %collective-permute-start.23 = (f32[64,1024]{1,0:T(8,128)S(1)}, f32[64,1024]{1,0:T(8,128)S(1)}, u32[]{:S(2)}, u32[]{:S(2)}) collective-permute-start(f32[64,1024]{1,0:T(8,128)S(1)} %collective-permute-done.21), channel_id=1, source_target_pairs={{0,4},{4,8},{8,12},{12,16},{16,20},{20,24},{24,28},{28,0},{1,5},{5... | collective-permute-start | bytes 786440 | tf_op jit(solution)/shard_map/ppermute | solution.py:119
  94.6 7.6 %collective-permute-start.24 = (f32[64,1024]{1,0:T(8,128)S(1)}, f32[64,1024]{1,0:T(8,128)S(1)}, u32[]{:S(2)}, u32[]{:S(2)}) collective-permute-start(f32[64,1024]{1,0:T(8,128)S(1)} %collective-permute-done.22), channel_id=1, source_target_pairs={{0,28},{4,0},{8,4},{12,8},{16,12},{20,16},{24,20},{28,24},{1,29},{... | collective-permute-start | bytes 786440 | tf_op jit(solution)/shard_map/ppermute | solution.py:122
  102.1 7.6 %collective-permute-start.25 = (f32[64,1024]{1,0:T(8,128)S(1)}, f32[64,1024]{1,0:T(8,128)S(1)}, u32[]{:S(2)}, u32[]{:S(2)}) collective-permute-start(f32[64,1024]{1,0:T(8,128)S(1)} %collective-permute-done.23), channel_id=1, source_target_pairs={{0,4},{4,8},{8,12},{12,16},{16,20},{20,24},{24,28},{28,0},{1,5},{5... | collective-permute-start | bytes 786440 | tf_op jit(solution)/shard_map/ppermute | solution.py:119
  109.8 1.4 %copy-start.2 = (f32[64,8192]{1,0:T(8,128)}, f32[64,8192]{1,0:T(8,128)S(1)}, u32[]{:S(2)}) copy-start(f32[64,8192]{1,0:T(8,128)S(1)} %constant_dynamic-update-slice_fusion) | copy-start | bytes 6291460
  112.5 0.7 copy-start.3

commit v8 on v7

--- a/solution.py
+++ b/solution.py
@@ -93,6 +93,9 @@
         chunk = lambda c: lax.dynamic_slice_in_dim(x, (c % n) * width, width, 1)
     up, down = n // 2, n - 1 - n // 2
     cw, ccw = chunk(i + up), chunk(i - down)
+    if x is not None:
+        width = x.shape[1] // n
+        chunk = lambda c: lax.dynamic_slice_in_dim(x, (c % n) * width, width, 1)
     for s in range(1, up + 1):
         cw = lax.ppermute(cw, axis, shift_perm(n, 1))
         if s <= down:
@@ -149,7 +152,7 @@
 
 def ring_allreduce(make_chunk, phases):
     axis, n = phases[0]
-    x = half_ring_rs(None, axis, n, lambda c: make_chunk(c % n, n))
+    x = half_ring_rs(make_chunk(None, n), axis, n, lambda c: make_chunk(c % n, n))
     for axis, n in phases[1:]:
         x = direct_rs(x, axis, n) if n in SHIFTS else half_ring_rs(x, axis, n)
     for axis, n in reversed(phases):
@@ -168,6 +171,8 @@
     electrons = inverse_rows.shape[1]
 
     def local_chunk(c, n):
+        if c is None:
+            return jnp.dot(change, inverse_rows, precision=HI)
         width = electrons // n
         return jnp.dot(change, lax.dynamic_slice_in_dim(inverse_rows, c * width, width, 1), precision=HI)
 

time: 129 us -> 127 us (0.984)
  waiting for transfers between devices: 46 us -> 43.7 us
    ppermute x4, starting transfers between devices: 0.17 us -> 8.18 us  [half_ring_ag(): cw = lax.ppermute(cw, axis, shift_perm(n, 1))]
    ppermute x3, starting transfers between devices: 9.74 us -> 3.11 us  [half_ring_ag(): ccw = lax.ppermute(ccw, axis, shift_perm(n, -1))]
    dot_general x8 -> x2, matrix products: 7.15 us -> 2.63 us  [local_chunk(): jnp.dot(change, lax.dynamic_slice_in_dim(inverse_rows, c * width, width,...]
    dot_general x0 -> x1, matrix products: none -> 3.47 us  [local_chunk(): return jnp.dot(change, inverse_rows, precision=HI)]
    ppermute x4, waiting for transfers between devices: 16.4 us -> 14.3 us  [half_ring_ag(): cw = lax.ppermute(cw, axis, shift_perm(n, 1))]
    unnamed x13 -> x15, local copies, waits for them, and re-layouts: 4.1 us -> 4.2 us
  transfers between devices with their start and end apart: 26 -> 26, of which waited for: 15 -> 16; matrix products, arithmetic and copies ran while one was open for 11% -> 10% of each run, Pallas kernels for 0% -> 0%
where the time goes in v8:
time: 127 us; the launch traced here: 126 us
  starting transfers between devices  44.7 us (35%)
  waiting for transfers between devices  43.7 us (34%)
  matrix products  13.7 us (11%)
  local copies, waits for them, and re-layouts  9.91 us (8%)
  Pallas kernels  8.63 us (7%)
  other arithmetic  4.22 us (3%)
    ppermute x4, waiting for transfers between devices, half_ring_rs(): cw = lax.ppermute(cw, axis, shift_perm(n, 1))  19.2 us
    ppermute x4, waiting for transfers between devices, half_ring_ag(): cw = lax.ppermute(cw, axis, shift_perm(n, 1))  14.3 us
    ppermute x6, starting transfers between devices, direct_rs(): total = total + lax.ppermute(chunk(i + d), axis, shift_perm(n, d))  12.9 us
    ppermute x3, starting transfers between devices, half_ring_rs(): ccw = lax.ppermute(ccw, axis, shift_perm(n, -1))  10.5 us
    ppermute x6, starting transfers between devices, direct_ag(): got = lax.ppermute(x, axis, shift_perm(n, d))  9.57 us
    pallas_call x1, Pallas kernels, border(): pl.pallas_call(_border_kernel, out_shape=(jax.ShapeDtypeStruct((n, n), jn...  8.63 us
    ppermute x4, starting transfers between devices, half_ring_ag(): cw = lax.ppermute(cw, axis, shift_perm(n, 1))  8.18 us
    ppermute x6, waiting for transfers between devices, direct_ag(): got = lax.ppermute(x, axis, shift_perm(n, d))  5.78 us
  transfers between devices with their start and end apart: 26, of which 16 were waited for; matrix products, arithmetic and copies ran while one was open for 10% of the time, Pallas kernels for 0%

profile of v8, /device:TPU:0, one launch (start us, length us, event | category | flops | bytes accessed | tf_op | source)
XLA Modules:
  0.0 125.8 jit_solution(15373991563656725810)
XLA Ops:
  0.7 0.7 compare_bitcast_fusion
  2.0 1.3 %fusion.4 = f32[64,1024]{1,0:T(8,128)S(1)} fusion(f32[64,64]{1,0:T(8,128)S(1)} %bitcast.18, f32[64,8192]{1,0:T(8,128)} %param.5, s32[]{:T(128)S(6)} %select_n.189), kind=kOutput, calls=%fused_computation.13 | convolution fusion | flops 50331648 | bytes 540676 | tf_op jit(solution)/shard_map/dot_general | solution.py:177
  3.6 1.3 %fusion.2 = f32[64,1024]{1,0:T(8,128)S(1)} fusion(f32[64,64]{1,0:T(8,128)S(1)} %bitcast.19, f32[64,8192]{1,0:T(8,128)} %param.5, s32[]{:T(128)S(6)} %select_n.197), kind=kOutput, calls=%fused_computation.7 | convolution fusion | flops 50331648 | bytes 540676 | tf_op jit(solution)/shard_map/dot_general | solution.py:177
  4.9 4.1 %collective-permute-start.4 = (f32[64,1024]{1,0:T(8,128)S(1)}, f32[64,1024]{1,0:T(8,128)S(1)}, u32[]{:S(2)}, u32[]{:S(2)}) collective-permute-start(f32[64,1024]{1,0:T(8,128)S(1)} %fusion.2), channel_id=1, source_target_pairs={{0,28},{4,0},{8,4},{12,8},{16,12},{20,16},{24,20},{28,24},{1,29},{... | collective-permute-start | bytes 786440 | tf_op jit(solution)/shard_map/ppermute | solution.py:102
  9.0 3.5 %fusion.14 = f32[64,8192]{1,0:T(8,128)S(1)} fusion(f32[64,64]{1,0:T(8,128)S(1)} %bitcast.20, f32[64,8192]{1,0:T(8,128)} %param.5), kind=kOutput, calls=%fused_computation.48 | convolution fusion | flops 402653184 | bytes 4210688 | tf_op jit(solution)/shard_map/dot_general | solution.py:175
  12.4 1.4 %collective-permute-done = f32[64,1024]{1,0:T(8,128)S(1)} collective-permute-done((f32[64,1024]{1,0:T(8,128)S(1)}, f32[64,1024]{1,0:T(8,128)S(1)}, u32[]{:S(2)}, u32[]{:S(2)}) %collective-permute-start) | collective-permute-done | bytes 262176 | tf_op jit(solution)/shard_map/ppermute | solution.py:100
  13.8 0.7 dynamic-slice_add_fusion.4
  14.5 8.9 %collective-permute-done.1 = f32[64,1024]{1,0:T(8,128)S(1)} collective-permute-done((f32[64,1024]{1,0:T(8,128)}, f32[64,1024]{1,0:T(8,128)S(1)}, u32[]{:S(2)}, u32[]{:S(2)}) %collective-permute-start.1) | collective-permute-done | bytes 262176 | tf_op jit(solution)/shard_map/ppermute | solution.py:100
  23.6 3.2 %collective-permute-start.5 = (f32[64,1024]{1,0:T(8,128)S(1)}, f32[64,1024]{1,0:T(8,128)}, u32[]{:S(2)}, u32[]{:S(2)}) collective-permute-start(f32[64,1024]{1,0:T(8,128)S(1)} %get-tuple-element.9), channel_id=1, source_target_pairs={{0,28},{4,0},{8,4},{12,8},{16,12},{20,16},{24,20},{28,24},{1,29},{... | collective-permute-start | bytes 786440 | tf_op jit(solution)/shard_map/ppermute | solution.py:102
  26.8 4.6 %collective-permute-done.2 = f32[64,1024]{1,0:T(8,128)S(1)} collective-permute-done((f32[64,1024]{1,0:T(8,128)S(1)}, f32[64,1024]{1,0:T(8,128)S(1)}, u32[]{:S(2)}, u32[]{:S(2)}) %collective-permute-start.2) | collective-permute-done | bytes 262176 | tf_op jit(solution)/shard_map/ppermute | solution.py:100
  31.4 1.0 dynamic-slice_add_fusion.2
  32.5 3.2 %collective-permute-start.6 = (f32[64,1024]{1,0:T(8,128)S(1)}, f32[64,1024]{1,0:T(8,128)S(1)}, u32[]{:S(2)}, u32[]{:S(2)}) collective-permute-start(f32[64,1024]{1,0:T(8,128)S(1)} %get-tuple-element.7), channel_id=1, source_target_pairs={{0,28},{4,0},{8,4},{12,8},{16,12},{20,16},{24,20},{28,24},{1,29},{... | collective-permute-start | bytes 786440 | tf_op jit(solution)/shard_map/ppermute | solution.py:102
  35.7 4.3 %collective-permute-done.3 = f32[64,1024]{1,0:T(8,128)S(1)} collective-permute-done((f32[64,1024]{1,0:T(8,128)S(1)}, f32[64,1024]{1,0:T(8,128)S(1)}, u32[]{:S(2)}, u32[]{:S(2)}) %collective-permute-start.3) | collective-permute-done | bytes 262176 | tf_op jit(solution)/shard_map/ppermute | solution.py:100
  40.1 1.0 add_add_fusion
  41.1 3.3 %collective-permute-start.7 = (f32[64,256]{1,0:T(8,128)S(1)}, f32[64,256]{1,0:T(8,128)S(1)}, u32[]{:S(2)}, u32[]{:S(2)}) collective-permute-start(f32[64,256]{1,0:T(8,128)S(1)} %get-tuple-element.10), channel_id=1, source_target_pairs={{0,2},{1,3},{2,0},{3,1},{4,6},{5,7},{6,4},{7,5},{8,10},{9,11},{10,... | collective-permute-start | bytes 196616 | tf_op jit(solution)/shard_map/ppermute | solution.py:135
  44.4 0.7 collective-permute-start.8
  45.1 2.6 %collective-permute-start.9 = (f32[64,256]{1,0:T(8,128)S(1)}, f32[64,256]{1,0:T(8,128)S(1)}, u32[]{:S(2)}, u32[]{:S(2)}) collective-permute-start(f32[64,256]{1,0:T(8,128)S(1)} %get-tuple-element.11), channel_id=1, source_target_pairs={{0,3},{1,0},{2,1},{3,2},{4,7},{5,4},{6,5},{7,6},{8,11},{9,8},{10,9... | collective-permute-start | bytes 196616 | tf_op jit(solution)/shard_map/ppermute | solution.py:135
  47.7 2.2 %collective-permute-done.8 = f32[64,256]{1,0:T(8,128)S(1)} collective-permute-done((f32[64,256]{1,0:T(8,128)S(1)}, f32[64,256]{1,0:T(8,128)S(1)}, u32[]{:S(2)}, u32[]{:S(2)}) %collective-permute-start.8) | collective-permute-done | bytes 65568 | tf_op jit(solution)/shard_map/ppermute | solution.py:135
  50.0 3.1 %collective-permute-start.10 = (f32[64,64]{1,0:T(8,128)S(1)}, f32[64,64]{1,0:T(8,128)S(1)}, u32[]{:S(2)}, u32[]{:S(2)}) collective-permute-start(f32[64,64]{1,0:T(8,128)S(1)} %get-tuple-element.13), channel_id=1, source_target_pairs={{0,64},{32,96},{64,0},{96,32},{1,65},{33,97},{65,1},{97,33},{2,66}... | collective-permute-start | bytes 49160 | tf_op jit(solution)/shard_map/ppermute | solution.py:135
  53.7 2.6 %collective-permute-start.12 = (f32[64,64]{1,0:T(8,128)S(1)}, f32[64,64]{1,0:T(8,128)S(1)}, u32[]{:S(2)}, u32[]{:S(2)}) collective-permute-start(f32[64,64]{1,0:T(8,128)S(1)} %get-tuple-element.14), channel_id=1, source_target_pairs={{0,96},{32,0},{64,32},{96,64},{1,97},{33,1},{65,33},{97,65},{2,98}... | collective-permute-start | bytes 49160 | tf_op jit(solution)/shard_map/ppermute | solution.py:135
  56.4 1.9 %collective-permute-done.11 = f32[64,64]{1,0:T(8,128)S(1)} collective-permute-done((f32[64,64]{1,0:T(8,128)S(1)}, f32[64,64]{1,0:T(8,128)S(1)}, u32[]{:S(2)}, u32[]{:S(2)}) %collective-permute-start.11) | collective-permute-done | bytes 16416 | tf_op jit(solution)/shard_map/ppermute | solution.py:135
  58.4 1.5 %collective-permute-start.13 = (f32[64,64]{1,0:T(8,128)S(1)}, f32[64,64]{1,0:T(8,128)S(1)}, u32[]{:S(2)}, u32[]{:S(2)}) collective-permute-start(f32[64,64]{1,0:T(8,128)S(1)} %add_add_fusion.2), channel_id=1, source_target_pairs={{0,64},{32,96},{64,0},{96,32},{1,65},{33,97},{65,1},{97,33},{2,66}... | collective-permute-start | bytes 49160 | tf_op jit(solution)/shard_map/ppermute | solution.py:145
  59.9 2.6 %collective-permute-start.14 = (f32[64,64]{1,0:T(8,128)S(1)}, f32[64,64]{1,0:T(8,128)S(1)}, u32[]{:S(2)}, u32[]{:S(2)}) collective-permute-start(f32[64,64]{1,0:T(8,128)S(1)} %add_add_fusion.2), channel_id=1, source_target_pairs={{0,32},{32,64},{64,96},{96,0},{1,33},{33,65},{65,97},{97,1},{2,34}... | collective-permute-start | bytes 49160 | tf_op jit(solution)/shard_map/ppermute | solution.py:145
  64.1 0.9 collective-permute-done.14
  65.4 1.0 collective-permute-done.15
  67.0 1.5 %collective-permute-start.16 = (f32[64,256]{1,0:T(8,128)S(1)}, f32[64,256]{1,0:T(8,128)S(1)}, u32[]{:S(2)}, u32[]{:S(2)}) collective-permute-start(f32[64,256]{1,0:T(8,128)S(1)} %dynamic_update_slice.51), channel_id=1, source_target_pairs={{0,2},{1,3},{2,0},{3,1},{4,6},{5,7},{6,4},{7,5},{8,10},{9,11},{10,... | collective-permute-start | bytes 196616 | tf_op jit(solution)/shard_map/ppermute | solution.py:145
  68.5 2.6 %collective-permute-start.17 = (f32[64,256]{1,0:T(8,128)S(1)}, f32[64,256]{1,0:T(8,128)S(1)}, u32[]{:S(2)}, u32[]{:S(2)}) collective-permute-start(f32[64,256]{1,0:T(8,128)S(1)} %dynamic_update_slice.51), channel_id=1, source_target_pairs={{0,1},{1,2},{2,3},{3,0},{4,5},{5,6},{6,7},{7,4},{8,9},{9,10},{10,1... | collective-permute-start | bytes 196616 | tf_op jit(solution)/shard_map/ppermute | solution.py:145
  71.8 1.0 collective-permute-done.16
  72.9 1.2 collective-permute-done.17
  74.0 1.4 %collective-permute-done.18 = f32[64,256]{1,0:T(8,128)S(1)} collective-permute-done((f32[64,256]{1,0:T(8,128)S(1)}, f32[64,256]{1,0:T(8,128)S(1)}, u32[]{:S(2)}, u32[]{:S(2)}) %collective-permute-start.18) | collective-permute-done | bytes 65568 | tf_op jit(solution)/shard_map/ppermute | solution.py:145
  75.4 2.4 %collective-permute-start.19 = (f32[64,1024]{1,0:T(8,128)S(1)}, f32[64,1024]{1,0:T(8,128)S(1)}, u32[]{:S(2)}, u32[]{:S(2)}) collective-permute-start(f32[64,1024]{1,0:T(8,128)S(1)} %constant_dynamic-update-slice_fusion.8), channel_id=1, source_target_pairs={{0,4},{4,8},{8,12},{12,16},{16,20},{20,24},{24,28},{28,0},{1,5},{5... | collective-permute-start | bytes 786440 | tf_op jit(solution)/shard_map/ppermute | solution.py:122
  77.8 1.0 collective-permute-start.20
  78.9 2.7 %copy.9 = f32[64,8192]{0,1:T(8,128)} copy(f32[64,8192]{1,0:T(8,128)S(1)} %copy-done.1) | data formatting | bytes 4194304 | tf_op args[0]
  81.6 2.8 %gather_fusion = f32[64,64]{1,0:T(8,128)S(1)} fusion(f32[64,8192]{0,1:T(8,128)} %copy.9, s32[1024]{0:T(1024)S(1)} %pad_clamp_fusion), kind=kCustom, calls=%fused_computation | custom fusion | bytes 33024 | tf_op jit(solution)/shard_map/jit(_take)/gather | solution.py:170
  84.4 2.1 %collective-permute-start.21 = (f32[64,1024]{1,0:T(8,128)S(1)}, f32[64,1024]{1,0:T(8,128)S(1)}, u32[]{:S(2)}, u32[]{:S(2)}) collective-permute-start(f32[64,1024]{1,0:T(8,128)S(1)} %collective-permute-done.19), channel_id=1, source_target_pairs={{0,4},{4,8},{8,12},{12,16},{16,20},{20,24},{24,28},{28,0},{1,5},{5... | collective-permute-start | bytes 786440 | tf_op jit(solution)/shard_map/ppermute | solution.py:122
  87.1 1.3 collective-permute-start.22
  88.5 4.1 %collective-permute-done.21 = f32[64,1024]{1,0:T(8,128)S(1)} collective-permute-done((f32[64,1024]{1,0:T(8,128)S(1)}, f32[64,1024]{1,0:T(8,128)S(1)}, u32[]{:S(2)}, u32[]{:S(2)}) %collective-permute-start.21) | collective-permute-done | bytes 262176 | tf_op jit(solution)/shard_map/ppermute | solution.py:122
  92.6 2.5 %collective-permute-start.23 = (f32[64,1024]{1,0:T(8,128)S(1)}, f32[64,1024]{1,0:T(8,128)S(1)}, u32[]{:S(2)}, u32[]{:S(2)}) collective-permute-start(f32[64,1024]{1,0:T(8,128)S(1)} %collective-permute-done.21), channel_id=1, source_target_pairs={{0,4},{4,8},{8,12},{12,16},{16,20},{20,24},{24,28},{28,0},{1,5},{5... | collective-permute-start | bytes 786440 | tf_op jit(solution)/shard_map/ppermute | solution.py:122
  95.2 0.8 collective-permute-start.24
  96.0 4.2 %collective-permute-done.23 = f32[64,1024]{1,0:T(8,128)S(1)} collective-permute-done((f32[64,1024]{1,0:T(8,128)S(1)}, f32[64,1024]{1,0:T(8,128)S(1)}, u32[]{:S(2)}, u32[]{:S(2)}) %collective-permute-start.23) | collective-permute-done | bytes 262176 | tf_op jit(solution)/shard_map/ppermute | solution.py:122
  100.2 1.3 %collective-permute-start.25 = (f32[64,1024]{1,0:T(8,128)S(1)}, f32[64,1024]{1,0:T(8,128)S(1)}, u32[]{:S(2)}, u32[]{:S(2)}) collective-permute-start(f32[64,1024]{1,0:T(8,128)S(1)} %collective-permute-done.23), channel_id=1, source_target_pairs={{0,4},{4,8},{8,12},{12,16},{16,20},{20,24},{24,28},{28,0},{1,5},{5... | collective-permute-start | bytes 786440 | tf_op jit(solution)/shard_map/ppermute | solution.py:122
  101.8 6.0 %collective-permute-done.25 = f32[64,1024]{1,0:T(8,128)S(1)} collective-permute-done((f32[64,1024]{1,0:T(8,128)S(1)}, f32[64,1024]{1,0:T(8,128)S(1)}, u32[]{:S(2)}, u32[]{:S(2)}) %collective-permute-start.25) | collective-permute-done | bytes 262176 | tf_op jit(solution)/shard_map/ppermute | solution.py:122
  107.8 1.3 %copy-done.2 = f32[64,8192]{1,0:T(8,128)} copy-done((f32[64,8192]{1,0:T(8,128)}, f32[64,8192]{1,0:T(8,128)S(1)}, u32[]{:S(2)}) %copy-start.2) | copy-done | bytes 2097176
  109.2 1.4 %fusion.m_ref = f32[64,64]{1,0:T(8,128)S(1)} fusion(f32[64,8192]{1,0:T(8,128)S(1)} %constant_dynamic-update-slice_fusion, s32[64]{0:T(128)S(1)} %copy-done.5), kind=kOutput, calls=%fused_computation.3 | convolution fusion | flops 403177472 | bytes 2113792 | tf_op jit(solution)/shard_map/dot_general | solution.py:181
  110.6 0.7 copy.10
  111.3 8.6 %shard_map.68 = (f32[64,64]{1,0:T(8,128)}, f32[1,64]{1,0:T(1,128)}) custom-call(f32[64,64]{1,0:T(8,128)} %copy-done.4, f32[64,64]{1,0:T(8,128)} %bitcast.21, f32[1,64]{1,0:T(1,128)} %convert_bitcast_fusion.acc_ref), custom_call_target="tpu_custom_call" | custom-call | tf_op jit(solution)/shard_map/pallas_call | solution.py:76
  119.9 1.1 fusion.6
  121.0 4.8 %convolution_subtract_fusion = f32[64,8192]{1,0:T(8,128)} fusion(f32[64,8192]{1,0:T(8,128)S(1)} %copy-done.1, f32[64,64]{1,0:T(8,128)S(1)} %fusion.6, f32[64,8192]{1,0:T(8,128)} %copy-done.2), kind=kOutput, calls=%fused_computation.1 | convolution fusion | flops 403177472 | bytes 6307840 | tf_op jit(solution)/shard_map/dot_general | solution.py:184
  (62 shorter events, 6.2 us)
Async XLA Ops:
  0.6 1.0 copy-start
  3.3 10.5 %collective-permute-start = (f32[64,1024]{1,0:T(8,128)S(1)}, f32[64,1024]{1,0:T(8,128)S(1)}, u32[]{:S(2)}, u32[]{:S(2)}) collective-permute-start(f32[64,1024]{1,0:T(8,128)S(1)} %fusion.4), channel_id=1, source_target_pairs={{0,4},{4,8},{8,12},{12,16},{16,20},{20,24},{24,28},{28,0},{1,5},{5... | collective-permute-start | bytes 786440 | tf_op jit(solution)/shard_map/ppermute | solution.py:100
  4.9 9.6 %collective-permute-start.4 = (f32[64,1024]{1,0:T(8,128)S(1)}, f32[64,1024]{1,0:T(8,128)S(1)}, u32[]{:S(2)}, u32[]{:S(2)}) collective-permute-start(f32[64,1024]{1,0:T(8,128)S(1)} %fusion.2), channel_id=1, source_target_pairs={{0,28},{4,0},{8,4},{12,8},{16,12},{20,16},{24,20},{28,24},{1,29},{... | collective-permute-start | bytes 786440 | tf_op jit(solution)/shard_map/ppermute | solution.py:102
  12.4 19.0 %copy-start.3 = (f32[64,8192]{1,0:T(8,128)}, f32[64,8192]{1,0:T(8,128)S(1)}, u32[]{:S(2)}) copy-start(f32[64,8192]{1,0:T(8,128)S(1)} %fusion.14) | copy-start | bytes 6291460
  14.5 8.9 %collective-permute-start.1 = (f32[64,1024]{1,0:T(8,128)}, f32[64,1024]{1,0:T(8,128)S(1)}, u32[]{:S(2)}, u32[]{:S(2)}) collective-permute-start(f32[64,1024]{1,0:T(8,128)} %dynamic-slice_add_fusion.4), channel_id=1, source_target_pairs={{0,4},{4,8},{8,12},{12,16},{16,20},{20,24},{24,28},{28,0},{1,5},{5... | collective-permute-start | bytes 786440 | tf_op jit(solution)/shard_map/ppermute | solution.py:100
  23.5 39.7 %copy-start.5 = (s32[64]{0:T(128)S(1)}, s32[64]{0:T(128)}, u32[]{:S(2)}) copy-start(s32[64]{0:T(128)} %param.8) | copy-start | bytes 772
  23.5 7.9 %collective-permute-start.2 = (f32[64,1024]{1,0:T(8,128)S(1)}, f32[64,1024]{1,0:T(8,128)S(1)}, u32[]{:S(2)}, u32[]{:S(2)}) collective-permute-start(f32[64,1024]{1,0:T(8,128)S(1)} %get-tuple-element.8), channel_id=1, source_target_pairs={{0,4},{4,8},{8,12},{12,16},{16,20},{20,24},{24,28},{28,0},{1,5},{5... | collective-permute-start | bytes 786440 | tf_op jit(solution)/shard_map/ppermute | solution.py:100
  23.6 7.8 %collective-permute-start.5 = (f32[64,1024]{1,0:T(8,128)S(1)}, f32[64,1024]{1,0:T(8,128)}, u32[]{:S(2)}, u32[]{:S(2)}) collective-permute-start(f32[64,1024]{1,0:T(8,128)S(1)} %get-tuple-element.9), channel_id=1, source_target_pairs={{0,28},{4,0},{8,4},{12,8},{16,12},{20,16},{24,20},{28,24},{1,29},{... | collective-permute-start | bytes 786440 | tf_op jit(solution)/shard_map/ppermute | solution.py:102
  32.4 46.4 %copy-start.1 = (f32[64,8192]{1,0:T(8,128)S(1)}, f32[64,8192]{1,0:T(8,128)}, u32[]{:S(2)}) copy-start(f32[64,8192]{1,0:T(8,128)} %param.5) | copy-start | bytes 6291460
  32.4 7.7 %collective-permute-start.3 = (f32[64,1024]{1,0:T(8,128)S(1)}, f32[64,1024]{1,0:T(8,128)S(1)}, u32[]{:S(2)}, u32[]{:S(2)}) collective-permute-start(f32[64,1024]{1,0:T(8,128)S(1)} %get-tuple-element.6), channel_id=1, source_target_pairs={{0,4},{4,8},{8,12},{12,16},{16,20},{20,24},{24,28},{28,0},{1,5},{5... | collective-permute-start | bytes 786440 | tf_op jit(solution)/shard_map/ppermute | solution.py:100
  32.5 7.6 %collective-permute-start.6 = (f32[64,1024]{1,0:T(8,128)S(1)}, f32[64,1024]{1,0:T(8,128)S(1)}, u32[]{:S(2)}, u32[]{:S(2)}) collective-permute-start(f32[64,1024]{1,0:T(8,128)S(1)} %get-tuple-element.7), channel_id=1, source_target_pairs={{0,28},{4,0},{8,4},{12,8},{16,12},{20,16},{24,20},{28,24},{1,29},{... | collective-permute-start | bytes 786440 | tf_op jit(solution)/shard_map/ppermute | solution.py:102
  41.1 6.5 %collective-permute-start.7 = (f32[64,256]{1,0:T(8,128)S(1)}, f32[64,256]{1,0:T(8,128)S(1)}, u32[]{:S(2)}, u32[]{:S(2)}) collective-permute-start(f32[64,256]{1,0:T(8,128)S(1)} %get-tuple-element.10), channel_id=1, source_target_pairs={{0,2},{1,3},{2,0},{3,1},{4,6},{5,7},{6,4},{7,5},{8,10},{9,11},{10,... | collective-permute-start | bytes 196616 | tf_op jit(solution)/shard_map/ppermute | solution.py:135
  44.4 5.5 %collective-permute-start.8 = (f32[64,256]{1,0:T(8,128)S(1)}, f32[64,256]{1,0:T(8,128)S(1)}, u32[]{:S(2)}, u32[]{:S(2)}) collective-permute-start(f32[64,256]{1,0:T(8,128)S(1)} %get-tuple-element.12), channel_id=1, source_target_pairs={{0,1},{1,2},{2,3},{3,0},{4,5},{5,6},{6,7},{7,4},{8,9},{9,10},{10,1... | collective-permute-start | bytes 196616 | tf_op jit(solution)/shard_map/ppermute | solution.py:135
  45.1 4.8 %collective-permute-start.9 = (f32[64,256]{1,0:T(8,128)S(1)}, f32[64,256]{1,0:T(8,128)S(1)}, u32[]{:S(2)}, u32[]{:S(2)}) collective-permute-start(f32[64,256]{1,0:T(8,128)S(1)} %get-tuple-element.11), channel_id=1, source_target_pairs={{0,3},{1,0},{2,1},{3,2},{4,7},{5,4},{6,5},{7,6},{8,11},{9,8},{10,9... | collective-permute-start | bytes 196616 | tf_op jit(solution)/shard_map/ppermute | solution.py:135
  50.0 6.4 %collective-permute-start.10 = (f32[64,64]{1,0:T(8,128)S(1)}, f32[64,64]{1,0:T(8,128)S(1)}, u32[]{:S(2)}, u32[]{:S(2)}) collective-permute-start(f32[64,64]{1,0:T(8,128)S(1)} %get-tuple-element.13), channel_id=1, source_target_pairs={{0,64},{32,96},{64,0},{96,32},{1,65},{33,97},{65,1},{97,33},{2,66}... | collective-permute-start | bytes 49160 | tf_op jit(solution)/shard_map/ppermute | solution.py:135
  53.1 5.1 %collective-permute-start.11 = (f32[64,64]{1,0:T(8,128)S(1)}, f32[64,64]{1,0:T(8,128)S(1)}, u32[]{:S(2)}, u32[]{:S(2)}) collective-permute-start(f32[64,64]{1,0:T(8,128)S(1)} %get-tuple-element.15), channel_id=1, source_target_pairs={{0,32},{32,64},{64,96},{96,0},{1,33},{33,65},{65,97},{97,1},{2,34}... | collective-permute-start | bytes 49160 | tf_op jit(solution)/shard_map/ppermute | solution.py:135
  53.7 4.5 %collective-permute-start.12 = (f32[64,64]{1,0:T(8,128)S(1)}, f32[64,64]{1,0:T(8,128)S(1)}, u32[]{:S(2)}, u32[]{:S(2)}) collective-permute-start(f32[64,64]{1,0:T(8,128)S(1)} %get-tuple-element.14), channel_id=1, source_target_pairs={{0,96},{32,0},{64,32},{96,64},{1,97},{33,1},{65,33},{97,65},{2,98}... | collective-permute-start | bytes 49160 | tf_op jit(solution)/shard_map/ppermute | solution.py:135
  58.4 5.5 %collective-permute-start.13 = (f32[64,64]{1,0:T(8,128)S(1)}, f32[64,64]{1,0:T(8,128)S(1)}, u32[]{:S(2)}, u32[]{:S(2)}) collective-permute-start(f32[64,64]{1,0:T(8,128)S(1)} %add_add_fusion.2), channel_id=1, source_target_pairs={{0,64},{32,96},{64,0},{96,32},{1,65},{33,97},{65,1},{97,33},{2,66}... | collective-permute-start | bytes 49160 | tf_op jit(solution)/shard_map/ppermute | solution.py:145
  59.9 5.1 %collective-permute-start.14 = (f32[64,64]{1,0:T(8,128)S(1)}, f32[64,64]{1,0:T(8,128)S(1)}, u32[]{:S(2)}, u32[]{:S(2)}) collective-permute-start(f32[64,64]{1,0:T(8,128)S(1)} %add_add_fusion.2), channel_id=1, source_target_pairs={{0,32},{32,64},{64,96},{96,0},{1,33},{33,65},{65,97},{97,1},{2,34}... | collective-permute-start | bytes 49160 | tf_op jit(solution)/shard_map/ppermute | solution.py:145
  62.5 3.9 %collective-permute-start.15 = (f32[64,64]{1,0:T(8,128)S(1)}, f32[64,64]{1,0:T(8,128)S(1)}, u32[]{:S(2)}, u32[]{:S(2)}) collective-permute-start(f32[64,64]{1,0:T(8,128)S(1)} %add_add_fusion.2), channel_id=1, source_target_pairs={{0,96},{32,0},{64,32},{96,64},{1,97},{33,1},{65,33},{97,65},{2,98}... | collective-permute-start | bytes 49160 | tf_op jit(solution)/shard_map/ppermute | solution.py:145
  67.0 5.9 %collective-permute-start.16 = (f32[64,256]{1,0:T(8,128)S(1)}, f32[64,256]{1,0:T(8,128)S(1)}, u32[]{:S(2)}, u32[]{:S(2)}) collective-permute-start(f32[64,256]{1,0:T(8,128)S(1)} %dynamic_update_slice.51), channel_id=1, source_target_pairs={{0,2},{1,3},{2,0},{3,1},{4,6},{5,7},{6,4},{7,5},{8,10},{9,11},{10,... | collective-permute-start | bytes 196616 | tf_op jit(solution)/shard_map/ppermute | solution.py:145
  68.5 5.5 %collective-permute-start.17 = (f32[64,256]{1,0:T(8,128)S(1)}, f32[64,256]{1,0:T(8,128)S(1)}, u32[]{:S(2)}, u32[]{:S(2)}) collective-permute-start(f32[64,256]{1,0:T(8,128)S(1)} %dynamic_update_slice.51), channel_id=1, source_target_pairs={{0,1},{1,2},{2,3},{3,0},{4,5},{5,6},{6,7},{7,4},{8,9},{9,10},{10,1... | collective-permute-start | bytes 196616 | tf_op jit(solution)/shard_map/ppermute | solution.py:145
  71.2 4.3 %collective-permute-start.18 = (f32[64,256]{1,0:T(8,128)S(1)}, f32[64,256]{1,0:T(8,128)S(1)}, u32[]{:S(2)}, u32[]{:S(2)}) collective-permute-start(f32[64,256]{1,0:T(8,128)S(1)} %dynamic_update_slice.51), channel_id=1, source_target_pairs={{0,3},{1,0},{2,1},{3,2},{4,7},{5,4},{6,5},{7,6},{8,11},{9,8},{10,9... | collective-permute-start | bytes 196616 | tf_op jit(solution)/shard_map/ppermute | solution.py:145
  75.4 9.0 %collective-permute-start.19 = (f32[64,1024]{1,0:T(8,128)S(1)}, f32[64,1024]{1,0:T(8,128)S(1)}, u32[]{:S(2)}, u32[]{:S(2)}) collective-permute-start(f32[64,1024]{1,0:T(8,128)S(1)} %constant_dynamic-update-slice_fusion.8), channel_id=1, source_target_pairs={{0,4},{4,8},{8,12},{12,16},{16,20},{20,24},{24,28},{28,0},{1,5},{5... | collective-permute-start | bytes 786440 | tf_op jit(solution)/shard_map/ppermute | solution.py:122
  77.8 9.2 %collective-permute-start.20 = (f32[64,1024]{1,0:T(8,128)S(1)}, f32[64,1024]{1,0:T(8,128)S(1)}, u32[]{:S(2)}, u32[]{:S(2)}) collective-permute-start(f32[64,1024]{1,0:T(8,128)S(1)} %constant_dynamic-update-slice_fusion.8), channel_id=1, source_target_pairs={{0,28},{4,0},{8,4},{12,8},{16,12},{20,16},{24,20},{28,24},{1,29},{... | collective-permute-start | bytes 786440 | tf_op jit(solution)/shard_map/ppermute | solution.py:125
  78.9 7.6 %copy-start.6 = (s32[64]{0:T(128)S(1)}, s32[64]{0:T(128)}, u32[]{:S(2)}) copy-start(s32[64]{0:T(128)} %param.9) | copy-start | bytes 772
  84.4 8.2 %collective-permute-start.21 = (f32[64,1024]{1,0:T(8,128)S(1)}, f32[64,1024]{1,0:T(8,128)S(1)}, u32[]{:S(2)}, u32[]{:S(2)}) collective-permute-start(f32[64,1024]{1,0:T(8,128)S(1)} %collective-permute-done.19), channel_id=1, source_target_pairs={{0,4},{4,8},{8,12},{12,16},{16,20},{20,24},{24,28},{28,0},{1,5},{5... | collective-permute-start | bytes 786440 | tf_op jit(solution)/shard_map/ppermute | solution.py:122
  87.1 8.1 %collective-permute-start.22 = (f32[64,1024]{1,0:T(8,128)S(1)}, f32[64,1024]{1,0:T(8,128)S(1)}, u32[]{:S(2)}, u32[]{:S(2)}) collective-permute-start(f32[64,1024]{1,0:T(8,128)S(1)} %collective-permute-done.20), channel_id=1, source_target_pairs={{0,28},{4,0},{8,4},{12,8},{16,12},{20,16},{24,20},{28,24},{1,29},{... | collective-permute-start | bytes 786440 | tf_op jit(solution)/shard_map/ppermute | solution.py:125
  92.6 7.6 %collective-permute-start.23 = (f32[64,1024]{1,0:T(8,128)S(1)}, f32[64,1024]{1,0:T(8,128)S(1)}, u32[]{:S(2)}, u32[]{:S(2)}) collective-permute-start(f32[64,1024]{1,0:T(8,128)S(1)} %collective-permute-done.21), channel_id=1, source_target_pairs={{0,4},{4,8},{8,12},{12,16},{16,20},{20,24},{24,28},{28,0},{1,5},{5... | collective-permute-start | bytes 786440 | tf_op jit(solution)/shard_map/ppermute | solution.py:122
  95.2 6.6 %collective-permute-start.24 = (f32[64,1024]{1,0:T(8,128)S(1)}, f32[64,1024]{1,0:T(8,128)S(1)}, u32[]{:S(2)}, u32[]{:S(2)}) collective-permute-start(f32[64,1024]{1,0:T(8,128)S(1)} %collective-permute-done.22), channel_id=1, source_target_pairs={{0,28},{4,0},{8,4},{12,8},{16,12},{20,16},{24,20},{28,24},{1,29},{... | collective-permute-start | bytes 786440 | tf_op jit(solution)/shard_map/ppermute | solution.py:125
  100.2 7.6 %collective-permute-start.25 = (f32[64,1024]{1,0:T(8,128)S(1)}, f32[64,1024]{1,0:T(8,128)S(1)}, u32[]{:S(2)}, u32[]{:S(2)}) collective-permute-start(f32[64,1024]{1,0:T(8,128)S(1)} %collective-permute-done.23), channel_id=1, source_target_pairs={{0,4},{4,8},{8,12},{12,16},{16,20},{20,24},{24,28},{28,0},{1,5},{5... | collective-permute-start | bytes 786440 | tf_op jit(solution)/shard_map/ppermute | solution.py:122
  107.8 1.4 %copy-start.2 = (f32[64,8192]{1,0:T(8,128)}, f32[64,8192]{1,0:T(8,128)S(1)}, u32[]{:S(2)}) copy-start(f32[64,8192]{1,0:T(8,128)S(1)} %constant_dynamic-update-slice_fusion) | copy-start | bytes 6291460
  110.6 0.7 copy-start.4

commit v9 on v8

--- a/solution.py
+++ b/solution.py
@@ -39,11 +39,12 @@
     return lax.scan(one_step, start_value, step_items)
 
 
-def _border_kernel(m_ref, mt_ref, acc_ref, c_ref, r_ref):
+def _border_kernel(m_ref, acc_ref, c_ref, r_ref, mt_ref):
     n = m_ref.shape[0]
     lane = lax.broadcasted_iota(jnp.int32, (1, n), 1)
     sub = lax.broadcasted_iota(jnp.int32, (n, 1), 0)
-    mt = mt_ref[...]
+    mt = jnp.transpose(m_ref[...])
+    mt_ref[...] = mt
     acc = acc_ref[...]
 
     def step(k, carry):
@@ -76,9 +77,10 @@
     c, r = pl.pallas_call(
         _border_kernel,
         out_shape=(jax.ShapeDtypeStruct((n, n), jnp.float32), jax.ShapeDtypeStruct((1, n), jnp.float32)),
-        in_specs=[vm, vm, vm],
+        in_specs=[vm, vm],
+        scratch_shapes=[pltpu.VMEM((n, n), jnp.float32)],
         out_specs=(vm, vm),
-    )(intersection, intersection.T, accepted.astype(jnp.float32).reshape(1, n))
+    )(intersection, accepted.astype(jnp.float32).reshape(1, n))
     return c, r.reshape(n)
 
 

time: 127 us -> 127 us (level)
    unnamed x15 -> x13, local copies, waits for them, and re-layouts: 4.2 us -> 4.17 us
where the time goes in v9:
time: 127 us; the launch traced here: 126 us
  starting transfers between devices  44.7 us (35%)
  waiting for transfers between devices  43.7 us (34%)
  matrix products  14.4 us (11%)
  local copies, waits for them, and re-layouts  9.19 us (7%)
  Pallas kernels  8.7 us (7%)
  other arithmetic  4.22 us (3%)
    ppermute x4, waiting for transfers between devices, half_ring_rs(): cw = lax.ppermute(cw, axis, shift_perm(n, 1))  19.2 us
    ppermute x4, waiting for transfers between devices, half_ring_ag(): cw = lax.ppermute(cw, axis, shift_perm(n, 1))  14.4 us
    ppermute x6, starting transfers between devices, direct_rs(): total = total + lax.ppermute(chunk(i + d), axis, shift_perm(n, d))  12.9 us
    ppermute x3, starting transfers between devices, half_ring_rs(): ccw = lax.ppermute(ccw, axis, shift_perm(n, -1))  10.5 us
    ppermute x6, starting transfers between devices, direct_ag(): got = lax.ppermute(x, axis, shift_perm(n, d))  9.57 us
    pallas_call x1, Pallas kernels, border(): pl.pallas_call(_border_kernel, out_shape=(jax.ShapeDtypeStruct((n, n), jn...  8.7 us
    ppermute x4, starting transfers between devices, half_ring_ag(): cw = lax.ppermute(cw, axis, shift_perm(n, 1))  8.22 us
    ppermute x6, waiting for transfers between devices, direct_ag(): got = lax.ppermute(x, axis, shift_perm(n, d))  5.78 us
  transfers between devices with their start and end apart: 26, of which 16 were waited for; matrix products, arithmetic and copies ran while one was open for 10% of the time, Pallas kernels for 0%

profile of v9, /device:TPU:0, one launch (start us, length us, event | category | flops | bytes accessed | tf_op | source)
XLA Modules:
  0.0 125.8 jit_solution(9194121990665265433)
XLA Ops:
  0.7 0.7 compare_bitcast_fusion
  2.0 1.3 %fusion.4 = f32[64,1024]{1,0:T(8,128)S(1)} fusion(f32[64,64]{1,0:T(8,128)S(1)} %bitcast.17, f32[64,8192]{1,0:T(8,128)} %param.5, s32[]{:T(128)S(6)} %select_n.189), kind=kOutput, calls=%fused_computation.13 | convolution fusion | flops 50331648 | bytes 540676 | tf_op jit(solution)/shard_map/dot_general | solution.py:179
  3.6 1.3 %fusion.2 = f32[64,1024]{1,0:T(8,128)S(1)} fusion(f32[64,64]{1,0:T(8,128)S(1)} %bitcast.18, f32[64,8192]{1,0:T(8,128)} %param.5, s32[]{:T(128)S(6)} %select_n.197), kind=kOutput, calls=%fused_computation.7 | convolution fusion | flops 50331648 | bytes 540676 | tf_op jit(solution)/shard_map/dot_general | solution.py:179
  4.9 4.1 %collective-permute-start.4 = (f32[64,1024]{1,0:T(8,128)S(1)}, f32[64,1024]{1,0:T(8,128)S(1)}, u32[]{:S(2)}, u32[]{:S(2)}) collective-permute-start(f32[64,1024]{1,0:T(8,128)S(1)} %fusion.2), channel_id=1, source_target_pairs={{0,28},{4,0},{8,4},{12,8},{16,12},{20,16},{24,20},{28,24},{1,29},{... | collective-permute-start | bytes 786440 | tf_op jit(solution)/shard_map/ppermute | solution.py:104
  9.0 3.5 %fusion.14 = f32[64,8192]{1,0:T(8,128)S(1)} fusion(f32[64,64]{1,0:T(8,128)S(1)} %bitcast.19, f32[64,8192]{1,0:T(8,128)} %param.5), kind=kOutput, calls=%fused_computation.48 | convolution fusion | flops 402653184 | bytes 4210688 | tf_op jit(solution)/shard_map/dot_general | solution.py:177
  12.4 1.4 %collective-permute-done = f32[64,1024]{1,0:T(8,128)S(1)} collective-permute-done((f32[64,1024]{1,0:T(8,128)S(1)}, f32[64,1024]{1,0:T(8,128)S(1)}, u32[]{:S(2)}, u32[]{:S(2)}) %collective-permute-start) | collective-permute-done | bytes 262176 | tf_op jit(solution)/shard_map/ppermute | solution.py:102
  13.8 0.7 dynamic-slice_add_fusion.4
  14.5 8.9 %collective-permute-done.1 = f32[64,1024]{1,0:T(8,128)S(1)} collective-permute-done((f32[64,1024]{1,0:T(8,128)}, f32[64,1024]{1,0:T(8,128)S(1)}, u32[]{:S(2)}, u32[]{:S(2)}) %collective-permute-start.1) | collective-permute-done | bytes 262176 | tf_op jit(solution)/shard_map/ppermute | solution.py:102
  23.6 3.2 %collective-permute-start.5 = (f32[64,1024]{1,0:T(8,128)S(1)}, f32[64,1024]{1,0:T(8,128)}, u32[]{:S(2)}, u32[]{:S(2)}) collective-permute-start(f32[64,1024]{1,0:T(8,128)S(1)} %get-tuple-element.9), channel_id=1, source_target_pairs={{0,28},{4,0},{8,4},{12,8},{16,12},{20,16},{24,20},{28,24},{1,29},{... | collective-permute-start | bytes 786440 | tf_op jit(solution)/shard_map/ppermute | solution.py:104
  26.8 4.6 %collective-permute-done.2 = f32[64,1024]{1,0:T(8,128)S(1)} collective-permute-done((f32[64,1024]{1,0:T(8,128)S(1)}, f32[64,1024]{1,0:T(8,128)S(1)}, u32[]{:S(2)}, u32[]{:S(2)}) %collective-permute-start.2) | collective-permute-done | bytes 262176 | tf_op jit(solution)/shard_map/ppermute | solution.py:102
  31.4 1.0 dynamic-slice_add_fusion.2
  32.5 3.2 %collective-permute-start.6 = (f32[64,1024]{1,0:T(8,128)S(1)}, f32[64,1024]{1,0:T(8,128)S(1)}, u32[]{:S(2)}, u32[]{:S(2)}) collective-permute-start(f32[64,1024]{1,0:T(8,128)S(1)} %get-tuple-element.7), channel_id=1, source_target_pairs={{0,28},{4,0},{8,4},{12,8},{16,12},{20,16},{24,20},{28,24},{1,29},{... | collective-permute-start | bytes 786440 | tf_op jit(solution)/shard_map/ppermute | solution.py:104
  35.7 4.3 %collective-permute-done.3 = f32[64,1024]{1,0:T(8,128)S(1)} collective-permute-done((f32[64,1024]{1,0:T(8,128)S(1)}, f32[64,1024]{1,0:T(8,128)S(1)}, u32[]{:S(2)}, u32[]{:S(2)}) %collective-permute-start.3) | collective-permute-done | bytes 262176 | tf_op jit(solution)/shard_map/ppermute | solution.py:102
  40.1 1.0 add_add_fusion
  41.1 3.3 %collective-permute-start.7 = (f32[64,256]{1,0:T(8,128)S(1)}, f32[64,256]{1,0:T(8,128)S(1)}, u32[]{:S(2)}, u32[]{:S(2)}) collective-permute-start(f32[64,256]{1,0:T(8,128)S(1)} %get-tuple-element.10), channel_id=1, source_target_pairs={{0,2},{1,3},{2,0},{3,1},{4,6},{5,7},{6,4},{7,5},{8,10},{9,11},{10,... | collective-permute-start | bytes 196616 | tf_op jit(solution)/shard_map/ppermute | solution.py:137
  44.4 0.7 collective-permute-start.8
  45.1 2.6 %collective-permute-start.9 = (f32[64,256]{1,0:T(8,128)S(1)}, f32[64,256]{1,0:T(8,128)S(1)}, u32[]{:S(2)}, u32[]{:S(2)}) collective-permute-start(f32[64,256]{1,0:T(8,128)S(1)} %get-tuple-element.11), channel_id=1, source_target_pairs={{0,3},{1,0},{2,1},{3,2},{4,7},{5,4},{6,5},{7,6},{8,11},{9,8},{10,9... | collective-permute-start | bytes 196616 | tf_op jit(solution)/shard_map/ppermute | solution.py:137
  47.7 2.2 %collective-permute-done.8 = f32[64,256]{1,0:T(8,128)S(1)} collective-permute-done((f32[64,256]{1,0:T(8,128)S(1)}, f32[64,256]{1,0:T(8,128)S(1)}, u32[]{:S(2)}, u32[]{:S(2)}) %collective-permute-start.8) | collective-permute-done | bytes 65568 | tf_op jit(solution)/shard_map/ppermute | solution.py:137
  50.0 3.1 %collective-permute-start.10 = (f32[64,64]{1,0:T(8,128)S(1)}, f32[64,64]{1,0:T(8,128)S(1)}, u32[]{:S(2)}, u32[]{:S(2)}) collective-permute-start(f32[64,64]{1,0:T(8,128)S(1)} %get-tuple-element.13), channel_id=1, source_target_pairs={{0,64},{32,96},{64,0},{96,32},{1,65},{33,97},{65,1},{97,33},{2,66}... | collective-permute-start | bytes 49160 | tf_op jit(solution)/shard_map/ppermute | solution.py:137
  53.7 2.6 %collective-permute-start.12 = (f32[64,64]{1,0:T(8,128)S(1)}, f32[64,64]{1,0:T(8,128)S(1)}, u32[]{:S(2)}, u32[]{:S(2)}) collective-permute-start(f32[64,64]{1,0:T(8,128)S(1)} %get-tuple-element.14), channel_id=1, source_target_pairs={{0,96},{32,0},{64,32},{96,64},{1,97},{33,1},{65,33},{97,65},{2,98}... | collective-permute-start | bytes 49160 | tf_op jit(solution)/shard_map/ppermute | solution.py:137
  56.4 1.9 %collective-permute-done.11 = f32[64,64]{1,0:T(8,128)S(1)} collective-permute-done((f32[64,64]{1,0:T(8,128)S(1)}, f32[64,64]{1,0:T(8,128)S(1)}, u32[]{:S(2)}, u32[]{:S(2)}) %collective-permute-start.11) | collective-permute-done | bytes 16416 | tf_op jit(solution)/shard_map/ppermute | solution.py:137
  58.4 1.5 %collective-permute-start.13 = (f32[64,64]{1,0:T(8,128)S(1)}, f32[64,64]{1,0:T(8,128)S(1)}, u32[]{:S(2)}, u32[]{:S(2)}) collective-permute-start(f32[64,64]{1,0:T(8,128)S(1)} %add_add_fusion.2), channel_id=1, source_target_pairs={{0,64},{32,96},{64,0},{96,32},{1,65},{33,97},{65,1},{97,33},{2,66}... | collective-permute-start | bytes 49160 | tf_op jit(solution)/shard_map/ppermute | solution.py:147
  59.9 2.6 %collective-permute-start.14 = (f32[64,64]{1,0:T(8,128)S(1)}, f32[64,64]{1,0:T(8,128)S(1)}, u32[]{:S(2)}, u32[]{:S(2)}) collective-permute-start(f32[64,64]{1,0:T(8,128)S(1)} %add_add_fusion.2), channel_id=1, source_target_pairs={{0,32},{32,64},{64,96},{96,0},{1,33},{33,65},{65,97},{97,1},{2,34}... | collective-permute-start | bytes 49160 | tf_op jit(solution)/shard_map/ppermute | solution.py:147
  62.5 0.6 collective-permute-start.15
  64.1 0.9 collective-permute-done.14
  65.4 1.0 collective-permute-done.15
  67.0 1.5 %collective-permute-start.16 = (f32[64,256]{1,0:T(8,128)S(1)}, f32[64,256]{1,0:T(8,128)S(1)}, u32[]{:S(2)}, u32[]{:S(2)}) collective-permute-start(f32[64,256]{1,0:T(8,128)S(1)} %dynamic_update_slice.51), channel_id=1, source_target_pairs={{0,2},{1,3},{2,0},{3,1},{4,6},{5,7},{6,4},{7,5},{8,10},{9,11},{10,... | collective-permute-start | bytes 196616 | tf_op jit(solution)/shard_map/ppermute | solution.py:147
  68.5 2.6 %collective-permute-start.17 = (f32[64,256]{1,0:T(8,128)S(1)}, f32[64,256]{1,0:T(8,128)S(1)}, u32[]{:S(2)}, u32[]{:S(2)}) collective-permute-start(f32[64,256]{1,0:T(8,128)S(1)} %dynamic_update_slice.51), channel_id=1, source_target_pairs={{0,1},{1,2},{2,3},{3,0},{4,5},{5,6},{6,7},{7,4},{8,9},{9,10},{10,1... | collective-permute-start | bytes 196616 | tf_op jit(solution)/shard_map/ppermute | solution.py:147
  71.8 1.0 collective-permute-done.16
  72.9 1.2 collective-permute-done.17
  74.0 1.4 %collective-permute-done.18 = f32[64,256]{1,0:T(8,128)S(1)} collective-permute-done((f32[64,256]{1,0:T(8,128)S(1)}, f32[64,256]{1,0:T(8,128)S(1)}, u32[]{:S(2)}, u32[]{:S(2)}) %collective-permute-start.18) | collective-permute-done | bytes 65568 | tf_op jit(solution)/shard_map/ppermute | solution.py:147
  75.4 2.4 %collective-permute-start.19 = (f32[64,1024]{1,0:T(8,128)S(1)}, f32[64,1024]{1,0:T(8,128)S(1)}, u32[]{:S(2)}, u32[]{:S(2)}) collective-permute-start(f32[64,1024]{1,0:T(8,128)S(1)} %constant_dynamic-update-slice_fusion.8), channel_id=1, source_target_pairs={{0,4},{4,8},{8,12},{12,16},{16,20},{20,24},{24,28},{28,0},{1,5},{5... | collective-permute-start | bytes 786440 | tf_op jit(solution)/shard_map/ppermute | solution.py:124
  77.8 1.0 collective-permute-start.20
  78.9 2.7 %copy.8 = f32[64,8192]{0,1:T(8,128)} copy(f32[64,8192]{1,0:T(8,128)S(1)} %copy-done.1) | data formatting | bytes 4194304 | tf_op args[0]
  81.6 2.8 %gather_fusion = f32[64,64]{1,0:T(8,128)S(1)} fusion(f32[64,8192]{0,1:T(8,128)} %copy.8, s32[1024]{0:T(1024)S(1)} %pad_clamp_fusion), kind=kCustom, calls=%fused_computation | custom fusion | bytes 33024 | tf_op jit(solution)/shard_map/jit(_take)/gather | solution.py:172
  84.4 2.1 %collective-permute-start.21 = (f32[64,1024]{1,0:T(8,128)S(1)}, f32[64,1024]{1,0:T(8,128)S(1)}, u32[]{:S(2)}, u32[]{:S(2)}) collective-permute-start(f32[64,1024]{1,0:T(8,128)S(1)} %collective-permute-done.19), channel_id=1, source_target_pairs={{0,4},{4,8},{8,12},{12,16},{16,20},{20,24},{24,28},{28,0},{1,5},{5... | collective-permute-start | bytes 786440 | tf_op jit(solution)/shard_map/ppermute | solution.py:124
  87.1 1.2 collective-permute-start.22
  88.5 4.2 %collective-permute-done.21 = f32[64,1024]{1,0:T(8,128)S(1)} collective-permute-done((f32[64,1024]{1,0:T(8,128)S(1)}, f32[64,1024]{1,0:T(8,128)S(1)}, u32[]{:S(2)}, u32[]{:S(2)}) %collective-permute-start.21) | collective-permute-done | bytes 262176 | tf_op jit(solution)/shard_map/ppermute | solution.py:124
  92.7 2.5 %collective-permute-start.23 = (f32[64,1024]{1,0:T(8,128)S(1)}, f32[64,1024]{1,0:T(8,128)S(1)}, u32[]{:S(2)}, u32[]{:S(2)}) collective-permute-start(f32[64,1024]{1,0:T(8,128)S(1)} %collective-permute-done.21), channel_id=1, source_target_pairs={{0,4},{4,8},{8,12},{12,16},{16,20},{20,24},{24,28},{28,0},{1,5},{5... | collective-permute-start | bytes 786440 | tf_op jit(solution)/shard_map/ppermute | solution.py:124
  95.2 0.8 collective-permute-start.24
  96.1 4.2 %collective-permute-done.23 = f32[64,1024]{1,0:T(8,128)S(1)} collective-permute-done((f32[64,1024]{1,0:T(8,128)S(1)}, f32[64,1024]{1,0:T(8,128)S(1)}, u32[]{:S(2)}, u32[]{:S(2)}) %collective-permute-start.23) | collective-permute-done | bytes 262176 | tf_op jit(solution)/shard_map/ppermute | solution.py:124
  100.3 1.3 %collective-permute-start.25 = (f32[64,1024]{1,0:T(8,128)S(1)}, f32[64,1024]{1,0:T(8,128)S(1)}, u32[]{:S(2)}, u32[]{:S(2)}) collective-permute-start(f32[64,1024]{1,0:T(8,128)S(1)} %collective-permute-done.23), channel_id=1, source_target_pairs={{0,4},{4,8},{8,12},{12,16},{16,20},{20,24},{24,28},{28,0},{1,5},{5... | collective-permute-start | bytes 786440 | tf_op jit(solution)/shard_map/ppermute | solution.py:124
  101.8 6.0 %collective-permute-done.25 = f32[64,1024]{1,0:T(8,128)S(1)} collective-permute-done((f32[64,1024]{1,0:T(8,128)S(1)}, f32[64,1024]{1,0:T(8,128)S(1)}, u32[]{:S(2)}, u32[]{:S(2)}) %collective-permute-start.25) | collective-permute-done | bytes 262176 | tf_op jit(solution)/shard_map/ppermute | solution.py:124
  107.9 1.3 %copy-done.2 = f32[64,8192]{1,0:T(8,128)} copy-done((f32[64,8192]{1,0:T(8,128)}, f32[64,8192]{1,0:T(8,128)S(1)}, u32[]{:S(2)}) %copy-start.2) | copy-done | bytes 2097176
  109.2 2.0 %fusion.m_ref = f32[64,64]{1,0:T(8,128)} fusion(f32[64,8192]{1,0:T(8,128)S(1)} %constant_dynamic-update-slice_fusion, s32[64]{0:T(128)S(1)} %copy-done.4), kind=kOutput, calls=%fused_computation.3 | convolution fusion | flops 403177472 | bytes 2113792 | tf_op jit(solution)/shard_map/dot_general | solution.py:183
  111.3 8.7 %shard_map.68 = (f32[64,64]{1,0:T(8,128)}, f32[1,64]{1,0:T(1,128)}) custom-call(f32[64,64]{1,0:T(8,128)} %fusion.m_ref, f32[1,64]{1,0:T(1,128)} %convert_bitcast_fusion.acc_ref), custom_call_target="tpu_custom_call" | custom-call | tf_op jit(solution)/shard_map/pallas_call | solution.py:77
  120.0 1.1 fusion.6
  121.0 4.8 %convolution_subtract_fusion = f32[64,8192]{1,0:T(8,128)} fusion(f32[64,8192]{1,0:T(8,128)S(1)} %copy-done.1, f32[64,64]{1,0:T(8,128)S(1)} %fusion.6, f32[64,8192]{1,0:T(8,128)} %copy-done.2), kind=kOutput, calls=%fused_computation.1 | convolution fusion | flops 403177472 | bytes 6307840 | tf_op jit(solution)/shard_map/dot_general | solution.py:186
  (59 shorter events, 5.6 us)
Async XLA Ops:
  0.6 1.0 copy-start
  3.3 10.5 %collective-permute-start = (f32[64,1024]{1,0:T(8,128)S(1)}, f32[64,1024]{1,0:T(8,128)S(1)}, u32[]{:S(2)}, u32[]{:S(2)}) collective-permute-start(f32[64,1024]{1,0:T(8,128)S(1)} %fusion.4), channel_id=1, source_target_pairs={{0,4},{4,8},{8,12},{12,16},{16,20},{20,24},{24,28},{28,0},{1,5},{5... | collective-permute-start | bytes 786440 | tf_op jit(solution)/shard_map/ppermute | solution.py:102
  4.9 9.7 %collective-permute-start.4 = (f32[64,1024]{1,0:T(8,128)S(1)}, f32[64,1024]{1,0:T(8,128)S(1)}, u32[]{:S(2)}, u32[]{:S(2)}) collective-permute-start(f32[64,1024]{1,0:T(8,128)S(1)} %fusion.2), channel_id=1, source_target_pairs={{0,28},{4,0},{8,4},{12,8},{16,12},{20,16},{24,20},{28,24},{1,29},{... | collective-permute-start | bytes 786440 | tf_op jit(solution)/shard_map/ppermute | solution.py:104
  12.4 19.0 %copy-start.3 = (f32[64,8192]{1,0:T(8,128)}, f32[64,8192]{1,0:T(8,128)S(1)}, u32[]{:S(2)}) copy-start(f32[64,8192]{1,0:T(8,128)S(1)} %fusion.14) | copy-start | bytes 6291460
  14.5 8.9 %collective-permute-start.1 = (f32[64,1024]{1,0:T(8,128)}, f32[64,1024]{1,0:T(8,128)S(1)}, u32[]{:S(2)}, u32[]{:S(2)}) collective-permute-start(f32[64,1024]{1,0:T(8,128)} %dynamic-slice_add_fusion.4), channel_id=1, source_target_pairs={{0,4},{4,8},{8,12},{12,16},{16,20},{20,24},{24,28},{28,0},{1,5},{5... | collective-permute-start | bytes 786440 | tf_op jit(solution)/shard_map/ppermute | solution.py:102
  23.5 39.7 %copy-start.4 = (s32[64]{0:T(128)S(1)}, s32[64]{0:T(128)}, u32[]{:S(2)}) copy-start(s32[64]{0:T(128)} %param.8) | copy-start | bytes 772
  23.5 7.9 %collective-permute-start.2 = (f32[64,1024]{1,0:T(8,128)S(1)}, f32[64,1024]{1,0:T(8,128)S(1)}, u32[]{:S(2)}, u32[]{:S(2)}) collective-permute-start(f32[64,1024]{1,0:T(8,128)S(1)} %get-tuple-element.8), channel_id=1, source_target_pairs={{0,4},{4,8},{8,12},{12,16},{16,20},{20,24},{24,28},{28,0},{1,5},{5... | collective-permute-start | bytes 786440 | tf_op jit(solution)/shard_map/ppermute | solution.py:102
  23.6 7.8 %collective-permute-start.5 = (f32[64,1024]{1,0:T(8,128)S(1)}, f32[64,1024]{1,0:T(8,128)}, u32[]{:S(2)}, u32[]{:S(2)}) collective-permute-start(f32[64,1024]{1,0:T(8,128)S(1)} %get-tuple-element.9), channel_id=1, source_target_pairs={{0,28},{4,0},{8,4},{12,8},{16,12},{20,16},{24,20},{28,24},{1,29},{... | collective-permute-start | bytes 786440 | tf_op jit(solution)/shard_map/ppermute | solution.py:104
  32.4 46.4 %copy-start.1 = (f32[64,8192]{1,0:T(8,128)S(1)}, f32[64,8192]{1,0:T(8,128)}, u32[]{:S(2)}) copy-start(f32[64,8192]{1,0:T(8,128)} %param.5) | copy-start | bytes 6291460
  32.4 7.7 %collective-permute-start.3 = (f32[64,1024]{1,0:T(8,128)S(1)}, f32[64,1024]{1,0:T(8,128)S(1)}, u32[]{:S(2)}, u32[]{:S(2)}) collective-permute-start(f32[64,1024]{1,0:T(8,128)S(1)} %get-tuple-element.6), channel_id=1, source_target_pairs={{0,4},{4,8},{8,12},{12,16},{16,20},{20,24},{24,28},{28,0},{1,5},{5... | collective-permute-start | bytes 786440 | tf_op jit(solution)/shard_map/ppermute | solution.py:102
  32.5 7.6 %collective-permute-start.6 = (f32[64,1024]{1,0:T(8,128)S(1)}, f32[64,1024]{1,0:T(8,128)S(1)}, u32[]{:S(2)}, u32[]{:S(2)}) collective-permute-start(f32[64,1024]{1,0:T(8,128)S(1)} %get-tuple-element.7), channel_id=1, source_target_pairs={{0,28},{4,0},{8,4},{12,8},{16,12},{20,16},{24,20},{28,24},{1,29},{... | collective-permute-start | bytes 786440 | tf_op jit(solution)/shard_map/ppermute | solution.py:104
  41.1 6.5 %collective-permute-start.7 = (f32[64,256]{1,0:T(8,128)S(1)}, f32[64,256]{1,0:T(8,128)S(1)}, u32[]{:S(2)}, u32[]{:S(2)}) collective-permute-start(f32[64,256]{1,0:T(8,128)S(1)} %get-tuple-element.10), channel_id=1, source_target_pairs={{0,2},{1,3},{2,0},{3,1},{4,6},{5,7},{6,4},{7,5},{8,10},{9,11},{10,... | collective-permute-start | bytes 196616 | tf_op jit(solution)/shard_map/ppermute | solution.py:137
  44.4 5.5 %collective-permute-start.8 = (f32[64,256]{1,0:T(8,128)S(1)}, f32[64,256]{1,0:T(8,128)S(1)}, u32[]{:S(2)}, u32[]{:S(2)}) collective-permute-start(f32[64,256]{1,0:T(8,128)S(1)} %get-tuple-element.12), channel_id=1, source_target_pairs={{0,1},{1,2},{2,3},{3,0},{4,5},{5,6},{6,7},{7,4},{8,9},{9,10},{10,1... | collective-permute-start | bytes 196616 | tf_op jit(solution)/shard_map/ppermute | solution.py:137
  45.1 4.8 %collective-permute-start.9 = (f32[64,256]{1,0:T(8,128)S(1)}, f32[64,256]{1,0:T(8,128)S(1)}, u32[]{:S(2)}, u32[]{:S(2)}) collective-permute-start(f32[64,256]{1,0:T(8,128)S(1)} %get-tuple-element.11), channel_id=1, source_target_pairs={{0,3},{1,0},{2,1},{3,2},{4,7},{5,4},{6,5},{7,6},{8,11},{9,8},{10,9... | collective-permute-start | bytes 196616 | tf_op jit(solution)/shard_map/ppermute | solution.py:137
  50.0 6.4 %collective-permute-start.10 = (f32[64,64]{1,0:T(8,128)S(1)}, f32[64,64]{1,0:T(8,128)S(1)}, u32[]{:S(2)}, u32[]{:S(2)}) collective-permute-start(f32[64,64]{1,0:T(8,128)S(1)} %get-tuple-element.13), channel_id=1, source_target_pairs={{0,64},{32,96},{64,0},{96,32},{1,65},{33,97},{65,1},{97,33},{2,66}... | collective-permute-start | bytes 49160 | tf_op jit(solution)/shard_map/ppermute | solution.py:137
  53.1 5.1 %collective-permute-start.11 = (f32[64,64]{1,0:T(8,128)S(1)}, f32[64,64]{1,0:T(8,128)S(1)}, u32[]{:S(2)}, u32[]{:S(2)}) collective-permute-start(f32[64,64]{1,0:T(8,128)S(1)} %get-tuple-element.15), channel_id=1, source_target_pairs={{0,32},{32,64},{64,96},{96,0},{1,33},{33,65},{65,97},{97,1},{2,34}... | collective-permute-start | bytes 49160 | tf_op jit(solution)/shard_map/ppermute | solution.py:137
  53.7 4.5 %collective-permute-start.12 = (f32[64,64]{1,0:T(8,128)S(1)}, f32[64,64]{1,0:T(8,128)S(1)}, u32[]{:S(2)}, u32[]{:S(2)}) collective-permute-start(f32[64,64]{1,0:T(8,128)S(1)} %get-tuple-element.14), channel_id=1, source_target_pairs={{0,96},{32,0},{64,32},{96,64},{1,97},{33,1},{65,33},{97,65},{2,98}... | collective-permute-start | bytes 49160 | tf_op jit(solution)/shard_map/ppermute | solution.py:137
  58.4 5.5 %collective-permute-start.13 = (f32[64,64]{1,0:T(8,128)S(1)}, f32[64,64]{1,0:T(8,128)S(1)}, u32[]{:S(2)}, u32[]{:S(2)}) collective-permute-start(f32[64,64]{1,0:T(8,128)S(1)} %add_add_fusion.2), channel_id=1, source_target_pairs={{0,64},{32,96},{64,0},{96,32},{1,65},{33,97},{65,1},{97,33},{2,66}... | collective-permute-start | bytes 49160 | tf_op jit(solution)/shard_map/ppermute | solution.py:147
  59.9 5.1 %collective-permute-start.14 = (f32[64,64]{1,0:T(8,128)S(1)}, f32[64,64]{1,0:T(8,128)S(1)}, u32[]{:S(2)}, u32[]{:S(2)}) collective-permute-start(f32[64,64]{1,0:T(8,128)S(1)} %add_add_fusion.2), channel_id=1, source_target_pairs={{0,32},{32,64},{64,96},{96,0},{1,33},{33,65},{65,97},{97,1},{2,34}... | collective-permute-start | bytes 49160 | tf_op jit(solution)/shard_map/ppermute | solution.py:147
  62.5 3.9 %collective-permute-start.15 = (f32[64,64]{1,0:T(8,128)S(1)}, f32[64,64]{1,0:T(8,128)S(1)}, u32[]{:S(2)}, u32[]{:S(2)}) collective-permute-start(f32[64,64]{1,0:T(8,128)S(1)} %add_add_fusion.2), channel_id=1, source_target_pairs={{0,96},{32,0},{64,32},{96,64},{1,97},{33,1},{65,33},{97,65},{2,98}... | collective-permute-start | bytes 49160 | tf_op jit(solution)/shard_map/ppermute | solution.py:147
  67.0 5.9 %collective-permute-start.16 = (f32[64,256]{1,0:T(8,128)S(1)}, f32[64,256]{1,0:T(8,128)S(1)}, u32[]{:S(2)}, u32[]{:S(2)}) collective-permute-start(f32[64,256]{1,0:T(8,128)S(1)} %dynamic_update_slice.51), channel_id=1, source_target_pairs={{0,2},{1,3},{2,0},{3,1},{4,6},{5,7},{6,4},{7,5},{8,10},{9,11},{10,... | collective-permute-start | bytes 196616 | tf_op jit(solution)/shard_map/ppermute | solution.py:147
  68.5 5.5 %collective-permute-start.17 = (f32[64,256]{1,0:T(8,128)S(1)}, f32[64,256]{1,0:T(8,128)S(1)}, u32[]{:S(2)}, u32[]{:S(2)}) collective-permute-start(f32[64,256]{1,0:T(8,128)S(1)} %dynamic_update_slice.51), channel_id=1, source_target_pairs={{0,1},{1,2},{2,3},{3,0},{4,5},{5,6},{6,7},{7,4},{8,9},{9,10},{10,1... | collective-permute-start | bytes 196616 | tf_op jit(solution)/shard_map/ppermute | solution.py:147
  71.2 4.3 %collective-permute-start.18 = (f32[64,256]{1,0:T(8,128)S(1)}, f32[64,256]{1,0:T(8,128)S(1)}, u32[]{:S(2)}, u32[]{:S(2)}) collective-permute-start(f32[64,256]{1,0:T(8,128)S(1)} %dynamic_update_slice.51), channel_id=1, source_target_pairs={{0,3},{1,0},{2,1},{3,2},{4,7},{5,4},{6,5},{7,6},{8,11},{9,8},{10,9... | collective-permute-start | bytes 196616 | tf_op jit(solution)/shard_map/ppermute | solution.py:147
  75.4 9.0 %collective-permute-start.19 = (f32[64,1024]{1,0:T(8,128)S(1)}, f32[64,1024]{1,0:T(8,128)S(1)}, u32[]{:S(2)}, u32[]{:S(2)}) collective-permute-start(f32[64,1024]{1,0:T(8,128)S(1)} %constant_dynamic-update-slice_fusion.8), channel_id=1, source_target_pairs={{0,4},{4,8},{8,12},{12,16},{16,20},{20,24},{24,28},{28,0},{1,5},{5... | collective-permute-start | bytes 786440 | tf_op jit(solution)/shard_map/ppermute | solution.py:124
  77.8 9.2 %collective-permute-start.20 = (f32[64,1024]{1,0:T(8,128)S(1)}, f32[64,1024]{1,0:T(8,128)S(1)}, u32[]{:S(2)}, u32[]{:S(2)}) collective-permute-start(f32[64,1024]{1,0:T(8,128)S(1)} %constant_dynamic-update-slice_fusion.8), channel_id=1, source_target_pairs={{0,28},{4,0},{8,4},{12,8},{16,12},{20,16},{24,20},{28,24},{1,29},{... | collective-permute-start | bytes 786440 | tf_op jit(solution)/shard_map/ppermute | solution.py:127
  78.9 7.6 %copy-start.5 = (s32[64]{0:T(128)S(1)}, s32[64]{0:T(128)}, u32[]{:S(2)}) copy-start(s32[64]{0:T(128)} %param.9) | copy-start | bytes 772
  84.4 8.3 %collective-permute-start.21 = (f32[64,1024]{1,0:T(8,128)S(1)}, f32[64,1024]{1,0:T(8,128)S(1)}, u32[]{:S(2)}, u32[]{:S(2)}) collective-permute-start(f32[64,1024]{1,0:T(8,128)S(1)} %collective-permute-done.19), channel_id=1, source_target_pairs={{0,4},{4,8},{8,12},{12,16},{16,20},{20,24},{24,28},{28,0},{1,5},{5... | collective-permute-start | bytes 786440 | tf_op jit(solution)/shard_map/ppermute | solution.py:124
  87.1 8.1 %collective-permute-start.22 = (f32[64,1024]{1,0:T(8,128)S(1)}, f32[64,1024]{1,0:T(8,128)S(1)}, u32[]{:S(2)}, u32[]{:S(2)}) collective-permute-start(f32[64,1024]{1,0:T(8,128)S(1)} %collective-permute-done.20), channel_id=1, source_target_pairs={{0,28},{4,0},{8,4},{12,8},{16,12},{20,16},{24,20},{28,24},{1,29},{... | collective-permute-start | bytes 786440 | tf_op jit(solution)/shard_map/ppermute | solution.py:127
  92.7 7.6 %collective-permute-start.23 = (f32[64,1024]{1,0:T(8,128)S(1)}, f32[64,1024]{1,0:T(8,128)S(1)}, u32[]{:S(2)}, u32[]{:S(2)}) collective-permute-start(f32[64,1024]{1,0:T(8,128)S(1)} %collective-permute-done.21), channel_id=1, source_target_pairs={{0,4},{4,8},{8,12},{12,16},{16,20},{20,24},{24,28},{28,0},{1,5},{5... | collective-permute-start | bytes 786440 | tf_op jit(solution)/shard_map/ppermute | solution.py:124
  95.2 6.6 %collective-permute-start.24 = (f32[64,1024]{1,0:T(8,128)S(1)}, f32[64,1024]{1,0:T(8,128)S(1)}, u32[]{:S(2)}, u32[]{:S(2)}) collective-permute-start(f32[64,1024]{1,0:T(8,128)S(1)} %collective-permute-done.22), channel_id=1, source_target_pairs={{0,28},{4,0},{8,4},{12,8},{16,12},{20,16},{24,20},{28,24},{1,29},{... | collective-permute-start | bytes 786440 | tf_op jit(solution)/shard_map/ppermute | solution.py:127
  100.3 7.6 %collective-permute-start.25 = (f32[64,1024]{1,0:T(8,128)S(1)}, f32[64,1024]{1,0:T(8,128)S(1)}, u32[]{:S(2)}, u32[]{:S(2)}) collective-permute-start(f32[64,1024]{1,0:T(8,128)S(1)} %collective-permute-done.23), channel_id=1, source_target_pairs={{0,4},{4,8},{8,12},{12,16},{16,20},{20,24},{24,28},{28,0},{1,5},{5... | collective-permute-start | bytes 786440 | tf_op jit(solution)/shard_map/ppermute | solution.py:124
  107.9 1.3 %copy-start.2 = (f32[64,8192]{1,0:T(8,128)}, f32[64,8192]{1,0:T(8,128)S(1)}, u32[]{:S(2)}) copy-start(f32[64,8192]{1,0:T(8,128)S(1)} %constant_dynamic-update-slice_fusion) | copy-start | bytes 6291460
